TPU v7x, 512 devices: a whole 4x8x8 slice. The times are simulated.
512 devices in a mesh: dp: 16 (over x, y_hi, core), tensor: 32 (over y_lo, z).
Axes of the slice: x: 4, y: 8 (y_hi: 2, y_lo: 4; y = y_hi * 4 + y_lo), z: 8, core: 2. Of those that a mesh axis runs over, the one named last changes fastest.
Arguments:
- tokens: bfloat16 [8192, 8192], P('dp', 'tensor'), may hold values from -6 to 6
- first_right: bfloat16 [32, 256, 1024], P('tensor'), may hold values from -0.375 to 0.375
- first_left: bfloat16 [128, 256, 256], P('tensor'), may hold values from -0.375 to 0.375
- second_right: bfloat16 [128, 256, 256], P('tensor'), may hold values from -0.375 to 0.375
- second_left: bfloat16 [32, 1024, 256], P('tensor'), may hold values from -0.1875 to 0.1875
- cotangent: bfloat16 [8192, 8192], P('dp', 'tensor'), may hold values from -6 to 6
Outputs:
- layer_out: bfloat16 [8192, 8192], P('dp', 'tensor')
- grad_tokens: bfloat16 [8192, 8192], P('dp', 'tensor')
- grad_first_right: float32 [32, 256, 1024], P('tensor', 'dp')
- grad_first_left: float32 [128, 256, 256], P('tensor', 'dp')
- grad_second_right: float32 [128, 256, 256], P('tensor', 'dp')
- grad_second_left: float32 [32, 1024, 256], P('tensor', 'dp')
All inputs are finite; a program needn't handle non-finite values.
Results may differ from a plain program's by a relative error of at most 0.018.
Values may be sent and summed in bfloat16 or wider, within the bound.
No kernel may reach another device: no remote copies, remote signals or barrier semaphores. Data moves between devices by JAX's collectives and lax.ppermute only.
A program may use at most 64 MiB of HBM per device.

v0:
```python
import jax
import jax.numpy as jnp
from jax import lax
from jax.sharding import PartitionSpec as P

half_root = 0.7071067811865476
inv_root_two_pi = 0.3989422804014327


def gelu_value(value):
    return 0.5 * value * (1.0 + jax.scipy.special.erf(value * half_root))


def gelu_slope(value):
    return (
        0.5 * (1.0 + jax.scipy.special.erf(value * half_root))
        + value * jnp.exp(-0.5 * value * value) * inv_root_two_pi
    )


def shards(tokens, first_right, first_left, second_right, second_left, cotangent):
    fp = jnp.float32
    bf = jnp.bfloat16
    tok_rows = tokens.shape[0]
    in_blocks = first_right.shape[0]
    block_width = first_right.shape[1]
    wide_width = first_right.shape[2]
    hid_blocks = first_left.shape[0]
    groups = lax.axis_size("tensor")
    replicas = lax.axis_size("dp")
    all_in = in_blocks * groups
    all_hid = hid_blocks * groups
    sub_width = wide_width // all_hid
    grad_scale = float(tok_rows * replicas) ** (-0.5)
    right_one = first_right.reshape(in_blocks, block_width, all_hid, sub_width)
    right_two = second_right.reshape(hid_blocks, block_width, all_in, sub_width)
    tok_parts = tokens.reshape(tok_rows, in_blocks, block_width)
    cot_parts = cotangent.reshape(tok_rows, in_blocks, block_width)
    up_inner = jnp.einsum("tkb,kbjg->jkgt", tok_parts, right_one, preferred_element_type=fp).astype(
        bf
    )
    arrived = lax.all_to_all(up_inner, "tensor", split_axis=0, concat_axis=1, tiled=True)
    mixed_piece = arrived.reshape(hid_blocks, block_width, arrived.shape[3])
    pre_piece = jnp.einsum("jbt,jbc->jct", mixed_piece, first_left, preferred_element_type=fp)
    hidden = gelu_value(pre_piece).astype(bf)
    down_inner = jnp.einsum("jbt,jbkg->kjgt", hidden, right_two, preferred_element_type=fp).astype(
        bf
    )
    mixed_down = lax.all_to_all(down_inner, "tensor", split_axis=0, concat_axis=1, tiled=True)
    mixed_down = mixed_down.reshape(in_blocks, wide_width, tok_rows)
    layer_out = jnp.einsum(
        "kwt,kwc->tkc", mixed_down, second_left, preferred_element_type=fp
    ).astype(bf)
    layer_out = layer_out.reshape(tok_rows, in_blocks * block_width)
    reduced = {}
    d_mixed_down = jnp.einsum(
        "tkc,kwc->kwt", cot_parts, second_left, preferred_element_type=fp
    ).astype(bf)
    d_mixed_down = d_mixed_down.reshape(in_blocks, all_hid, sub_width, tok_rows)
    d_down_inner = lax.all_to_all(d_mixed_down, "tensor", split_axis=1, concat_axis=0, tiled=True)
    d_hidden = jnp.einsum("kjgt,jbkg->jbt", d_down_inner, right_two, preferred_element_type=fp)
    d_pre = (d_hidden * gelu_slope(pre_piece)).astype(bf)
    d_mixed_up = jnp.einsum("jct,jbc->jbt", d_pre, first_left, preferred_element_type=fp).astype(bf)
    d_mixed_up = d_mixed_up.reshape(hid_blocks, all_in, sub_width, tok_rows)
    d_up_inner = lax.all_to_all(d_mixed_up, "tensor", split_axis=1, concat_axis=0, tiled=True)
    grad_tokens = jnp.einsum(
        "jkgt,kbjg->tkb", d_up_inner, right_one, preferred_element_type=fp
    ).astype(bf)
    grad_tokens = grad_tokens.reshape(tok_rows, in_blocks * block_width)
    result = jnp.einsum("jbt,kjgt->bjkg", hidden, d_down_inner, preferred_element_type=fp)
    term_result = jnp.einsum("tkb,jkgt->bkjg", tok_parts, d_up_inner, preferred_element_type=fp)
    summed = (
        lax.psum_scatter(
            (term_result.reshape(block_width, in_blocks, wide_width) * grad_scale).astype(
                jnp.bfloat16
            ),
            "dp",
            scatter_dimension=0,
            tiled=True,
        ).astype(jnp.float32),
        lax.psum_scatter(
            (
                jnp.einsum("jbt,jct->bjc", mixed_piece, d_pre, preferred_element_type=fp)
                * grad_scale
            ).astype(jnp.bfloat16),
            "dp",
            scatter_dimension=0,
            tiled=True,
        ).astype(jnp.float32),
        lax.psum_scatter(
            (result.reshape(block_width, hid_blocks, block_width) * grad_scale).astype(
                jnp.bfloat16
            ),
            "dp",
            scatter_dimension=0,
            tiled=True,
        ).astype(jnp.float32),
        lax.psum_scatter(
            (
                jnp.einsum("kwt,tkc->wkc", mixed_down, cot_parts, preferred_element_type=fp)
                * grad_scale
            ).astype(jnp.bfloat16),
            "dp",
            scatter_dimension=0,
            tiled=True,
        ).astype(jnp.float32),
    )
    reduced["right_one"] = summed[0]
    reduced["left_one"] = summed[1]
    reduced["right_two"] = summed[2]
    reduced["left_two"] = summed[3]
    grad_right_one = jnp.transpose(reduced["right_one"], (1, 0, 2))
    grad_left_one = jnp.transpose(reduced["left_one"], (1, 0, 2))
    grad_right_two = jnp.transpose(reduced["right_two"], (1, 0, 2))
    grad_left_two = jnp.transpose(reduced["left_two"], (1, 0, 2))
    return (layer_out, grad_tokens, grad_right_one, grad_left_one, grad_right_two, grad_left_two)


def solution(mesh):
    in_specs = (
        P("dp", "tensor"),
        P("tensor", None, None),
        P("tensor", None, None),
        P("tensor", None, None),
        P("tensor", None, None),
        P("dp", "tensor"),
    )
    out_specs = (
        P("dp", "tensor"),
        P("dp", "tensor"),
        P("tensor", "dp", None),
        P("tensor", "dp", None),
        P("tensor", "dp", None),
        P("tensor", "dp", None),
    )
    return jax.shard_map(shards, mesh=mesh, in_specs=in_specs, out_specs=out_specs, check_vma=False)
```

profile of v0, /device:TPU:1, one launch (start us, length us, event | category | flops | bytes accessed | tf_op | source)
XLA Modules:
  0.0 503.9 jit_solution(12077980124356621023)
XLA Ops:
  7.2 0.0 copy-start
  7.2 1.3 copy.71
  8.5 1.4 fusion.10
  9.9 0.0 copy-start.4
  9.9 0.0 copy-start.7
  9.9 1.6 copy.73
  11.5 14.3 %all-to-all-start = ((bf16[128,1,8,512]{3,2,1,0:T(8,128)(2,1)}), bf16[128,1,8,512]{3,2,1,0:T(8,128)(2,1)S(1)}, u32[]{:S(2)}, u32[]{:S(2)}) async-start(bf16[128,1,8,512]{3,2,1,0:T(8,128)(2,1)} %copy.73), calls=%async_computation | async-start | bytes 2097152 | tf_op jit(solution)/shard_map/all_to_all | solution.py:42
  25.8 0.0 copy-done.4
  25.8 0.0 copy-done.7
  25.8 1.5 fusion.11
  27.3 24.4 %all-to-all-done = bf16[128,1,8,512]{3,2,1,0:T(8,128)(2,1)S(1)} async-done(((bf16[128,1,8,512]{3,2,1,0:T(8,128)(2,1)}), bf16[128,1,8,512]{3,2,1,0:T(8,128)(2,1)S(1)}, u32[]{:S(2)}, u32[]{:S(2)}) %all-to-all-start) | async-done | bytes 1048608 | tf_op jit(solution)/shard_map/all_to_all | solution.py:42
  51.6 7.6 %all-to-all-start.2 = ((bf16[1,128,8,512]{3,2,0,1:T(8,128)(2,1)}), bf16[1,128,8,512]{3,2,0,1:T(8,128)(2,1)S(1)}, u32[]{:S(2)}, u32[]{:S(2)}) async-start(bf16[1,128,8,512]{3,2,0,1:T(8,128)(2,1)} %fusion.11), calls=%async_computation.2 | async-start | bytes 2097152 | tf_op jit(solution)/shard_map/all_to_all | solution.py:60
  59.2 2.0 copy.76
  61.3 0.0 copy-start.6
  61.3 0.0 copy-done
  61.3 0.5 fusion.25
  61.8 0.0 copy-start.1
  61.8 1.3 copy-done.1
  63.1 0.0 copy-done.6
  63.1 0.7 fusion.12
  63.9 1.5 copy.79
  65.4 19.5 %all-to-all-done.2 = bf16[1,128,8,512]{3,2,0,1:T(8,128)(2,1)S(1)} async-done(((bf16[1,128,8,512]{3,2,0,1:T(8,128)(2,1)}), bf16[1,128,8,512]{3,2,0,1:T(8,128)(2,1)S(1)}, u32[]{:S(2)}, u32[]{:S(2)}) %all-to-all-start.2) | async-done | bytes 1048608 | tf_op jit(solution)/shard_map/all_to_all | solution.py:60
  84.9 0.0 copy-start.3
  84.9 1.0 copy-done.3
  85.9 7.7 %all-to-all-start.1 = ((bf16[32,4,8,512]{3,2,1,0:T(8,128)(2,1)}), bf16[32,4,8,512]{3,2,1,0:T(8,128)(2,1)S(1)}, u32[]{:S(2)}, u32[]{:S(2)}) async-start(bf16[32,4,8,512]{3,2,1,0:T(8,128)(2,1)} %copy.79), calls=%async_computation.1 | async-start | bytes 2097152 | tf_op jit(solution)/shard_map/all_to_all | solution.py:49
  93.7 3.2 fusion.5
  96.9 0.0 copy-start.2
  96.9 0.5 fusion.13
  97.4 0.5 copy-done.2
  97.9 1.1 copy.83
  99.0 20.4 %all-to-all-done.1 = bf16[32,4,8,512]{3,2,1,0:T(8,128)(2,1)S(1)} async-done(((bf16[32,4,8,512]{3,2,1,0:T(8,128)(2,1)}), bf16[32,4,8,512]{3,2,1,0:T(8,128)(2,1)S(1)}, u32[]{:S(2)}, u32[]{:S(2)}) %all-to-all-start.1) | async-done | bytes 1048608 | tf_op jit(solution)/shard_map/all_to_all | solution.py:49
  119.4 7.9 %all-to-all-start.3 = ((bf16[4,32,8,512]{3,2,0,1:T(8,128)(2,1)}), bf16[4,32,8,512]{3,2,0,1:T(8,128)(2,1)}, u32[]{:S(2)}, u32[]{:S(2)}) async-start(bf16[4,32,8,512]{3,2,0,1:T(8,128)(2,1)} %copy.83), calls=%async_computation.3 | async-start | bytes 2097152 | tf_op jit(solution)/shard_map/all_to_all | solution.py:65
  127.2 0.0 reduce-scatter.3.cloned.1.call-start
  127.3 3.4 fusion.20
  130.7 2.0 copy.91
  132.7 0.0 reduce-scatter.3.cloned.1.call-update
  132.7 0.0 reduce-scatter.5.cloned.1.call-start
  132.8 1.3 dynamic-slice
  134.7 1.3 fusion.18
  136.0 0.0 reduce-scatter.5.cloned.1.call-update
  136.0 0.0 copy-start.8
  136.0 0.0 all-reduce.5.cloned.1.call-start
  136.1 2.6 fusion.21
  138.6 2.1 copy.88
  140.7 74.1 %reduce-scatter.3.cloned.1.call-done = bf16[16,4,256]{2,0,1:T(8,128)(2,1)} async-done(((bf16[256,4,256]{2,0,1:T(8,128)(2,1)}), bf16[16,4,256]{2,0,1:T(8,128)(2,1)}) %reduce-scatter.3.cloned.1.call-update) | async-done | bytes 32784 | tf_op jit(solution)/shard_map/reduce_scatter | solution.py:90
  214.8 1.4 convert_bitcast_fusion
  216.2 0.0 all-to-all-done.3
  216.2 0.0 copy-done.8
  216.2 0.0 copy-start.5
  216.2 2.0 fusion.19
  218.3 0.3 copy.122
  218.6 2.1 copy.86
  220.7 0.0 copy-done.5
  220.7 1.2 convolution_convert_fusion.4
  221.9 0.0 all-reduce.5.cloned.1.call-update
  221.9 2.5 fusion.22
  224.3 76.8 %reduce-scatter.5.cloned.1.call-done = bf16[64,1,256]{2,0,1:T(8,128)(2,1)} async-done(((bf16[1024,1,256]{2,0,1:T(8,128)(2,1)}), bf16[64,1,256]{2,0,1:T(8,128)(2,1)}) %reduce-scatter.5.cloned.1.call-update) | async-done | bytes 32784 | tf_op jit(solution)/shard_map/reduce_scatter | solution.py:98
  301.1 1.4 bitcast_convert_fusion.1
  302.5 191.9 %all-reduce.5.cloned.1.call-done = (bf16[256,1,1024]{2,1,0:T(2,128)(2,1)}, bf16[256,4,256]{2,1,0:T(4,128)(2,1)}) async-done(((bf16[256,1,1024]{2,1,0:T(2,128)(2,1)}, bf16[256,4,256]{2,1,0:T(4,128)(2,1)}), (bf16[256,1,1024]{2,1,0:T(2,128)(2,1)}, bf16[256,4,256]{2,1,0:T(4,128)(2,1)})) %all-reduce.5.cloned.1.call-update) | async-done | bytes 1048592
  494.4 0.9 bitcast_convert_fusion
  495.3 0.8 convert_bitcast_fusion.1
  496.1 0.6 copy.93
  496.7 0.6 copy.92
Async XLA Ops:
  7.2 54.1 %copy-start = (bf16[4,256,256]{2,1,0:T(8,128)(2,1)S(1)}, bf16[4,256,256]{2,1,0:T(8,128)(2,1)}, u32[]{:S(2)}) copy-start(bf16[4,256,256]{2,1,0:T(8,128)(2,1)} %param.8) | copy-start | bytes 1572868
  9.9 15.9 %copy-start.4 = (bf16[1,1024,256]{2,1,0:T(8,128)(2,1)S(1)}, bf16[1,1024,256]{2,1,0:T(8,128)(2,1)}, u32[]{:S(2)}) copy-start(bf16[1,1024,256]{2,1,0:T(8,128)(2,1)} %param.10) | copy-start | bytes 1572868
  9.9 15.9 %copy-start.7 = (bf16[512,256]{1,0:T(8,128)(2,1)S(1)}, bf16[512,256]{1,0:T(8,128)(2,1)}, u32[]{:S(2)}) copy-start(bf16[512,256]{1,0:T(8,128)(2,1)} %param.11) | copy-start | bytes 786436
  11.5 40.1 %all-to-all-start = ((bf16[128,1,8,512]{3,2,1,0:T(8,128)(2,1)}), bf16[128,1,8,512]{3,2,1,0:T(8,128)(2,1)S(1)}, u32[]{:S(2)}, u32[]{:S(2)}) async-start(bf16[128,1,8,512]{3,2,1,0:T(8,128)(2,1)} %copy.73), calls=%async_computation | async-start | bytes 2097152 | tf_op jit(solution)/shard_map/all_to_all | solution.py:42
  51.6 33.3 %all-to-all-start.2 = ((bf16[1,128,8,512]{3,2,0,1:T(8,128)(2,1)}), bf16[1,128,8,512]{3,2,0,1:T(8,128)(2,1)S(1)}, u32[]{:S(2)}, u32[]{:S(2)}) async-start(bf16[1,128,8,512]{3,2,0,1:T(8,128)(2,1)} %fusion.11), calls=%async_computation.2 | async-start | bytes 2097152 | tf_op jit(solution)/shard_map/all_to_all | solution.py:60
  61.3 1.9 copy-start.6
  61.8 1.3 copy-start.1
  84.9 1.0 copy-start.3
  85.9 33.4 %all-to-all-start.1 = ((bf16[32,4,8,512]{3,2,1,0:T(8,128)(2,1)}), bf16[32,4,8,512]{3,2,1,0:T(8,128)(2,1)S(1)}, u32[]{:S(2)}, u32[]{:S(2)}) async-start(bf16[32,4,8,512]{3,2,1,0:T(8,128)(2,1)} %copy.79), calls=%async_computation.1 | async-start | bytes 2097152 | tf_op jit(solution)/shard_map/all_to_all | solution.py:49
  96.9 1.0 copy-start.2
  119.4 96.8 %all-to-all-start.3 = ((bf16[4,32,8,512]{3,2,0,1:T(8,128)(2,1)}), bf16[4,32,8,512]{3,2,0,1:T(8,128)(2,1)}, u32[]{:S(2)}, u32[]{:S(2)}) async-start(bf16[4,32,8,512]{3,2,0,1:T(8,128)(2,1)} %copy.83), calls=%async_computation.3 | async-start | bytes 2097152 | tf_op jit(solution)/shard_map/all_to_all | solution.py:65
  127.2 87.6 %reduce-scatter.3.cloned.1.call-start = ((), (), s32[]{:S(2)}) async-start(), calls=%async_computation.6 | async-start | bytes 557056 | tf_op jit(solution)/shard_map/reduce_scatter | solution.py:90
  132.7 168.4 %reduce-scatter.5.cloned.1.call-start = ((), (), s32[]{:S(2)}) async-start(), calls=%async_computation.7 | async-start | bytes 557056 | tf_op jit(solution)/shard_map/reduce_scatter | solution.py:98
  136.0 80.2 %copy-start.8 = (bf16[512,256]{1,0:T(8,128)(2,1)S(1)}, bf16[512,256]{1,0:T(8,128)(2,1)}, u32[]{:S(2)}) copy-start(bf16[512,256]{1,0:T(8,128)(2,1)} %param.6) | copy-start | bytes 786436
  136.0 358.4 %all-reduce.5.cloned.1.call-start = ((), (), s32[]{:S(2)}) async-start(), calls=%async_computation.8 | async-start | bytes 3145728
  216.2 4.5 copy-start.5
Sparse Core Ops, SparseCore 0:
  132.9 81.9 reduce-scatter.2
  219.4 81.6 reduce-scatter.4
  304.1 190.2 all-reduce.4
where the time goes:
time: 505 us; the launch traced here: 504 us
  waiting for transfers between devices  407 us (81%)
  starting transfers between devices  37.6 us (7%)
  matrix products  20.7 us (4%)
  local copies, waits for them, and re-layouts  19.5 us (4%)
  between operations  14.6 us (3%)
    unnamed x4, waiting for transfers between devices  192 us
    reduce_scatter x1, waiting for transfers between devices, shards(): lax.psum_scatter((jnp.einsum('kwt,tkc->wkc', mixed_down, cot_parts, prefe...  76.8 us
    reduce_scatter x1, waiting for transfers between devices, shards(): lax.psum_scatter((result.reshape(block_width, hid_blocks, block_width) *...  74.1 us
    all_to_all x1, waiting for transfers between devices, shards(): lax.all_to_all(up_inner, 'tensor', split_axis=0, concat_axis=1, tiled=True)  24.4 us
    all_to_all x1, waiting for transfers between devices, shards(): lax.all_to_all(down_inner, 'tensor', split_axis=0, concat_axis=1, tiled=T...  20.4 us
    all_to_all x1, waiting for transfers between devices, shards(): lax.all_to_all(d_mixed_down, 'tensor', split_axis=1, concat_axis=0, tiled...  19.5 us
    all_to_all x1, starting transfers between devices, shards(): lax.all_to_all(up_inner, 'tensor', split_axis=0, concat_axis=1, tiled=True)  14.3 us
  transfers between devices with their start and end apart: 7, of which 6 were waited for; matrix products, arithmetic and copies ran while one was open for 7% of the time, Pallas kernels for 0%

commit v1 on v0

--- a/solution.py
+++ b/solution.py
@@ -16,6 +16,34 @@
         0.5 * (1.0 + jax.scipy.special.erf(value * half_root))
         + value * jnp.exp(-0.5 * value * value) * inv_root_two_pi
     )
+
+
+def dp_bit_order(replicas):
+    bits = replicas.bit_length() - 1
+    assert 1 << bits == replicas
+    preferred = [0, 2, 3, 1]
+    if bits == 4:
+        return preferred
+    return list(range(bits))
+
+
+def dp_reduce_scatter(buf, replicas):
+    idx = lax.axis_index("dp")
+    order = dp_bit_order(replicas)
+    bits = len(order)
+    width = buf.shape[1]
+    buf = buf.reshape((2,) * bits + (width,))
+    live = list(range(bits - 1, -1, -1))
+    for bit in order:
+        axis = live.index(bit)
+        me = (idx >> bit) & 1
+        keep = lax.dynamic_index_in_dim(buf, me, axis, keepdims=False)
+        send = lax.dynamic_index_in_dim(buf, 1 - me, axis, keepdims=False)
+        perm = [(i, i ^ (1 << bit)) for i in range(replicas)]
+        got = lax.ppermute(send.astype(jnp.bfloat16), "dp", perm)
+        buf = keep + got.astype(jnp.float32)
+        live.pop(axis)
+    return buf.reshape(width)
 
 
 def shards(tokens, first_right, first_left, second_right, second_left, cotangent):
@@ -67,52 +95,23 @@
         "jkgt,kbjg->tkb", d_up_inner, right_one, preferred_element_type=fp
     ).astype(bf)
     grad_tokens = grad_tokens.reshape(tok_rows, in_blocks * block_width)
-    result = jnp.einsum("jbt,kjgt->bjkg", hidden, d_down_inner, preferred_element_type=fp)
-    term_result = jnp.einsum("tkb,jkgt->bkjg", tok_parts, d_up_inner, preferred_element_type=fp)
-    summed = (
-        lax.psum_scatter(
-            (term_result.reshape(block_width, in_blocks, wide_width) * grad_scale).astype(
-                jnp.bfloat16
-            ),
-            "dp",
-            scatter_dimension=0,
-            tiled=True,
-        ).astype(jnp.float32),
-        lax.psum_scatter(
-            (
-                jnp.einsum("jbt,jct->bjc", mixed_piece, d_pre, preferred_element_type=fp)
-                * grad_scale
-            ).astype(jnp.bfloat16),
-            "dp",
-            scatter_dimension=0,
-            tiled=True,
-        ).astype(jnp.float32),
-        lax.psum_scatter(
-            (result.reshape(block_width, hid_blocks, block_width) * grad_scale).astype(
-                jnp.bfloat16
-            ),
-            "dp",
-            scatter_dimension=0,
-            tiled=True,
-        ).astype(jnp.float32),
-        lax.psum_scatter(
-            (
-                jnp.einsum("kwt,tkc->wkc", mixed_down, cot_parts, preferred_element_type=fp)
-                * grad_scale
-            ).astype(jnp.bfloat16),
-            "dp",
-            scatter_dimension=0,
-            tiled=True,
-        ).astype(jnp.float32),
+    grads = (
+        jnp.einsum("tkb,jkgt->bkjg", tok_parts, d_up_inner, preferred_element_type=fp),
+        jnp.einsum("jbt,jct->bjc", mixed_piece, d_pre, preferred_element_type=fp),
+        jnp.einsum("jbt,kjgt->bjkg", hidden, d_down_inner, preferred_element_type=fp),
+        jnp.einsum("kwt,tkc->wkc", mixed_down, cot_parts, preferred_element_type=fp),
     )
-    reduced["right_one"] = summed[0]
-    reduced["left_one"] = summed[1]
-    reduced["right_two"] = summed[2]
-    reduced["left_two"] = summed[3]
-    grad_right_one = jnp.transpose(reduced["right_one"], (1, 0, 2))
-    grad_left_one = jnp.transpose(reduced["left_one"], (1, 0, 2))
-    grad_right_two = jnp.transpose(reduced["right_two"], (1, 0, 2))
-    grad_left_two = jnp.transpose(reduced["left_two"], (1, 0, 2))
+    pieces = [g.reshape(replicas, -1) for g in grads]
+    widths = [p.shape[1] for p in pieces]
+    total = dp_reduce_scatter(jnp.concatenate(pieces, axis=1), replicas) * grad_scale
+    outs = []
+    offset = 0
+    for g, w in zip(grads, widths):
+        part = total[offset : offset + w]
+        offset += w
+        lead = g.shape[0] // replicas
+        outs.append(jnp.transpose(part.reshape(lead, g.shape[1], -1), (1, 0, 2)))
+    grad_right_one, grad_left_one, grad_right_two, grad_left_two = outs
     return (layer_out, grad_tokens, grad_right_one, grad_left_one, grad_right_two, grad_left_two)
 
 

time: 505 us -> 253 us (0.50)
  waiting for transfers between devices: 407 us -> 85.1 us
  local copies, waits for them, and re-layouts: 19.5 us -> 81.7 us
  starting transfers between devices: 37.6 us -> 53.1 us
  between operations: 14.6 us -> 0.98 us
    unnamed x4 -> x0, waiting for transfers between devices: 192 us -> none
    reduce_scatter x2 -> x0, waiting for transfers between devices: 151 us -> none  [the longest x1 76.8 us: shards(): lax.psum_scatter((jnp.einsum('kwt,tkc->wkc', mixed_down, cot_parts, prefe...]
    concatenate x0 -> x5, local copies, waits for them, and re-layouts: none -> 30.4 us  [shards(): jnp.concatenate(pieces, axis=1)]
    transpose x0 -> x3, local copies, waits for them, and re-layouts: none -> 30.4 us  [the longest x1 14.2 us: shards(): jnp.einsum('jbt,kjgt->bjkg', hidden, d_down_inner, preferred_element_type...]
    all_to_all x1, waiting for transfers between devices: 0.01 us -> 21.8 us  [shards(): lax.all_to_all(d_mixed_up, 'tensor', split_axis=1, concat_axis=0, tiled=T...]
    all_to_all x1, waiting for transfers between devices: 20.4 us -> 0.01 us  [shards(): lax.all_to_all(down_inner, 'tensor', split_axis=0, concat_axis=1, tiled=T...]
    ppermute x0 -> x4, waiting for transfers between devices: none -> 17.1 us  [dp_reduce_scatter(): got = lax.ppermute(send.astype(jnp.bfloat16), 'dp', perm)]
    ppermute x0 -> x4, starting transfers between devices: none -> 15.3 us  [dp_reduce_scatter(): got = lax.ppermute(send.astype(jnp.bfloat16), 'dp', perm)]
  transfers between devices with their start and end apart: 7 -> 8, of which waited for: 6 -> 7; matrix products, arithmetic and copies ran while one was open for 7% -> 22% of each run, Pallas kernels for 0% -> 0%
where the time goes in v1:
time: 253 us; the launch traced here: 248 us
  waiting for transfers between devices  85.1 us (34%)
  local copies, waits for them, and re-layouts  81.7 us (32%)
  starting transfers between devices  53.1 us (21%)
  matrix products  24.5 us (10%)
  other arithmetic  2.92 us (1%)
    concatenate x5, local copies, waits for them, and re-layouts, shards(): jnp.concatenate(pieces, axis=1)  30.4 us
    all_to_all x1, waiting for transfers between devices, shards(): lax.all_to_all(up_inner, 'tensor', split_axis=0, concat_axis=1, tiled=True)  24.4 us
    all_to_all x1, waiting for transfers between devices, shards(): lax.all_to_all(d_mixed_down, 'tensor', split_axis=1, concat_axis=0, tiled...  21.8 us
    all_to_all x1, waiting for transfers between devices, shards(): lax.all_to_all(d_mixed_up, 'tensor', split_axis=1, concat_axis=0, tiled=T...  21.8 us
    ppermute x4, waiting for transfers between devices, dp_reduce_scatter(): got = lax.ppermute(send.astype(jnp.bfloat16), 'dp', perm)  17.1 us
    ppermute x4, starting transfers between devices, dp_reduce_scatter(): got = lax.ppermute(send.astype(jnp.bfloat16), 'dp', perm)  15.3 us
    all_to_all x1, starting transfers between devices, shards(): lax.all_to_all(up_inner, 'tensor', split_axis=0, concat_axis=1, tiled=True)  14.3 us
    transpose x1, local copies, waits for them, and re-layouts, shards(): jnp.einsum('jbt,kjgt->bjkg', hidden, d_down_inner, preferred_element_type...  14.2 us
  transfers between devices with their start and end apart: 8, of which 7 were waited for; matrix products, arithmetic and copies ran while one was open for 22% of the time, Pallas kernels for 0%

profile of v1, /device:TPU:1, one launch (start us, length us, event | category | flops | bytes accessed | tf_op | source)
XLA Modules:
  0.0 248.3 jit_solution(9206176117885369486)
XLA Ops:
  0.6 0.0 copy-start
  0.6 1.3 copy.69
  2.0 1.4 fusion.10
  3.4 0.0 copy-start.7
  3.4 0.0 copy-start.8
  3.4 1.6 copy.71
  5.0 14.3 %all-to-all-start = ((bf16[128,1,8,512]{3,2,1,0:T(8,128)(2,1)}), bf16[128,1,8,512]{3,2,1,0:T(8,128)(2,1)S(1)}, u32[]{:S(2)}, u32[]{:S(2)}) async-start(bf16[128,1,8,512]{3,2,1,0:T(8,128)(2,1)} %copy.71), calls=%async_computation | async-start | bytes 2097152 | tf_op jit(solution)/shard_map/all_to_all | solution.py:70
  19.3 1.4 fusion.11
  20.7 24.4 %all-to-all-done = bf16[128,1,8,512]{3,2,1,0:T(8,128)(2,1)S(1)} async-done(((bf16[128,1,8,512]{3,2,1,0:T(8,128)(2,1)}), bf16[128,1,8,512]{3,2,1,0:T(8,128)(2,1)S(1)}, u32[]{:S(2)}, u32[]{:S(2)}) %all-to-all-start) | async-done | bytes 1048608 | tf_op jit(solution)/shard_map/all_to_all | solution.py:70
  45.1 7.6 %all-to-all-start.2 = ((bf16[1,128,8,512]{3,2,0,1:T(8,128)(2,1)}), bf16[1,128,8,512]{3,2,0,1:T(8,128)(2,1)S(1)}, u32[]{:S(2)}, u32[]{:S(2)}) async-start(bf16[1,128,8,512]{3,2,0,1:T(8,128)(2,1)} %fusion.11), calls=%async_computation.2 | async-start | bytes 2097152 | tf_op jit(solution)/shard_map/all_to_all | solution.py:88
  52.7 2.0 copy.74
  54.7 1.9 fusion.17
  56.6 21.8 %all-to-all-done.2 = bf16[1,128,8,512]{3,2,0,1:T(8,128)(2,1)S(1)} async-done(((bf16[1,128,8,512]{3,2,0,1:T(8,128)(2,1)}), bf16[1,128,8,512]{3,2,0,1:T(8,128)(2,1)S(1)}, u32[]{:S(2)}, u32[]{:S(2)}) %all-to-all-start.2) | async-done | bytes 1048608 | tf_op jit(solution)/shard_map/all_to_all | solution.py:88
  78.4 1.0 copy-done.5
  79.4 3.2 %fusion.5 = bf16[4,256,512]{1,2,0:T(8,128)(2,1)S(1)} fusion(f32[4,512,256]{2,1,0:T(8,128)} %fusion.17, bf16[32,4,8,512]{3,2,1,0:T(8,128)(2,1)} %bitcast.129, bf16[4,256,256]{1,2,0:T(8,128)(2,1)} %copy.74), kind=kOutput, calls=%fused_computation.6 | convolution fusion | flops 273678336 | bytes 4718592 | tf_op jit(solution)/shard_map/kjgt,jbkg->jbt/dot_general | solution.py:89
  82.6 0.5 fusion.13
  83.1 1.1 copy.81
  84.2 7.9 %all-to-all-start.3 = ((bf16[4,32,8,512]{3,2,0,1:T(8,128)(2,1)}), bf16[4,32,8,512]{3,2,0,1:T(8,128)(2,1)}, u32[]{:S(2)}, u32[]{:S(2)}) async-start(bf16[4,32,8,512]{3,2,0,1:T(8,128)(2,1)} %copy.81), calls=%async_computation.3 | async-start | bytes 2097152 | tf_op jit(solution)/shard_map/all_to_all | solution.py:93
  92.0 2.3 fusion.12
  94.3 1.6 copy.77
  95.9 21.8 %all-to-all-done.3 = bf16[4,32,8,512]{3,2,0,1:T(8,128)(2,1)} async-done(((bf16[4,32,8,512]{3,2,0,1:T(8,128)(2,1)}), bf16[4,32,8,512]{3,2,0,1:T(8,128)(2,1)}, u32[]{:S(2)}, u32[]{:S(2)}) %all-to-all-start.3) | async-done | bytes 1048608 | tf_op jit(solution)/shard_map/all_to_all | solution.py:93
  117.7 8.1 %all-to-all-start.1 = ((bf16[32,4,8,512]{3,2,1,0:T(8,128)(2,1)}), bf16[32,4,8,512]{3,2,1,0:T(8,128)(2,1)}, u32[]{:S(2)}, u32[]{:S(2)}) async-start(bf16[32,4,8,512]{3,2,1,0:T(8,128)(2,1)} %copy.77), calls=%async_computation.1 | async-start | bytes 2097152 | tf_op jit(solution)/shard_map/all_to_all | solution.py:77
  125.8 1.5 convolution_bitcast_fusion.2
  127.3 2.7 %copy.85 = f32[256,4,256]{2,1,0:T(4,128)} copy(f32[256,4,256]{0,2,1:T(8,128)} %convolution_bitcast_fusion.2) | data formatting | bytes 2097152 | tf_op jit(solution)/shard_map/jbt,jct->bjc/transpose | solution.py:100
  130.0 3.1 %concatenate.13 = f32[2,2,2,2,16384]{4,3,2,1,0:T(2,128)} reshape(f32[256,4,256]{2,1,0:T(4,128)} %copy.85) | data formatting | bytes 2097152 | tf_op jit(solution)/shard_map/concatenate | solution.py:106
  133.1 2.8 %convolution_bitcast_fusion.1 = f32[256,4,32,8]{0,3,2,1:T(8,128)} fusion(bf16[32,4,8,512]{3,2,1,0:T(8,128)(2,1)} %bitcast.130, f32[4,512,256]{2,1,0:T(8,128)S(1)} %copy-done.2), kind=kOutput, calls=%fused_computation.22 | convolution fusion | flops 271056896 | bytes 4194304 | tf_op jit(solution)/shard_map/jbt,kjgt->bjkg/dot_general | solution.py:101
  135.9 14.2 %copy.88 = f32[256,4,32,8]{3,2,1,0:T(8,128)} copy(f32[256,4,32,8]{0,3,2,1:T(8,128)} %convolution_bitcast_fusion.1) | data formatting | bytes 2097152 | tf_op jit(solution)/shard_map/jbt,kjgt->bjkg/transpose | solution.py:101
  150.2 12.1 %concatenate.14 = f32[2,2,2,2,16384]{4,3,2,1,0:T(2,128)S(1)} reshape(f32[256,4,32,8]{3,2,1,0:T(8,128)} %copy.88) | data formatting | bytes 2097152 | tf_op jit(solution)/shard_map/concatenate | solution.py:106
  162.2 1.9 convolution_bitcast_fusion.3
  164.2 2.6 %convolution_bitcast_fusion = f32[1024,1,256]{2,0,1:T(8,128)} fusion(bf16[1024,512]{1,0:T(8,128)(2,1)} %bitcast.10, bf16[512,256]{1,0:T(8,128)(2,1)S(1)} %copy-done.7), kind=kOutput, calls=%fused_computation.21 | convolution fusion | flops 268435456 | bytes 2359296 | tf_op jit(solution)/shard_map/kwt,tkc->wkc/dot_general | solution.py:102
  166.8 2.9 %concatenate.15 = f32[2,2,2,2,16384]{4,3,2,1,0:T(2,128)} reshape(f32[1024,1,256]{2,0,1:T(8,128)} %convolution_bitcast_fusion) | data formatting | bytes 2097152 | tf_op jit(solution)/shard_map/concatenate | solution.py:106
  169.7 13.4 %copy.83 = f32[256,1,128,8]{3,2,0,1:T(8,128)} copy(f32[256,1,128,8]{0,2,3,1:T(8,128)S(1)} %convolution_bitcast_fusion.3) | data formatting | bytes 2097152 | tf_op jit(solution)/shard_map/tkb,jkgt->bkjg/transpose | solution.py:99
  183.2 12.2 %concatenate.12 = f32[2,2,2,2,16384]{4,3,2,1,0:T(2,128)S(1)} reshape(f32[256,1,128,8]{3,2,0,1:T(8,128)} %copy.83) | data formatting | bytes 2097152 | tf_op jit(solution)/shard_map/concatenate | solution.py:106
  195.4 0.1 constant_dynamic-update-slice_fusion.3
  195.5 1.1 copy-done.3
  196.6 0.1 constant_dynamic-update-slice_fusion.2
  196.8 0.1 constant_dynamic-update-slice_fusion.1
  196.9 0.9 copy-done.4
  197.9 0.1 constant_dynamic-update-slice_fusion
  198.0 1.9 dynamic-slice_convert_fusion
  199.9 1.6 copy.122
  201.5 2.8 %collective-permute-start = (bf16[2,2,2,65536]{3,2,1,0:T(2,128)(2,1)S(1)}, bf16[2,2,2,65536]{3,2,1,0:T(2,128)(2,1)S(1)}, u32[]{:S(2)}, u32[]{:S(2)}) collective-permute-start(bf16[2,2,2,65536]{3,2,1,0:T(2,128)(2,1)S(1)} %bitcast.132), channel_id=1, source_target_pairs={{0,32},{32,0},{64,96},{96,64},{128,160},{160,128},{192,224},{224,1... | collective-permute-start | bytes 3145736 | tf_op jit(solution)/shard_map/ppermute | solution.py:43
  204.3 2.2 constant_dynamic-slice_fusion.1
  206.5 0.1 collective-permute-done
  206.6 2.0 bitcast_add_fusion
  208.6 0.4 fusion.23
  209.0 3.1 %collective-permute-start.1 = (bf16[2,2,65536]{2,1,0:T(2,128)(2,1)S(1)}, bf16[2,2,65536]{2,1,0:T(2,128)(2,1)S(1)}, u32[]{:S(2)}, u32[]{:S(2)}) collective-permute-start(bf16[2,2,65536]{2,1,0:T(2,128)(2,1)S(1)} %fusion.23), channel_id=1, source_target_pairs={{0,128},{32,160},{64,192},{96,224},{128,0},{160,32},{192,64},{224,... | collective-permute-start | bytes 1572872 | tf_op jit(solution)/shard_map/ppermute | solution.py:43
  212.1 2.5 fusion.14
  214.6 9.4 %collective-permute-done.1 = bf16[2,2,65536]{2,1,0:T(2,128)(2,1)S(1)} collective-permute-done((bf16[2,2,65536]{2,1,0:T(2,128)(2,1)S(1)}, bf16[2,2,65536]{2,1,0:T(2,128)(2,1)S(1)}, u32[]{:S(2)}, u32[]{:S(2)}) %collective-permute-start.1) | collective-permute-done | bytes 524320 | tf_op jit(solution)/shard_map/ppermute | solution.py:43
  224.0 0.6 bitcast_add_fusion.1
  224.6 0.2 fusion.29
  224.8 4.6 %collective-permute-start.2 = (bf16[2,65536]{1,0:T(2,128)(2,1)S(1)}, bf16[2,65536]{1,0:T(2,128)(2,1)S(1)}, u32[]{:S(2)}, u32[]{:S(2)}) collective-permute-start(bf16[2,65536]{1,0:T(2,128)(2,1)S(1)} %fusion.29), channel_id=1, source_target_pairs={{0,256},{32,288},{64,320},{96,352},{128,384},{160,416},{192,448},{... | collective-permute-start | bytes 786440 | tf_op jit(solution)/shard_map/ppermute | solution.py:43
  229.4 0.0 copy-start.1
  229.4 2.5 convolution_convert_fusion.4
  231.9 2.9 %collective-permute-done.2 = bf16[2,65536]{1,0:T(2,128)(2,1)S(1)} collective-permute-done((bf16[2,65536]{1,0:T(2,128)(2,1)S(1)}, bf16[2,65536]{1,0:T(2,128)(2,1)S(1)}, u32[]{:S(2)}, u32[]{:S(2)}) %collective-permute-start.2) | collective-permute-done | bytes 262176 | tf_op jit(solution)/shard_map/ppermute | solution.py:43
  234.8 0.3 bitcast_add_fusion.2
  235.1 0.8 convert_reduce_fusion
  235.9 4.8 %collective-permute-start.3 = (bf16[65536]{0:T(1024)(128)(2,1)S(1)}, bf16[65536]{0:T(1024)(128)(2,1)S(1)}, u32[]{:S(2)}, u32[]{:S(2)}) collective-permute-start(bf16[65536]{0:T(1024)(128)(2,1)S(1)} %convert_reduce_fusion), channel_id=1, source_target_pairs={{0,64},{32,96},{64,0},{96,32},{128,192},{160,224},{192,128},{224,1... | collective-permute-start | bytes 393224 | tf_op jit(solution)/shard_map/ppermute | solution.py:43
  240.6 0.2 constant_dynamic-slice_fusion
  240.9 4.7 %collective-permute-done.3 = bf16[65536]{0:T(1024)(128)(2,1)S(1)} collective-permute-done((bf16[65536]{0:T(1024)(128)(2,1)S(1)}, bf16[65536]{0:T(1024)(128)(2,1)S(1)}, u32[]{:S(2)}, u32[]{:S(2)}) %collective-permute-start.3) | collective-permute-done | bytes 131104 | tf_op jit(solution)/shard_map/ppermute | solution.py:43
  245.6 0.6 slice.59
  246.3 0.6 copy.90
  247.0 0.6 copy.89
  247.7 0.6 slice.53
  (20 shorter events, 0.1 us)
Async XLA Ops:
  0.6 54.1 %copy-start = (bf16[4,256,256]{2,1,0:T(8,128)(2,1)S(1)}, bf16[4,256,256]{2,1,0:T(8,128)(2,1)}, u32[]{:S(2)}) copy-start(bf16[4,256,256]{2,1,0:T(8,128)(2,1)} %param.8) | copy-start | bytes 1572868
  3.4 15.9 %copy-start.7 = (bf16[512,256]{1,0:T(8,128)(2,1)S(1)}, bf16[512,256]{1,0:T(8,128)(2,1)}, u32[]{:S(2)}) copy-start(bf16[512,256]{1,0:T(8,128)(2,1)} %param.11) | copy-start | bytes 786436
  3.4 15.9 %copy-start.8 = (bf16[1,1024,256]{2,1,0:T(8,128)(2,1)S(1)}, bf16[1,1024,256]{2,1,0:T(8,128)(2,1)}, u32[]{:S(2)}) copy-start(bf16[1,1024,256]{2,1,0:T(8,128)(2,1)} %param.10) | copy-start | bytes 1572868
  5.0 40.2 %all-to-all-start = ((bf16[128,1,8,512]{3,2,1,0:T(8,128)(2,1)}), bf16[128,1,8,512]{3,2,1,0:T(8,128)(2,1)S(1)}, u32[]{:S(2)}, u32[]{:S(2)}) async-start(bf16[128,1,8,512]{3,2,1,0:T(8,128)(2,1)} %copy.71), calls=%async_computation | async-start | bytes 2097152 | tf_op jit(solution)/shard_map/all_to_all | solution.py:70
  45.1 33.3 %all-to-all-start.2 = ((bf16[1,128,8,512]{3,2,0,1:T(8,128)(2,1)}), bf16[1,128,8,512]{3,2,0,1:T(8,128)(2,1)S(1)}, u32[]{:S(2)}, u32[]{:S(2)}) async-start(bf16[1,128,8,512]{3,2,0,1:T(8,128)(2,1)} %fusion.11), calls=%async_computation.2 | async-start | bytes 2097152 | tf_op jit(solution)/shard_map/all_to_all | solution.py:88
  78.4 1.0 copy-start.5
  83.1 9.0 %copy-start.10 = (bf16[4,256,256]{1,2,0:T(8,128)(2,1)S(1)}, bf16[4,256,256]{1,2,0:T(8,128)(2,1)}, u32[]{:S(2)}) copy-start(bf16[4,256,256]{1,2,0:T(8,128)(2,1)} %copy.74) | copy-start | bytes 1572868
  84.2 33.5 %all-to-all-start.3 = ((bf16[4,32,8,512]{3,2,0,1:T(8,128)(2,1)}), bf16[4,32,8,512]{3,2,0,1:T(8,128)(2,1)}, u32[]{:S(2)}, u32[]{:S(2)}) async-start(bf16[4,32,8,512]{3,2,0,1:T(8,128)(2,1)} %copy.81), calls=%async_computation.3 | async-start | bytes 2097152 | tf_op jit(solution)/shard_map/all_to_all | solution.py:93
  117.7 46.5 %all-to-all-start.1 = ((bf16[32,4,8,512]{3,2,1,0:T(8,128)(2,1)}), bf16[32,4,8,512]{3,2,1,0:T(8,128)(2,1)}, u32[]{:S(2)}, u32[]{:S(2)}) async-start(bf16[32,4,8,512]{3,2,1,0:T(8,128)(2,1)} %copy.77), calls=%async_computation.1 | async-start | bytes 2097152 | tf_op jit(solution)/shard_map/all_to_all | solution.py:77
  127.3 5.8 %copy-start.2 = (f32[4,512,256]{2,1,0:T(8,128)S(1)}, f32[4,512,256]{2,1,0:T(8,128)}, u32[]{:S(2)}) copy-start(f32[4,512,256]{2,1,0:T(8,128)} %fusion.17) | copy-start | bytes 6291460
  150.2 12.1 %copy-start.6 = (bf16[512,256]{1,0:T(8,128)(2,1)S(1)}, bf16[512,256]{1,0:T(8,128)(2,1)}, u32[]{:S(2)}) copy-start(bf16[512,256]{1,0:T(8,128)(2,1)} %param.6) | copy-start | bytes 786436
  195.4 1.2 copy-start.3
  196.6 1.2 copy-start.4
  201.5 5.1 %collective-permute-start = (bf16[2,2,2,65536]{3,2,1,0:T(2,128)(2,1)S(1)}, bf16[2,2,2,65536]{3,2,1,0:T(2,128)(2,1)S(1)}, u32[]{:S(2)}, u32[]{:S(2)}) collective-permute-start(bf16[2,2,2,65536]{3,2,1,0:T(2,128)(2,1)S(1)} %bitcast.132), channel_id=1, source_target_pairs={{0,32},{32,0},{64,96},{96,64},{128,160},{160,128},{192,224},{224,1... | collective-permute-start | bytes 3145736 | tf_op jit(solution)/shard_map/ppermute | solution.py:43
  209.0 15.0 %collective-permute-start.1 = (bf16[2,2,65536]{2,1,0:T(2,128)(2,1)S(1)}, bf16[2,2,65536]{2,1,0:T(2,128)(2,1)S(1)}, u32[]{:S(2)}, u32[]{:S(2)}) collective-permute-start(bf16[2,2,65536]{2,1,0:T(2,128)(2,1)S(1)} %fusion.23), channel_id=1, source_target_pairs={{0,128},{32,160},{64,192},{96,224},{128,0},{160,32},{192,64},{224,... | collective-permute-start | bytes 1572872 | tf_op jit(solution)/shard_map/ppermute | solution.py:43
  214.6 14.9 %copy-start.9 = (bf16[1,1024,256]{2,1,0:T(8,128)(2,1)S(1)}, bf16[1,1024,256]{2,1,0:T(8,128)(2,1)}, u32[]{:S(2)}) copy-start(bf16[1,1024,256]{2,1,0:T(8,128)(2,1)} %param.10) | copy-start | bytes 1572868
  224.8 10.0 %collective-permute-start.2 = (bf16[2,65536]{1,0:T(2,128)(2,1)S(1)}, bf16[2,65536]{1,0:T(2,128)(2,1)S(1)}, u32[]{:S(2)}, u32[]{:S(2)}) collective-permute-start(bf16[2,65536]{1,0:T(2,128)(2,1)S(1)} %fusion.29), channel_id=1, source_target_pairs={{0,256},{32,288},{64,320},{96,352},{128,384},{160,416},{192,448},{... | collective-permute-start | bytes 786440 | tf_op jit(solution)/shard_map/ppermute | solution.py:43
  229.4 18.9 %copy-start.1 = (bf16[4,256,256]{2,1,0:T(8,128)(2,1)S(1)}, bf16[4,256,256]{2,1,0:T(8,128)(2,1)}, u32[]{:S(2)}) copy-start(bf16[4,256,256]{2,1,0:T(8,128)(2,1)} %param.8) | copy-start | bytes 1572868
  235.9 9.7 %collective-permute-start.3 = (bf16[65536]{0:T(1024)(128)(2,1)S(1)}, bf16[65536]{0:T(1024)(128)(2,1)S(1)}, u32[]{:S(2)}, u32[]{:S(2)}) collective-permute-start(bf16[65536]{0:T(1024)(128)(2,1)S(1)} %convert_reduce_fusion), channel_id=1, source_target_pairs={{0,64},{32,96},{64,0},{96,32},{128,192},{160,224},{192,128},{224,1... | collective-permute-start | bytes 393224 | tf_op jit(solution)/shard_map/ppermute | solution.py:43

commit v2 on v1

--- a/solution.py
+++ b/solution.py
@@ -27,23 +27,28 @@
     return list(range(bits))
 
 
-def dp_reduce_scatter(buf, replicas):
+def dp_reduce_scatter(arrays, replicas):
     idx = lax.axis_index("dp")
     order = dp_bit_order(replicas)
     bits = len(order)
-    width = buf.shape[1]
-    buf = buf.reshape((2,) * bits + (width,))
+    views = [a.reshape(a.shape[:1] + (2,) * bits + a.shape[2:]) for a in arrays]
     live = list(range(bits - 1, -1, -1))
     for bit in order:
-        axis = live.index(bit)
+        axis = 1 + live.index(bit)
         me = (idx >> bit) & 1
-        keep = lax.dynamic_index_in_dim(buf, me, axis, keepdims=False)
-        send = lax.dynamic_index_in_dim(buf, 1 - me, axis, keepdims=False)
+        keeps = [lax.dynamic_index_in_dim(v, me, axis, keepdims=False) for v in views]
+        sends = [lax.dynamic_index_in_dim(v, 1 - me, axis, keepdims=False) for v in views]
+        packed = jnp.concatenate([s.astype(jnp.bfloat16).reshape(-1) for s in sends])
         perm = [(i, i ^ (1 << bit)) for i in range(replicas)]
-        got = lax.ppermute(send.astype(jnp.bfloat16), "dp", perm)
-        buf = keep + got.astype(jnp.float32)
-        live.pop(axis)
-    return buf.reshape(width)
+        got = lax.ppermute(packed, "dp", perm)
+        views = []
+        offset = 0
+        for k in keeps:
+            n = k.size
+            views.append(k + got[offset : offset + n].reshape(k.shape).astype(jnp.float32))
+            offset += n
+        live.pop(axis - 1)
+    return views
 
 
 def shards(tokens, first_right, first_left, second_right, second_left, cotangent):
@@ -95,23 +100,20 @@
         "jkgt,kbjg->tkb", d_up_inner, right_one, preferred_element_type=fp
     ).astype(bf)
     grad_tokens = grad_tokens.reshape(tok_rows, in_blocks * block_width)
+    d_up_flat = d_up_inner.reshape(all_hid * in_blocks * sub_width, tok_rows)
     grads = (
-        jnp.einsum("tkb,jkgt->bkjg", tok_parts, d_up_inner, preferred_element_type=fp),
-        jnp.einsum("jbt,jct->bjc", mixed_piece, d_pre, preferred_element_type=fp),
-        jnp.einsum("jbt,kjgt->bjkg", hidden, d_down_inner, preferred_element_type=fp),
-        jnp.einsum("kwt,tkc->wkc", mixed_down, cot_parts, preferred_element_type=fp),
+        jnp.einsum("tb,nt->bn", tok_parts[:, 0, :], d_up_flat, preferred_element_type=fp).reshape(
+            in_blocks, block_width, wide_width
+        ),
+        jnp.einsum("jbt,jct->jbc", mixed_piece, d_pre, preferred_element_type=fp),
+        jnp.einsum("jbt,kjgt->jbkg", hidden, d_down_inner, preferred_element_type=fp).reshape(
+            hid_blocks, block_width, block_width
+        ),
+        jnp.einsum("kwt,tkc->kwc", mixed_down, cot_parts, preferred_element_type=fp),
     )
-    pieces = [g.reshape(replicas, -1) for g in grads]
-    widths = [p.shape[1] for p in pieces]
-    total = dp_reduce_scatter(jnp.concatenate(pieces, axis=1), replicas) * grad_scale
-    outs = []
-    offset = 0
-    for g, w in zip(grads, widths):
-        part = total[offset : offset + w]
-        offset += w
-        lead = g.shape[0] // replicas
-        outs.append(jnp.transpose(part.reshape(lead, g.shape[1], -1), (1, 0, 2)))
-    grad_right_one, grad_left_one, grad_right_two, grad_left_two = outs
+    views = [g.reshape(g.shape[0], replicas, g.shape[1] // replicas, g.shape[2]) for g in grads]
+    reduced = dp_reduce_scatter(views, replicas)
+    grad_right_one, grad_left_one, grad_right_two, grad_left_two = [r * grad_scale for r in reduced]
     return (layer_out, grad_tokens, grad_right_one, grad_left_one, grad_right_two, grad_left_two)
 
 

time: 253 us -> 245 us (0.968)
  local copies, waits for them, and re-layouts: 81.7 us -> 70.4 us
  other arithmetic: 2.92 us -> 11 us
  matrix products: 24.5 us -> 20 us
    concatenate x5 -> x0, local copies, waits for them, and re-layouts: 30.4 us -> none  [shards(): jnp.concatenate(pieces, axis=1)]
    transpose x3 -> x0, local copies, waits for them, and re-layouts: 30.4 us -> none  [the longest x1 14.2 us: shards(): jnp.einsum('jbt,kjgt->bjkg', hidden, d_down_inner, preferred_element_type...]
    dynamic_slice x2 -> x3, local copies, waits for them, and re-layouts: 2.39 us -> 27.5 us  [the longest x2 18.4 us: dp_reduce_scatter(): lax.dynamic_index_in_dim(v, me, axis, keepdims=False)]
    all_to_all x1, waiting for transfers between devices: 21.8 us -> 0.01 us  [shards(): lax.all_to_all(d_mixed_up, 'tensor', split_axis=1, concat_axis=0, tiled=T...]
    all_to_all x1, waiting for transfers between devices: 0.01 us -> 21.1 us  [shards(): lax.all_to_all(down_inner, 'tensor', split_axis=0, concat_axis=1, tiled=T...]
    another operation x0 -> x1, local copies, waits for them, and re-layouts: none -> 13.8 us  [dp_reduce_scatter(): views = [a.reshape(a.shape[:1] + (2,) * bits + a.shape[2:]) for a in arrays]]
    unnamed x30 -> x67, local copies, waits for them, and re-layouts: 9.68 us -> 17.4 us
    convert_element_type x4 -> x28, local copies, waits for them, and re-layouts: 3.21 us -> 7.48 us  [the longest x16 7.19 us: dp_reduce_scatter(): got[offset:offset + n].reshape(k.shape).astype(jnp.float32)]
  transfers between devices with their start and end apart: 8 -> 8, of which waited for: 7 -> 6; matrix products, arithmetic and copies ran while one was open for 22% -> 30% of each run, Pallas kernels for 0% -> 0%
where the time goes in v2:
time: 245 us; the launch traced here: 240 us
  waiting for transfers between devices  83.9 us (34%)
  local copies, waits for them, and re-layouts  70.4 us (29%)
  starting transfers between devices  53.4 us (22%)
  matrix products  20 us (8%)
  other arithmetic  11 us (4%)
    all_to_all x1, waiting for transfers between devices, shards(): lax.all_to_all(up_inner, 'tensor', split_axis=0, concat_axis=1, tiled=True)  24.4 us
    all_to_all x1, waiting for transfers between devices, shards(): lax.all_to_all(down_inner, 'tensor', split_axis=0, concat_axis=1, tiled=T...  21.1 us
    all_to_all x1, waiting for transfers between devices, shards(): lax.all_to_all(d_mixed_down, 'tensor', split_axis=1, concat_axis=0, tiled...  20.5 us
    dynamic_slice x2, local copies, waits for them, and re-layouts, dp_reduce_scatter(): lax.dynamic_index_in_dim(v, me, axis, keepdims=False)  18.4 us
    ppermute x4, waiting for transfers between devices, dp_reduce_scatter(): got = lax.ppermute(packed, 'dp', perm)  18 us
    unnamed x67, local copies, waits for them, and re-layouts  17.4 us
    ppermute x4, starting transfers between devices, dp_reduce_scatter(): got = lax.ppermute(packed, 'dp', perm)  15.7 us
    all_to_all x1, starting transfers between devices, shards(): lax.all_to_all(up_inner, 'tensor', split_axis=0, concat_axis=1, tiled=True)  14.3 us
  transfers between devices with their start and end apart: 8, of which 6 were waited for; matrix products, arithmetic and copies ran while one was open for 30% of the time, Pallas kernels for 0%

profile of v2, /device:TPU:1, one launch (start us, length us, event | category | flops | bytes accessed | tf_op | source)
XLA Modules:
  0.0 240.2 jit_solution(9235066460710457274)
XLA Ops:
  0.6 1.3 copy.99
  2.0 1.6 fusion.10
  3.6 1.6 copy.101
  5.2 14.3 %all-to-all-start = ((bf16[128,1,8,512]{3,2,1,0:T(8,128)(2,1)}), bf16[128,1,8,512]{3,2,1,0:T(8,128)(2,1)S(1)}, u32[]{:S(2)}, u32[]{:S(2)}) async-start(bf16[128,1,8,512]{3,2,1,0:T(8,128)(2,1)} %copy.101), calls=%async_computation | async-start | bytes 2097152 | tf_op jit(solution)/shard_map/all_to_all | solution.py:75
  19.5 1.5 fusion.11
  20.9 24.4 %all-to-all-done = bf16[128,1,8,512]{3,2,1,0:T(8,128)(2,1)S(1)} async-done(((bf16[128,1,8,512]{3,2,1,0:T(8,128)(2,1)}), bf16[128,1,8,512]{3,2,1,0:T(8,128)(2,1)S(1)}, u32[]{:S(2)}, u32[]{:S(2)}) %all-to-all-start) | async-done | bytes 1048608 | tf_op jit(solution)/shard_map/all_to_all | solution.py:75
  45.3 7.6 %all-to-all-start.2 = ((bf16[1,128,8,512]{3,2,0,1:T(8,128)(2,1)}), bf16[1,128,8,512]{3,2,0,1:T(8,128)(2,1)S(1)}, u32[]{:S(2)}, u32[]{:S(2)}) async-start(bf16[1,128,8,512]{3,2,0,1:T(8,128)(2,1)} %fusion.11), calls=%async_computation.2 | async-start | bytes 2097152 | tf_op jit(solution)/shard_map/all_to_all | solution.py:93
  52.9 1.0 copy.104
  53.9 0.5 fusion.20
  54.4 1.4 copy-done.4
  55.8 0.7 fusion.12
  56.5 1.6 copy.107
  58.1 20.5 %all-to-all-done.2 = bf16[1,128,8,512]{3,2,0,1:T(8,128)(2,1)S(1)} async-done(((bf16[1,128,8,512]{3,2,0,1:T(8,128)(2,1)}), bf16[1,128,8,512]{3,2,0,1:T(8,128)(2,1)S(1)}, u32[]{:S(2)}, u32[]{:S(2)}) %all-to-all-start.2) | async-done | bytes 1048608 | tf_op jit(solution)/shard_map/all_to_all | solution.py:93
  78.6 7.9 %all-to-all-start.1 = ((bf16[32,4,8,512]{3,2,1,0:T(8,128)(2,1)}), bf16[32,4,8,512]{3,2,1,0:T(8,128)(2,1)}, u32[]{:S(2)}, u32[]{:S(2)}) async-start(bf16[32,4,8,512]{3,2,1,0:T(8,128)(2,1)} %copy.107), calls=%async_computation.1 | async-start | bytes 2097152 | tf_op jit(solution)/shard_map/all_to_all | solution.py:82
  86.5 3.0 %fusion.5 = bf16[4,256,512]{1,2,0:T(8,128)(2,1)S(1)} fusion(f32[4,512,256]{2,1,0:T(8,128)} %copy-done.4, bf16[32,4,8,512]{3,2,1,0:T(8,128)(2,1)} %bitcast.197, bf16[4,256,256]{1,2,0:T(8,128)(2,1)S(1)} %copy-done.22), kind=kOutput, calls=%fused_computation.6 | convolution fusion | flops 273678336 | bytes 4718592 | tf_op jit(solution)/shard_map/kjgt,jbkg->jbt/dot_general | solution.py:94
  89.5 0.5 fusion.13
  90.0 1.1 copy.111
  91.1 21.1 %all-to-all-done.1 = bf16[32,4,8,512]{3,2,1,0:T(8,128)(2,1)} async-done(((bf16[32,4,8,512]{3,2,1,0:T(8,128)(2,1)}), bf16[32,4,8,512]{3,2,1,0:T(8,128)(2,1)}, u32[]{:S(2)}, u32[]{:S(2)}) %all-to-all-start.1) | async-done | bytes 1048608 | tf_op jit(solution)/shard_map/all_to_all | solution.py:82
  112.2 8.0 %all-to-all-start.3 = ((bf16[4,32,8,512]{3,2,0,1:T(8,128)(2,1)}), bf16[4,32,8,512]{3,2,0,1:T(8,128)(2,1)}, u32[]{:S(2)}, u32[]{:S(2)}) async-start(bf16[4,32,8,512]{3,2,0,1:T(8,128)(2,1)} %copy.111), calls=%async_computation.3 | async-start | bytes 2097152 | tf_op jit(solution)/shard_map/all_to_all | solution.py:98
  120.2 3.5 %fusion.16 = f32[4,256,32,8]{1,3,2,0:T(8,128)} fusion(bf16[32,4,8,512]{3,2,1,0:T(8,128)(2,1)} %bitcast.198, f32[4,512,256]{2,1,0:T(8,128)} %copy-done.4), kind=kOutput, calls=%fused_computation.26 | convolution fusion | flops 271056896 | bytes 4194304 | tf_op jit(solution)/shard_map/jbt,kjgt->jbkg/dot_general | solution.py:109
  123.7 13.8 %reshape_reshape_reshape.7 = f32[4,2,2,2,2,16,256]{5,4,3,2,1,6,0:T(2,128)} reshape(f32[4,256,32,8]{1,3,2,0:T(8,128)} %fusion.16) | data formatting | bytes 2097152 | tf_op jit(solution)/shard_map/reshape;reshape;reshape | solution.py:34
  137.5 9.2 %constant_dynamic-slice_fusion.1 = bf16[4,2,2,2,1,16,256]{5,4,3,2,1,6,0:T(2,128)(2,1)} fusion(f32[4,2,2,2,2,16,256]{5,4,3,2,1,6,0:T(2,128)} %reshape_reshape_reshape.7, s32[]{:T(128)S(6)} %select_n.61), kind=kLoop, calls=%fused_computation.101 | loop fusion | bytes 524292 | tf_op jit(solution)/shard_map/jit(dynamic_index_in_dim)/dynamic_slice | solution.py:40
  146.6 8.6 %copy.131 = bf16[4,2,2,2,1,16,256]{6,5,4,3,2,1,0:T(8,128)(2,1)S(1)} copy(bf16[4,2,2,2,1,16,256]{5,4,3,2,1,6,0:T(2,128)(2,1)} %constant_dynamic-slice_fusion.1) | data formatting | bytes 524288
  155.2 0.2 copy.134
  155.4 0.4 fusion.18
  155.9 1.0 copy-done.1
  156.9 0.2 copy.133
  157.1 1.7 fusion.29
  158.8 1.0 copy-done.3
  159.8 0.2 copy.135
  160.0 1.7 fusion.43
  161.9 3.0 %collective-permute-start = (bf16[524288]{0:T(1024)(128)(2,1)S(1)}, bf16[524288]{0:T(1024)(128)(2,1)}, u32[]{:S(2)}, u32[]{:S(2)}) collective-permute-start(bf16[524288]{0:T(1024)(128)(2,1)S(1)} %pad_maximum_fusion), channel_id=1, source_target_pairs={{0,32},{32,0},{64,96},{96,64},{128,160},{160,128},{192,224},{224,1... | collective-permute-start | bytes 3145736 | tf_op jit(solution)/shard_map/ppermute | solution.py:43
  164.9 9.7 %constant_dynamic-slice_fusion = f32[4,2,2,2,1,16,256]{5,4,3,2,1,6,0:T(1,128)} fusion(f32[4,2,2,2,2,16,256]{5,4,3,2,1,6,0:T(2,128)} %reshape_reshape_reshape.7, s32[]{:T(128)S(6)} %select_n.60), kind=kLoop, calls=%fused_computation.100 | loop fusion | bytes 1048580 | tf_op jit(solution)/shard_map/jit(dynamic_index_in_dim)/dynamic_slice | solution.py:39
  174.6 8.7 %copy.117 = f32[4,2,2,2,1,16,256]{6,5,3,2,1,0,4:T(8,128)S(1)} copy(f32[4,2,2,2,1,16,256]{5,4,3,2,1,6,0:T(1,128)} %constant_dynamic-slice_fusion) | data formatting | bytes 1048576 | tf_op jit(solution)/shard_map/jit(dynamic_index_in_dim)/dynamic_slice | solution.py:39
  183.3 2.4 slice_convert_fusion.3
  185.7 1.0 reshape.410
  186.6 1.4 bitcast_add_fusion
  188.0 0.8 copy-done.12
  188.8 0.1 copy.139
  188.9 2.0 reshape.409
  190.9 2.0 reshape.408
  192.9 1.1 bitcast_add_fusion.2
  194.0 1.3 bitcast_add_fusion.1
  195.4 0.1 copy.138
  195.5 0.1 copy.137
  195.7 0.5 copy-done.8
  196.2 0.1 reshape.407
  196.5 3.2 %collective-permute-start.1 = (bf16[262144]{0:T(1024)(128)(2,1)S(1)}, bf16[262144]{0:T(1024)(128)(2,1)S(1)}, u32[]{:S(2)}, u32[]{:S(2)}) collective-permute-start(bf16[262144]{0:T(1024)(128)(2,1)S(1)} %pad_maximum_fusion.1), channel_id=1, source_target_pairs={{0,128},{32,160},{64,192},{96,224},{128,0},{160,32},{192,64},{224,... | collective-permute-start | bytes 1572872 | tf_op jit(solution)/shard_map/ppermute | solution.py:43
  199.7 12.2 %collective-permute-done.1 = bf16[262144]{0:T(1024)(128)(2,1)S(1)} collective-permute-done((bf16[262144]{0:T(1024)(128)(2,1)S(1)}, bf16[262144]{0:T(1024)(128)(2,1)S(1)}, u32[]{:S(2)}, u32[]{:S(2)}) %collective-permute-start.1) | collective-permute-done | bytes 524320 | tf_op jit(solution)/shard_map/ppermute | solution.py:43
  212.0 0.8 slice_convert_fusion.7
  212.7 1.8 reshape.414
  214.5 1.0 bitcast_add_fusion.4
  215.6 0.6 copy-done.17
  216.4 0.1 reshape.412
  216.8 4.6 %collective-permute-start.2 = (bf16[131072]{0:T(1024)(128)(2,1)S(1)}, bf16[131072]{0:T(1024)(128)(2,1)S(1)}, u32[]{:S(2)}, u32[]{:S(2)}) collective-permute-start(bf16[131072]{0:T(1024)(128)(2,1)S(1)} %pad_maximum_fusion.2), channel_id=1, source_target_pairs={{0,256},{32,288},{64,320},{96,352},{128,384},{160,416},{192,448},{... | collective-permute-start | bytes 786440 | tf_op jit(solution)/shard_map/ppermute | solution.py:43
  221.5 2.5 %fusion.14 = bf16[512,256]{1,0:T(8,128)(2,1)} fusion(bf16[128,8,512]{2,1,0:T(8,128)(2,1)} %bitcast.21, bf16[1,256,1024]{1,2,0:T(8,128)(2,1)S(1)} %copy-done.6), kind=kOutput, calls=%fused_computation.22 | convolution fusion | flops 268566528 | bytes 1835008 | tf_op jit(solution)/shard_map/jkgt,kbjg->tkb/dot_general | solution.py:99
  224.0 3.2 %collective-permute-done.2 = bf16[131072]{0:T(1024)(128)(2,1)S(1)} collective-permute-done((bf16[131072]{0:T(1024)(128)(2,1)S(1)}, bf16[131072]{0:T(1024)(128)(2,1)S(1)}, u32[]{:S(2)}, u32[]{:S(2)}) %collective-permute-start.2) | collective-permute-done | bytes 262176 | tf_op jit(solution)/shard_map/ppermute | solution.py:43
  227.8 4.8 %collective-permute-start.3 = (bf16[65536]{0:T(1024)(128)(2,1)S(1)}, bf16[65536]{0:T(1024)(128)(2,1)S(1)}, u32[]{:S(2)}, u32[]{:S(2)}) collective-permute-start(bf16[65536]{0:T(1024)(128)(2,1)S(1)} %pad_maximum_fusion.3), channel_id=1, source_target_pairs={{0,64},{32,96},{64,0},{96,32},{128,192},{160,224},{192,128},{224,1... | collective-permute-start | bytes 393224 | tf_op jit(solution)/shard_map/ppermute | solution.py:43
  232.6 2.4 %convolution_convert_fusion.4 = bf16[512,256]{1,0:T(8,128)(2,1)} fusion(bf16[1024,512]{1,0:T(8,128)(2,1)} %bitcast.10, bf16[1,1024,256]{2,1,0:T(8,128)(2,1)S(1)} %copy-done.20), kind=kOutput, calls=%fused_computation.23 | convolution fusion | flops 268566528 | bytes 1835008 | tf_op jit(solution)/shard_map/kwt,kwc->tkc/dot_general | solution.py:84
  235.0 2.5 %collective-permute-done.3 = bf16[65536]{0:T(1024)(128)(2,1)S(1)} collective-permute-done((bf16[65536]{0:T(1024)(128)(2,1)S(1)}, bf16[65536]{0:T(1024)(128)(2,1)S(1)}, u32[]{:S(2)}, u32[]{:S(2)}) %collective-permute-start.3) | collective-permute-done | bytes 131104 | tf_op jit(solution)/shard_map/ppermute | solution.py:43
  237.6 0.6 fusion.37
  238.2 0.6 fusion.35
  238.9 0.6 fusion.34
  239.6 0.6 fusion.33
  (90 shorter events, 1.5 us)
Async XLA Ops:
  0.6 53.3 %copy-start = (bf16[4,256,256]{2,1,0:T(8,128)(2,1)S(1)}, bf16[4,256,256]{2,1,0:T(8,128)(2,1)}, u32[]{:S(2)}) copy-start(bf16[4,256,256]{2,1,0:T(8,128)(2,1)} %param.8) | copy-start | bytes 1572868
  2.0 3.2 %copy-start.5 = (bf16[1,256,1024]{1,2,0:T(8,128)(2,1)}, bf16[1,256,1024]{1,2,0:T(8,128)(2,1)S(1)}, u32[]{:S(2)}) copy-start(bf16[1,256,1024]{1,2,0:T(8,128)(2,1)S(1)} %copy.99) | copy-start | bytes 1572868
  3.6 15.9 %copy-start.14 = (bf16[512,256]{1,0:T(8,128)(2,1)S(1)}, bf16[512,256]{1,0:T(8,128)(2,1)}, u32[]{:S(2)}) copy-start(bf16[512,256]{1,0:T(8,128)(2,1)} %param.11) | copy-start | bytes 786436
  3.6 15.9 %copy-start.19 = (bf16[1,1024,256]{2,1,0:T(8,128)(2,1)S(1)}, bf16[1,1024,256]{2,1,0:T(8,128)(2,1)}, u32[]{:S(2)}) copy-start(bf16[1,1024,256]{2,1,0:T(8,128)(2,1)} %param.10) | copy-start | bytes 1572868
  5.2 40.1 %all-to-all-start = ((bf16[128,1,8,512]{3,2,1,0:T(8,128)(2,1)}), bf16[128,1,8,512]{3,2,1,0:T(8,128)(2,1)S(1)}, u32[]{:S(2)}, u32[]{:S(2)}) async-start(bf16[128,1,8,512]{3,2,1,0:T(8,128)(2,1)} %copy.101), calls=%async_computation | async-start | bytes 2097152 | tf_op jit(solution)/shard_map/all_to_all | solution.py:75
  19.5 33.4 %copy-start.21 = (bf16[4,256,256]{2,1,0:T(8,128)(2,1)S(1)}, bf16[4,256,256]{2,1,0:T(8,128)(2,1)}, u32[]{:S(2)}) copy-start(bf16[4,256,256]{2,1,0:T(8,128)(2,1)} %param.9) | copy-start | bytes 1572868
  45.3 33.3 %all-to-all-start.2 = ((bf16[1,128,8,512]{3,2,0,1:T(8,128)(2,1)}), bf16[1,128,8,512]{3,2,0,1:T(8,128)(2,1)S(1)}, u32[]{:S(2)}, u32[]{:S(2)}) async-start(bf16[1,128,8,512]{3,2,0,1:T(8,128)(2,1)} %fusion.11), calls=%async_computation.2 | async-start | bytes 2097152 | tf_op jit(solution)/shard_map/all_to_all | solution.py:93
  53.9 1.9 copy-start.22
  54.4 1.4 copy-start.4
  78.6 7.9 %copy-start.16 = (bf16[1,128,8,512]{3,2,0,1:T(8,128)(2,1)}, bf16[1,128,8,512]{3,2,0,1:T(8,128)(2,1)S(1)}, u32[]{:S(2)}) copy-start(bf16[1,128,8,512]{3,2,0,1:T(8,128)(2,1)S(1)} %all-to-all-done.2) | copy-start | bytes 3145732
  78.6 33.6 %all-to-all-start.1 = ((bf16[32,4,8,512]{3,2,1,0:T(8,128)(2,1)}), bf16[32,4,8,512]{3,2,1,0:T(8,128)(2,1)}, u32[]{:S(2)}, u32[]{:S(2)}) async-start(bf16[32,4,8,512]{3,2,1,0:T(8,128)(2,1)} %copy.107), calls=%async_computation.1 | async-start | bytes 2097152 | tf_op jit(solution)/shard_map/all_to_all | solution.py:82
  112.2 47.8 %all-to-all-start.3 = ((bf16[4,32,8,512]{3,2,0,1:T(8,128)(2,1)}), bf16[4,32,8,512]{3,2,0,1:T(8,128)(2,1)}, u32[]{:S(2)}, u32[]{:S(2)}) async-start(bf16[4,32,8,512]{3,2,0,1:T(8,128)(2,1)} %copy.111), calls=%async_computation.3 | async-start | bytes 2097152 | tf_op jit(solution)/shard_map/all_to_all | solution.py:98
  155.9 1.0 copy-start.1
  156.9 3.1 %copy-start.15 = (bf16[512,256]{1,0:T(8,128)(2,1)S(1)}, bf16[512,256]{1,0:T(8,128)(2,1)}, u32[]{:S(2)}) copy-start(bf16[512,256]{1,0:T(8,128)(2,1)} %param.6) | copy-start | bytes 786436
  158.8 1.0 copy-start.3
  161.9 21.4 %collective-permute-start = (bf16[524288]{0:T(1024)(128)(2,1)S(1)}, bf16[524288]{0:T(1024)(128)(2,1)}, u32[]{:S(2)}, u32[]{:S(2)}) collective-permute-start(bf16[524288]{0:T(1024)(128)(2,1)S(1)} %pad_maximum_fusion), channel_id=1, source_target_pairs={{0,32},{32,0},{64,96},{96,64},{128,160},{160,128},{192,224},{224,1... | collective-permute-start | bytes 3145736 | tf_op jit(solution)/shard_map/ppermute | solution.py:43
  186.6 6.3 %copy-start.2 = (f32[4,256,256]{2,1,0:T(8,128)S(1)}, f32[4,256,256]{2,1,0:T(8,128)}, u32[]{:S(2)}) copy-start(f32[4,256,256]{2,1,0:T(8,128)} %copy-done.1) | copy-start | bytes 3145732
  188.0 0.8 copy-start.12
  194.0 1.6 copy-start.10
  194.0 2.1 copy-start.7
  195.4 0.8 copy-start.8
  196.3 18.2 %copy-start.13 = (f32[2,2,2,64,256]{4,3,2,1,0:T(8,128)S(1)}, f32[2,2,2,64,256]{4,3,2,1,0:T(8,128)}, u32[]{:S(2)}) copy-start(f32[2,2,2,64,256]{4,3,2,1,0:T(8,128)} %copy-done.12) | copy-start | bytes 1572868
  196.4 19.8 %copy-start.9 = (f32[4,2,2,2,16,256]{5,4,3,2,1,0:T(8,128)S(1)}, f32[4,2,2,2,16,256]{5,4,3,2,1,0:T(8,128)}, u32[]{:S(2)}) copy-start(f32[4,2,2,2,16,256]{5,4,3,2,1,0:T(8,128)} %copy-done.8) | copy-start | bytes 1572868
  196.5 15.5 %collective-permute-start.1 = (bf16[262144]{0:T(1024)(128)(2,1)S(1)}, bf16[262144]{0:T(1024)(128)(2,1)S(1)}, u32[]{:S(2)}, u32[]{:S(2)}) collective-permute-start(bf16[262144]{0:T(1024)(128)(2,1)S(1)} %pad_maximum_fusion.1), channel_id=1, source_target_pairs={{0,128},{32,160},{64,192},{96,224},{128,0},{160,32},{192,64},{224,... | collective-permute-start | bytes 1572872 | tf_op jit(solution)/shard_map/ppermute | solution.py:43
  212.7 3.8 %copy-start.11 = (f32[4,2,2,2,16,256]{5,4,3,2,1,0:T(8,128)S(1)}, f32[4,2,2,2,16,256]{5,4,3,2,1,0:T(8,128)}, u32[]{:S(2)}) copy-start(f32[4,2,2,2,16,256]{5,4,3,2,1,0:T(8,128)} %copy-done.10) | copy-start | bytes 1572868
  215.5 0.7 copy-start.17
  216.3 5.1 %copy-start.6 = (bf16[1,256,1024]{1,2,0:T(8,128)(2,1)S(1)}, bf16[1,256,1024]{1,2,0:T(8,128)(2,1)}, u32[]{:S(2)}) copy-start(bf16[1,256,1024]{1,2,0:T(8,128)(2,1)} %copy-done.5) | copy-start | bytes 1572868
  216.8 10.4 %collective-permute-start.2 = (bf16[131072]{0:T(1024)(128)(2,1)S(1)}, bf16[131072]{0:T(1024)(128)(2,1)S(1)}, u32[]{:S(2)}, u32[]{:S(2)}) collective-permute-start(bf16[131072]{0:T(1024)(128)(2,1)S(1)} %pad_maximum_fusion.2), channel_id=1, source_target_pairs={{0,256},{32,288},{64,320},{96,352},{128,384},{160,416},{192,448},{... | collective-permute-start | bytes 786440 | tf_op jit(solution)/shard_map/ppermute | solution.py:43
  221.5 5.8 %copy-start.18 = (f32[2,2,64,256]{3,2,1,0:T(8,128)S(1)}, f32[2,2,64,256]{3,2,1,0:T(8,128)}, u32[]{:S(2)}) copy-start(f32[2,2,64,256]{3,2,1,0:T(8,128)} %copy-done.17) | copy-start | bytes 786436
  224.0 8.5 %copy-start.20 = (bf16[1,1024,256]{2,1,0:T(8,128)(2,1)S(1)}, bf16[1,1024,256]{2,1,0:T(8,128)(2,1)}, u32[]{:S(2)}) copy-start(bf16[1,1024,256]{2,1,0:T(8,128)(2,1)} %param.10) | copy-start | bytes 1572868
  227.8 9.7 %collective-permute-start.3 = (bf16[65536]{0:T(1024)(128)(2,1)S(1)}, bf16[65536]{0:T(1024)(128)(2,1)S(1)}, u32[]{:S(2)}, u32[]{:S(2)}) collective-permute-start(bf16[65536]{0:T(1024)(128)(2,1)S(1)} %pad_maximum_fusion.3), channel_id=1, source_target_pairs={{0,64},{32,96},{64,0},{96,32},{128,192},{160,224},{192,128},{224,1... | collective-permute-start | bytes 393224 | tf_op jit(solution)/shard_map/ppermute | solution.py:43

commit v3 on v2

--- a/solution.py
+++ b/solution.py
@@ -27,28 +27,40 @@
     return list(range(bits))
 
 
-def dp_reduce_scatter(arrays, replicas):
+def chunk_order(x, axis, replicas):
+    order = dp_bit_order(replicas)
+    bits = len(order)
+    shape = x.shape
+    view = x.reshape(shape[:axis] + (2,) * bits + (shape[axis] // replicas,) + shape[axis + 1 :])
+    moved = [axis + bits - 1 - b for b in order]
+    perm = list(range(axis)) + moved + list(range(axis + bits, view.ndim))
+    return jnp.transpose(view, perm).reshape(shape)
+
+
+def dp_reduce_scatter(wide, narrow, replicas):
     idx = lax.axis_index("dp")
     order = dp_bit_order(replicas)
-    bits = len(order)
-    views = [a.reshape(a.shape[:1] + (2,) * bits + a.shape[2:]) for a in arrays]
-    live = list(range(bits - 1, -1, -1))
+    arrays = [wide] + list(narrow)
+    size = replicas
     for bit in order:
-        axis = 1 + live.index(bit)
+        half = size // 2
         me = (idx >> bit) & 1
-        keeps = [lax.dynamic_index_in_dim(v, me, axis, keepdims=False) for v in views]
-        sends = [lax.dynamic_index_in_dim(v, 1 - me, axis, keepdims=False) for v in views]
-        packed = jnp.concatenate([s.astype(jnp.bfloat16).reshape(-1) for s in sends])
+        keeps = [lax.dynamic_slice_in_dim(a, me * half, half, axis=1) for a in arrays]
+        sends = [lax.dynamic_slice_in_dim(a, (1 - me) * half, half, axis=1) for a in arrays]
+        sends = [s.astype(jnp.bfloat16) for s in sends]
+        first = sends[0].reshape(-1, sends[0].shape[-1])
+        rest = jnp.concatenate([s.reshape(-1, s.shape[-1]) for s in sends[1:]], axis=0)
         perm = [(i, i ^ (1 << bit)) for i in range(replicas)]
-        got = lax.ppermute(packed, "dp", perm)
-        views = []
+        got_first, got_rest = lax.ppermute((first, rest), "dp", perm)
+        arrays = [keeps[0] + got_first.reshape(keeps[0].shape).astype(jnp.float32)]
         offset = 0
-        for k in keeps:
-            n = k.size
-            views.append(k + got[offset : offset + n].reshape(k.shape).astype(jnp.float32))
-            offset += n
-        live.pop(axis - 1)
-    return views
+        for k in keeps[1:]:
+            rows = k.size // k.shape[-1]
+            part = got_rest[offset : offset + rows].reshape(k.shape)
+            arrays.append(k + part.astype(jnp.float32))
+            offset += rows
+        size = half
+    return [a.reshape(a.shape[:1] + a.shape[2:]) for a in arrays]
 
 
 def shards(tokens, first_right, first_left, second_right, second_left, cotangent):
@@ -101,18 +113,23 @@
     ).astype(bf)
     grad_tokens = grad_tokens.reshape(tok_rows, in_blocks * block_width)
     d_up_flat = d_up_inner.reshape(all_hid * in_blocks * sub_width, tok_rows)
-    grads = (
-        jnp.einsum("tb,nt->bn", tok_parts[:, 0, :], d_up_flat, preferred_element_type=fp).reshape(
-            in_blocks, block_width, wide_width
-        ),
-        jnp.einsum("jbt,jct->jbc", mixed_piece, d_pre, preferred_element_type=fp),
-        jnp.einsum("jbt,kjgt->jbkg", hidden, d_down_inner, preferred_element_type=fp).reshape(
-            hid_blocks, block_width, block_width
-        ),
-        jnp.einsum("kwt,tkc->kwc", mixed_down, cot_parts, preferred_element_type=fp),
+    tok_sorted = chunk_order(tok_parts[:, 0, :], 1, replicas)
+    mixed_sorted = chunk_order(mixed_piece, 1, replicas)
+    hidden_sorted = chunk_order(hidden, 1, replicas)
+    down_sorted = chunk_order(mixed_down, 1, replicas)
+    g_right_one = jnp.einsum("tb,nt->bn", tok_sorted, d_up_flat, preferred_element_type=fp)
+    g_left_one = jnp.einsum("jbt,jct->jbc", mixed_sorted, d_pre, preferred_element_type=fp)
+    g_right_two = jnp.einsum(
+        "jbt,kjgt->jbkg", hidden_sorted, d_down_inner, preferred_element_type=fp
+    ).reshape(hid_blocks, block_width, block_width)
+    g_left_two = jnp.einsum("kwt,tkc->kwc", down_sorted, cot_parts, preferred_element_type=fp)
+
+    def view(g):
+        return g.reshape(in_blocks if g.ndim == 2 else g.shape[0], replicas, -1, g.shape[-1])
+
+    reduced = dp_reduce_scatter(
+        view(g_right_one), [view(g_left_one), view(g_right_two), view(g_left_two)], replicas
     )
-    views = [g.reshape(g.shape[0], replicas, g.shape[1] // replicas, g.shape[2]) for g in grads]
-    reduced = dp_reduce_scatter(views, replicas)
     grad_right_one, grad_left_one, grad_right_two, grad_left_two = [r * grad_scale for r in reduced]
     return (layer_out, grad_tokens, grad_right_one, grad_left_one, grad_right_two, grad_left_two)
 

time: 245 us -> 201 us (0.82)
  the two profiles are of different devices: /device:TPU:1 before, /device:TPU:24 now
where the time goes in v3:
time: 201 us; the launch traced here: 200 us
  waiting for transfers between devices  78.7 us (39%)
  starting transfers between devices  65.4 us (33%)
  local copies, waits for them, and re-layouts  35.5 us (18%)
  matrix products  15.8 us (8%)
  other arithmetic  3.13 us (2%)
    ppermute x8, starting transfers between devices, dp_reduce_scatter(): got_first, got_rest = lax.ppermute((first, rest), 'dp', perm)  29.6 us
    all_to_all x1, waiting for transfers between devices, shards(): lax.all_to_all(up_inner, 'tensor', split_axis=0, concat_axis=1, tiled=True)  24.6 us
    all_to_all x1, waiting for transfers between devices, shards(): lax.all_to_all(d_mixed_up, 'tensor', split_axis=1, concat_axis=0, tiled=T...  22.7 us
    all_to_all x1, waiting for transfers between devices, shards(): lax.all_to_all(d_mixed_down, 'tensor', split_axis=1, concat_axis=0, tiled...  21.8 us
    all_to_all x1, starting transfers between devices, shards(): lax.all_to_all(up_inner, 'tensor', split_axis=0, concat_axis=1, tiled=True)  13.8 us
    unnamed x39, local copies, waits for them, and re-layouts  13 us
    ppermute x8, waiting for transfers between devices, dp_reduce_scatter(): got_first, got_rest = lax.ppermute((first, rest), 'dp', perm)  9.59 us
    all_to_all x1, starting transfers between devices, shards(): lax.all_to_all(d_mixed_up, 'tensor', split_axis=1, concat_axis=0, tiled=T...  7.42 us
  transfers between devices with their start and end apart: 12, of which 5 were waited for; matrix products, arithmetic and copies ran while one was open for 21% of the time, Pallas kernels for 0%

profile of v3, /device:TPU:24, one launch (start us, length us, event | category | flops | bytes accessed | tf_op | source)
XLA Modules:
  0.0 199.8 jit_solution(4172672627379516322)
XLA Ops:
  0.6 0.0 copy-start
  0.6 1.3 copy.135
  2.0 1.4 fusion.10
  3.4 0.0 copy-start.10
  3.4 0.0 copy-start.15
  3.4 1.5 copy.137
  5.0 13.8 %all-to-all-start = ((bf16[128,1,8,512]{3,2,1,0:T(8,128)(2,1)}), bf16[128,1,8,512]{3,2,1,0:T(8,128)(2,1)S(1)}, u32[]{:S(2)}, u32[]{:S(2)}) async-start(bf16[128,1,8,512]{3,2,1,0:T(8,128)(2,1)} %copy.137), calls=%async_computation | async-start | bytes 2097152 | tf_op jit(solution)/shard_map/all_to_all | solution.py:87
  18.8 1.4 fusion.11
  20.2 24.6 %all-to-all-done = bf16[128,1,8,512]{3,2,1,0:T(8,128)(2,1)S(1)} async-done(((bf16[128,1,8,512]{3,2,1,0:T(8,128)(2,1)}), bf16[128,1,8,512]{3,2,1,0:T(8,128)(2,1)S(1)}, u32[]{:S(2)}, u32[]{:S(2)}) %all-to-all-start) | async-done | bytes 1048608 | tf_op jit(solution)/shard_map/all_to_all | solution.py:87
  44.8 7.3 %all-to-all-start.2 = ((bf16[1,128,8,512]{3,2,0,1:T(8,128)(2,1)}), bf16[1,128,8,512]{3,2,0,1:T(8,128)(2,1)S(1)}, u32[]{:S(2)}, u32[]{:S(2)}) async-start(bf16[1,128,8,512]{3,2,0,1:T(8,128)(2,1)} %fusion.11), calls=%async_computation.2 | async-start | bytes 2097152 | tf_op jit(solution)/shard_map/all_to_all | solution.py:105
  52.1 2.1 %copy.140 = bf16[4,256,256]{1,2,0:T(8,128)(2,1)} copy(bf16[4,256,256]{2,1,0:T(8,128)(2,1)} %param.9) | data formatting | bytes 1048576 | tf_op args[3]
  54.1 2.2 %fusion.7 = (bf16[4,256,512]{2,1,0:T(8,128)(2,1)}, f32[4,512,256]{1,2,0:T(8,128)}) fusion(bf16[4,256,256]{2,1,0:T(8,128)(2,1)S(1)} %copy-done, bf16[4,32,1,8,512]{4,3,0,1,2:T(8,128)(2,1)S(1)} %bitcast.181), kind=kOutput, calls=%fused_computation.10 | convolution fusion | flops 271056896 | bytes 4718592 | tf_op jit(solution)/shard_map/jbt,jbc->jct/dot_general | solution.py:89
  56.4 21.8 %all-to-all-done.2 = bf16[1,128,8,512]{3,2,0,1:T(8,128)(2,1)S(1)} async-done(((bf16[1,128,8,512]{3,2,0,1:T(8,128)(2,1)}), bf16[1,128,8,512]{3,2,0,1:T(8,128)(2,1)S(1)}, u32[]{:S(2)}, u32[]{:S(2)}) %all-to-all-start.2) | async-done | bytes 1048608 | tf_op jit(solution)/shard_map/all_to_all | solution.py:105
  78.2 3.0 %fusion.5 = bf16[4,256,512]{2,1,0:T(8,128)(2,1)S(1)} fusion(f32[4,512,256]{1,2,0:T(8,128)} %get-tuple-element.36, bf16[32,4,8,512]{3,2,1,0:T(8,128)(2,1)S(1)} %bitcast.195, bf16[4,256,256]{1,2,0:T(8,128)(2,1)} %copy.140), kind=kOutput, calls=%fused_computation.6 | convolution fusion | flops 273678336 | bytes 4718592 | tf_op jit(solution)/shard_map/kjgt,jbkg->jbt/dot_general | solution.py:106
  81.2 1.0 copy-done.1
  82.2 0.4 fusion.13
  82.6 1.1 copy.146
  83.8 7.4 %all-to-all-start.3 = ((bf16[4,32,8,512]{3,2,0,1:T(8,128)(2,1)}), bf16[4,32,8,512]{3,2,0,1:T(8,128)(2,1)S(1)}, u32[]{:S(2)}, u32[]{:S(2)}) async-start(bf16[4,32,8,512]{3,2,0,1:T(8,128)(2,1)} %copy.146), calls=%async_computation.3 | async-start | bytes 2097152 | tf_op jit(solution)/shard_map/all_to_all | solution.py:110
  91.2 1.8 fusion.12
  93.0 1.6 copy.142
  94.5 22.7 %all-to-all-done.3 = bf16[4,32,8,512]{3,2,0,1:T(8,128)(2,1)S(1)} async-done(((bf16[4,32,8,512]{3,2,0,1:T(8,128)(2,1)}), bf16[4,32,8,512]{3,2,0,1:T(8,128)(2,1)S(1)}, u32[]{:S(2)}, u32[]{:S(2)}) %all-to-all-start.3) | async-done | bytes 1048608 | tf_op jit(solution)/shard_map/all_to_all | solution.py:110
  117.2 7.3 %all-to-all-start.1 = ((bf16[32,4,8,512]{3,2,1,0:T(8,128)(2,1)}), bf16[32,4,8,512]{3,2,1,0:T(8,128)(2,1)}, u32[]{:S(2)}, u32[]{:S(2)}) async-start(bf16[32,4,8,512]{3,2,1,0:T(8,128)(2,1)} %copy.142), calls=%async_computation.1 | async-start | bytes 2097152 | tf_op jit(solution)/shard_map/all_to_all | solution.py:94
  124.6 1.8 copy.147
  126.4 1.7 copy.148
  128.1 1.1 copy.138
  129.2 0.5 copy-done.6
  129.7 0.1 copy.151
  129.8 0.2 copy-done.13
  130.0 0.5 fusion.16
  130.5 4.7 %reshape_reshape.10 = f32[4,16,16,256]{2,1,3,0:T(8,128)} reshape(f32[4,256,32,8]{1,3,2,0:T(8,128)S(1)} %fusion.16) | data formatting | bytes 2097152 | tf_op jit(solution)/shard_map/reshape;reshape | solution.py:128
  135.2 2.5 %constant_dynamic-slice_fusion.1 = bf16[4,8,16,256]{2,1,3,0:T(8,128)(2,1)S(1)} fusion(f32[4,16,16,256]{2,1,3,0:T(8,128)} %reshape_reshape.10, s32[]{:T(128)S(6)} %select_n.17), kind=kLoop, calls=%fused_computation.84 | loop fusion | bytes 524292 | tf_op jit(solution)/shard_map/dynamic_slice | solution.py:49
  137.7 1.8 copy.165
  139.4 1.3 copy.150
  140.7 4.5 %constant_dynamic-slice_fusion = f32[4,8,16,256]{2,1,3,0:T(8,128)} fusion(f32[4,16,16,256]{2,1,3,0:T(8,128)} %reshape_reshape.10, s32[]{:T(128)S(6)} %select_n.16), kind=kLoop, calls=%fused_computation.83 | loop fusion | bytes 1048580 | tf_op jit(solution)/shard_map/dynamic_slice | solution.py:48
  145.2 3.6 %copy.166 = f32[4,8,16,256]{3,2,1,0:T(8,128)} copy(f32[4,8,16,256]{2,1,3,0:T(8,128)} %constant_dynamic-slice_fusion) | data formatting | bytes 1048576
  148.8 0.5 fusion.45
  149.3 0.7 copy-done.4
  150.0 0.0 copy-done.11
  150.0 0.5 fusion.44
  150.5 0.7 dynamic-slice_convert_fusion.2
  151.3 1.9 collective-permute-start
  153.2 1.4 copy.155
  154.6 0.4 fusion.25
  155.1 0.1 pad_maximum_fusion
  155.1 2.4 %collective-permute-start.4 = (bf16[1536,256]{1,0:T(8,128)(2,1)S(1)}, bf16[1536,256]{1,0:T(8,128)(2,1)S(1)}, u32[]{:S(2)}, u32[]{:S(2)}) collective-permute-start(bf16[1536,256]{1,0:T(8,128)(2,1)S(1)} %pad_maximum_fusion), channel_id=1, source_target_pairs={{0,32},{32,0},{64,96},{96,64},{128,160},{160,128},{192,224},{224,1... | collective-permute-start | bytes 2359304 | tf_op jit(solution)/shard_map/ppermute | solution.py:54
  157.6 1.2 fusion.14
  158.8 0.1 convert_add_fusion.3
  158.9 3.5 %collective-permute-start.1 = (bf16[64,1024]{1,0:T(8,128)(2,1)S(1)}, bf16[64,1024]{1,0:T(8,128)(2,1)S(1)}, u32[]{:S(2)}, u32[]{:S(2)}) collective-permute-start(bf16[64,1024]{1,0:T(8,128)(2,1)S(1)} %bitcast.219), channel_id=1, source_target_pairs={{0,128},{32,160},{64,192},{96,224},{128,0},{160,32},{192,64},{224,... | collective-permute-start | bytes 393224 | tf_op jit(solution)/shard_map/ppermute | solution.py:54
  162.5 0.1 fusion.40
  162.5 0.1 convert_add_fusion
  162.7 0.1 convert_add_fusion.2
  162.7 0.1 convert_add_fusion.1
  162.9 2.4 %collective-permute-start.5 = (bf16[768,256]{1,0:T(8,128)(2,1)S(1)}, bf16[768,256]{1,0:T(8,128)(2,1)S(1)}, u32[]{:S(2)}, u32[]{:S(2)}) collective-permute-start(bf16[768,256]{1,0:T(8,128)(2,1)S(1)} %pad_maximum_fusion.1), channel_id=1, source_target_pairs={{0,128},{32,160},{64,192},{96,224},{128,0},{160,32},{192,64},{224,... | collective-permute-start | bytes 1179656 | tf_op jit(solution)/shard_map/ppermute | solution.py:54
  165.4 2.4 %convolution_convert_fusion.4 = bf16[512,256]{1,0:T(8,128)(2,1)} fusion(bf16[1024,512]{1,0:T(8,128)(2,1)} %bitcast.11, bf16[1,1024,256]{2,1,0:T(8,128)(2,1)S(1)} %copy-done.16), kind=kOutput, calls=%fused_computation.23 | convolution fusion | flops 268566528 | bytes 1835008 | tf_op jit(solution)/shard_map/kwt,kwc->tkc/dot_general | solution.py:96
  167.8 4.9 %collective-permute-start.2 = (bf16[32,1024]{1,0:T(8,128)(2,1)S(1)}, bf16[32,1024]{1,0:T(8,128)(2,1)S(1)}, u32[]{:S(2)}, u32[]{:S(2)}) collective-permute-start(bf16[32,1024]{1,0:T(8,128)(2,1)S(1)} %bitcast.226), channel_id=1, source_target_pairs={{0,256},{32,288},{64,320},{96,352},{128,384},{160,416},{192,448},{... | collective-permute-start | bytes 196616 | tf_op jit(solution)/shard_map/ppermute | solution.py:54
  172.8 3.5 %collective-permute-done.5 = bf16[768,256]{1,0:T(8,128)(2,1)S(1)} collective-permute-done((bf16[768,256]{1,0:T(8,128)(2,1)S(1)}, bf16[768,256]{1,0:T(8,128)(2,1)S(1)}, u32[]{:S(2)}, u32[]{:S(2)}) %collective-permute-start.5) | collective-permute-done | bytes 393248 | tf_op jit(solution)/shard_map/ppermute | solution.py:54
  176.5 4.6 %collective-permute-start.6 = (bf16[384,256]{1,0:T(8,128)(2,1)S(1)}, bf16[384,256]{1,0:T(8,128)(2,1)S(1)}, u32[]{:S(2)}, u32[]{:S(2)}) collective-permute-start(bf16[384,256]{1,0:T(8,128)(2,1)S(1)} %pad_maximum_fusion.2), channel_id=1, source_target_pairs={{0,256},{32,288},{64,320},{96,352},{128,384},{160,416},{192,448},{... | collective-permute-start | bytes 589832 | tf_op jit(solution)/shard_map/ppermute | solution.py:54
  181.2 5.0 %collective-permute-start.3 = (bf16[16,1024]{1,0:T(8,128)(2,1)S(1)}, bf16[16,1024]{1,0:T(8,128)(2,1)S(1)}, u32[]{:S(2)}, u32[]{:S(2)}) collective-permute-start(bf16[16,1024]{1,0:T(8,128)(2,1)S(1)} %fusion.36), channel_id=1, source_target_pairs={{0,64},{32,96},{64,0},{96,32},{128,192},{160,224},{192,128},{224,1... | collective-permute-start | bytes 98312 | tf_op jit(solution)/shard_map/ppermute | solution.py:54
  186.4 4.7 %collective-permute-start.7 = (bf16[192,256]{1,0:T(8,128)(2,1)S(1)}, bf16[192,256]{1,0:T(8,128)(2,1)S(1)}, u32[]{:S(2)}, u32[]{:S(2)}) collective-permute-start(bf16[192,256]{1,0:T(8,128)(2,1)S(1)} %pad_maximum_fusion.3), channel_id=1, source_target_pairs={{0,64},{32,96},{64,0},{96,32},{128,192},{160,224},{192,128},{224,1... | collective-permute-start | bytes 294920 | tf_op jit(solution)/shard_map/ppermute | solution.py:54
  191.2 0.6 fusion.35
  191.8 6.1 %collective-permute-done.7 = bf16[192,256]{1,0:T(8,128)(2,1)S(1)} collective-permute-done((bf16[192,256]{1,0:T(8,128)(2,1)S(1)}, bf16[192,256]{1,0:T(8,128)(2,1)S(1)}, u32[]{:S(2)}, u32[]{:S(2)}) %collective-permute-start.7) | collective-permute-done | bytes 98336 | tf_op jit(solution)/shard_map/ppermute | solution.py:54
  197.9 0.6 fusion.33
  198.6 0.6 fusion.31
  199.2 0.6 fusion.29
  (60 shorter events, 0.7 us)
Async XLA Ops:
  0.6 53.5 %copy-start = (bf16[4,256,256]{2,1,0:T(8,128)(2,1)S(1)}, bf16[4,256,256]{2,1,0:T(8,128)(2,1)}, u32[]{:S(2)}) copy-start(bf16[4,256,256]{2,1,0:T(8,128)(2,1)} %param.8) | copy-start | bytes 1572868
  3.4 15.4 %copy-start.10 = (bf16[512,256]{1,0:T(8,128)(2,1)S(1)}, bf16[512,256]{1,0:T(8,128)(2,1)}, u32[]{:S(2)}) copy-start(bf16[512,256]{1,0:T(8,128)(2,1)} %param.11) | copy-start | bytes 786436
  3.4 15.4 %copy-start.15 = (bf16[1,1024,256]{2,1,0:T(8,128)(2,1)S(1)}, bf16[1,1024,256]{2,1,0:T(8,128)(2,1)}, u32[]{:S(2)}) copy-start(bf16[1,1024,256]{2,1,0:T(8,128)(2,1)} %param.10) | copy-start | bytes 1572868
  5.0 39.9 %all-to-all-start = ((bf16[128,1,8,512]{3,2,1,0:T(8,128)(2,1)}), bf16[128,1,8,512]{3,2,1,0:T(8,128)(2,1)S(1)}, u32[]{:S(2)}, u32[]{:S(2)}) async-start(bf16[128,1,8,512]{3,2,1,0:T(8,128)(2,1)} %copy.137), calls=%async_computation | async-start | bytes 2097152 | tf_op jit(solution)/shard_map/all_to_all | solution.py:87
  44.8 33.4 %all-to-all-start.2 = ((bf16[1,128,8,512]{3,2,0,1:T(8,128)(2,1)}), bf16[1,128,8,512]{3,2,0,1:T(8,128)(2,1)S(1)}, u32[]{:S(2)}, u32[]{:S(2)}) async-start(bf16[1,128,8,512]{3,2,0,1:T(8,128)(2,1)} %fusion.11), calls=%async_computation.2 | async-start | bytes 2097152 | tf_op jit(solution)/shard_map/all_to_all | solution.py:105
  78.2 3.0 %copy-start.12 = (bf16[1,128,8,512]{3,2,0,1:T(8,128)(2,1)}, bf16[1,128,8,512]{3,2,0,1:T(8,128)(2,1)S(1)}, u32[]{:S(2)}) copy-start(bf16[1,128,8,512]{3,2,0,1:T(8,128)(2,1)S(1)} %all-to-all-done.2) | copy-start | bytes 3145732
  81.2 1.0 copy-start.1
  83.8 33.5 %all-to-all-start.3 = ((bf16[4,32,8,512]{3,2,0,1:T(8,128)(2,1)}), bf16[4,32,8,512]{3,2,0,1:T(8,128)(2,1)S(1)}, u32[]{:S(2)}, u32[]{:S(2)}) async-start(bf16[4,32,8,512]{3,2,0,1:T(8,128)(2,1)} %copy.146), calls=%async_computation.3 | async-start | bytes 2097152 | tf_op jit(solution)/shard_map/all_to_all | solution.py:110
  117.2 11.9 %copy-start.3 = (bf16[4,32,8,512]{3,2,0,1:T(8,128)(2,1)}, bf16[4,32,8,512]{3,2,0,1:T(8,128)(2,1)S(1)}, u32[]{:S(2)}) copy-start(bf16[4,32,8,512]{3,2,0,1:T(8,128)(2,1)S(1)} %all-to-all-done.3) | copy-start | bytes 3145732
  117.2 36.0 %all-to-all-start.1 = ((bf16[32,4,8,512]{3,2,1,0:T(8,128)(2,1)}), bf16[32,4,8,512]{3,2,1,0:T(8,128)(2,1)}, u32[]{:S(2)}, u32[]{:S(2)}) async-start(bf16[32,4,8,512]{3,2,1,0:T(8,128)(2,1)} %copy.142), calls=%async_computation.1 | async-start | bytes 2097152 | tf_op jit(solution)/shard_map/all_to_all | solution.py:94
  128.1 1.6 copy-start.6
  128.1 1.9 copy-start.13
  145.2 3.6 %copy-start.2 = (bf16[4,256,512]{2,1,0:T(8,128)(2,1)S(1)}, bf16[4,256,512]{2,1,0:T(8,128)(2,1)}, u32[]{:S(2)}) copy-start(bf16[4,256,512]{2,1,0:T(8,128)(2,1)} %copy-done.1) | copy-start | bytes 3145732
  148.8 1.2 copy-start.4
  148.8 1.3 copy-start.11
  149.3 1.3 copy-start.7
  151.3 7.5 %collective-permute-start = (bf16[128,1024]{1,0:T(8,128)(2,1)}, bf16[128,1024]{1,0:T(8,128)(2,1)S(1)}, u32[]{:S(2)}, u32[]{:S(2)}) collective-permute-start(bf16[128,1024]{1,0:T(8,128)(2,1)} %bitcast.32), channel_id=1, source_target_pairs={{0,32},{32,0},{64,96},{96,64},{128,160},{160,128},{192,224},{224,1... | collective-permute-start | bytes 786440 | tf_op jit(solution)/shard_map/ppermute | solution.py:54
  153.2 1.9 copy-start.14
  154.6 3.0 %copy-start.5 = (bf16[4,32,8,512]{3,2,0,1:T(8,128)(2,1)S(1)}, bf16[4,32,8,512]{3,2,0,1:T(8,128)(2,1)}, u32[]{:S(2)}) copy-start(bf16[4,32,8,512]{3,2,0,1:T(8,128)(2,1)} %copy-done.3) | copy-start | bytes 3145732
  155.1 7.3 %collective-permute-start.4 = (bf16[1536,256]{1,0:T(8,128)(2,1)S(1)}, bf16[1536,256]{1,0:T(8,128)(2,1)S(1)}, u32[]{:S(2)}, u32[]{:S(2)}) collective-permute-start(bf16[1536,256]{1,0:T(8,128)(2,1)S(1)} %pad_maximum_fusion), channel_id=1, source_target_pairs={{0,32},{32,0},{64,96},{96,64},{128,160},{160,128},{192,224},{224,1... | collective-permute-start | bytes 2359304 | tf_op jit(solution)/shard_map/ppermute | solution.py:54
  158.8 3.8 %copy-start.8 = (f32[4,256,256]{2,1,0:T(8,128)S(1)}, f32[4,256,256]{2,1,0:T(8,128)}, u32[]{:S(2)}) copy-start(f32[4,256,256]{2,1,0:T(8,128)} %copy-done.7) | copy-start | bytes 3145732
  158.9 3.8 %copy-start.9 = (f32[4,8,16,256]{3,2,1,0:T(8,128)S(1)}, f32[4,8,16,256]{3,2,1,0:T(8,128)}, u32[]{:S(2)}) copy-start(f32[4,8,16,256]{3,2,1,0:T(8,128)} %copy.166) | copy-start | bytes 1572868
  158.9 8.9 %collective-permute-start.1 = (bf16[64,1024]{1,0:T(8,128)(2,1)S(1)}, bf16[64,1024]{1,0:T(8,128)(2,1)S(1)}, u32[]{:S(2)}, u32[]{:S(2)}) collective-permute-start(bf16[64,1024]{1,0:T(8,128)(2,1)S(1)} %bitcast.219), channel_id=1, source_target_pairs={{0,128},{32,160},{64,192},{96,224},{128,0},{160,32},{192,64},{224,... | collective-permute-start | bytes 393224 | tf_op jit(solution)/shard_map/ppermute | solution.py:54
  162.6 2.8 %copy-start.16 = (bf16[1,1024,256]{2,1,0:T(8,128)(2,1)S(1)}, bf16[1,1024,256]{2,1,0:T(8,128)(2,1)}, u32[]{:S(2)}) copy-start(bf16[1,1024,256]{2,1,0:T(8,128)(2,1)} %param.10) | copy-start | bytes 1572868
  162.9 13.3 %collective-permute-start.5 = (bf16[768,256]{1,0:T(8,128)(2,1)S(1)}, bf16[768,256]{1,0:T(8,128)(2,1)S(1)}, u32[]{:S(2)}, u32[]{:S(2)}) collective-permute-start(bf16[768,256]{1,0:T(8,128)(2,1)S(1)} %pad_maximum_fusion.1), channel_id=1, source_target_pairs={{0,128},{32,160},{64,192},{96,224},{128,0},{160,32},{192,64},{224,... | collective-permute-start | bytes 1179656 | tf_op jit(solution)/shard_map/ppermute | solution.py:54
  167.8 13.3 %collective-permute-start.2 = (bf16[32,1024]{1,0:T(8,128)(2,1)S(1)}, bf16[32,1024]{1,0:T(8,128)(2,1)S(1)}, u32[]{:S(2)}, u32[]{:S(2)}) collective-permute-start(bf16[32,1024]{1,0:T(8,128)(2,1)S(1)} %bitcast.226), channel_id=1, source_target_pairs={{0,256},{32,288},{64,320},{96,352},{128,384},{160,416},{192,448},{... | collective-permute-start | bytes 196616 | tf_op jit(solution)/shard_map/ppermute | solution.py:54
  176.5 9.7 %collective-permute-start.6 = (bf16[384,256]{1,0:T(8,128)(2,1)S(1)}, bf16[384,256]{1,0:T(8,128)(2,1)S(1)}, u32[]{:S(2)}, u32[]{:S(2)}) collective-permute-start(bf16[384,256]{1,0:T(8,128)(2,1)S(1)} %pad_maximum_fusion.2), channel_id=1, source_target_pairs={{0,256},{32,288},{64,320},{96,352},{128,384},{160,416},{192,448},{... | collective-permute-start | bytes 589832 | tf_op jit(solution)/shard_map/ppermute | solution.py:54
  181.2 10.0 %collective-permute-start.3 = (bf16[16,1024]{1,0:T(8,128)(2,1)S(1)}, bf16[16,1024]{1,0:T(8,128)(2,1)S(1)}, u32[]{:S(2)}, u32[]{:S(2)}) collective-permute-start(bf16[16,1024]{1,0:T(8,128)(2,1)S(1)} %fusion.36), channel_id=1, source_target_pairs={{0,64},{32,96},{64,0},{96,32},{128,192},{160,224},{192,128},{224,1... | collective-permute-start | bytes 98312 | tf_op jit(solution)/shard_map/ppermute | solution.py:54
  186.4 11.5 %collective-permute-start.7 = (bf16[192,256]{1,0:T(8,128)(2,1)S(1)}, bf16[192,256]{1,0:T(8,128)(2,1)S(1)}, u32[]{:S(2)}, u32[]{:S(2)}) collective-permute-start(bf16[192,256]{1,0:T(8,128)(2,1)S(1)} %pad_maximum_fusion.3), channel_id=1, source_target_pairs={{0,64},{32,96},{64,0},{96,32},{128,192},{160,224},{192,128},{224,1... | collective-permute-start | bytes 294920 | tf_op jit(solution)/shard_map/ppermute | solution.py:54

commit v4 on v3

v4 whole, which is shorter than its diff:
```python
import jax
import jax.numpy as jnp
from jax import lax
from jax.sharding import PartitionSpec as P

half_root = 0.7071067811865476
inv_root_two_pi = 0.3989422804014327


def gelu_value(value):
    return 0.5 * value * (1.0 + jax.scipy.special.erf(value * half_root))


def gelu_slope(value):
    return (
        0.5 * (1.0 + jax.scipy.special.erf(value * half_root))
        + value * jnp.exp(-0.5 * value * value) * inv_root_two_pi
    )


def dp_bit_order(replicas):
    bits = replicas.bit_length() - 1
    assert 1 << bits == replicas
    preferred = [0, 2, 3, 1]
    if bits == 4:
        return preferred
    return list(range(bits))


def chunk_order(x, axis, replicas):
    order = dp_bit_order(replicas)
    bits = len(order)
    shape = x.shape
    view = x.reshape(shape[:axis] + (2,) * bits + (shape[axis] // replicas,) + shape[axis + 1 :])
    moved = [axis + bits - 1 - b for b in order]
    perm = list(range(axis)) + moved + list(range(axis + bits, view.ndim))
    return jnp.transpose(view, perm).reshape(shape)


def dp_reduce_scatter(arrays, replicas):
    idx = lax.axis_index("dp")
    order = dp_bit_order(replicas)
    size = replicas
    for bit in order:
        half = size // 2
        me = (idx >> bit) & 1
        keeps = [lax.dynamic_slice_in_dim(a, me * half, half, axis=1) for a in arrays]
        sends = [lax.dynamic_slice_in_dim(a, (1 - me) * half, half, axis=1) for a in arrays]
        packed = jnp.concatenate([s.astype(jnp.bfloat16).reshape(-1, s.shape[-1]) for s in sends], axis=0)
        perm = [(i, i ^ (1 << bit)) for i in range(replicas)]
        got = lax.ppermute(packed, "dp", perm)
        arrays = []
        offset = 0
        for k in keeps:
            rows = k.size // k.shape[-1]
            arrays.append(k + got[offset : offset + rows].reshape(k.shape).astype(jnp.float32))
            offset += rows
        size = half
    return [a.reshape(a.shape[:1] + a.shape[2:]) for a in arrays]


def shards(tokens, first_right, first_left, second_right, second_left, cotangent):
    fp = jnp.float32
    bf = jnp.bfloat16
    tok_rows = tokens.shape[0]
    in_blocks = first_right.shape[0]
    block_width = first_right.shape[1]
    wide_width = first_right.shape[2]
    hid_blocks = first_left.shape[0]
    groups = lax.axis_size("tensor")
    replicas = lax.axis_size("dp")
    all_in = in_blocks * groups
    all_hid = hid_blocks * groups
    sub_width = wide_width // all_hid
    grad_scale = float(tok_rows * replicas) ** (-0.5)
    right_one = first_right.reshape(in_blocks, block_width, all_hid, sub_width)
    right_two = second_right.reshape(hid_blocks, block_width, all_in, sub_width)
    tok_parts = tokens.reshape(tok_rows, in_blocks, block_width)
    cot_parts = cotangent.reshape(tok_rows, in_blocks, block_width)

    up_inner = jnp.einsum("tkb,kbjg->jkgt", tok_parts, right_one, preferred_element_type=fp).astype(bf)
    d_mixed_down = jnp.einsum("tkc,kwc->kwt", cot_parts, second_left, preferred_element_type=fp).astype(bf)
    d_mixed_down = jnp.transpose(d_mixed_down.reshape(in_blocks, all_hid, sub_width, tok_rows), (1, 0, 2, 3))
    first_send = jnp.stack([up_inner, d_mixed_down], axis=1)
    first_got = lax.all_to_all(first_send, "tensor", split_axis=0, concat_axis=2, tiled=True)
    mixed_piece = first_got[:, 0].reshape(hid_blocks, block_width, tok_rows)
    d_down_inner = first_got[:, 1]

    pre_piece = jnp.einsum("jbt,jbc->jct", mixed_piece, first_left, preferred_element_type=fp)
    hidden = gelu_value(pre_piece).astype(bf)
    down_inner = jnp.einsum("jbt,jbkg->kjgt", hidden, right_two, preferred_element_type=fp).astype(bf)
    d_hidden = jnp.einsum("jkgt,jbkg->jbt", d_down_inner, right_two, preferred_element_type=fp)
    d_pre = (d_hidden * gelu_slope(pre_piece)).astype(bf)
    d_mixed_up = jnp.einsum("jct,jbc->jbt", d_pre, first_left, preferred_element_type=fp).astype(bf)
    d_mixed_up = jnp.transpose(d_mixed_up.reshape(hid_blocks, all_in, sub_width, tok_rows), (1, 0, 2, 3))

    second_send = jnp.stack([down_inner, d_mixed_up], axis=1)
    second_got = lax.all_to_all(second_send, "tensor", split_axis=0, concat_axis=2, tiled=True)
    mixed_down = second_got[:, 0].reshape(in_blocks, wide_width, tok_rows)
    d_up_inner = second_got[:, 1]

    layer_out = jnp.einsum("kwt,kwc->tkc", mixed_down, second_left, preferred_element_type=fp).astype(bf)
    layer_out = layer_out.reshape(tok_rows, in_blocks * block_width)
    grad_tokens = jnp.einsum("kjgt,kbjg->tkb", d_up_inner, right_one, preferred_element_type=fp).astype(bf)
    grad_tokens = grad_tokens.reshape(tok_rows, in_blocks * block_width)

    quarters = wide_width // block_width
    d_up_flat = d_up_inner.reshape(quarters, block_width, tok_rows)
    tok_sorted = chunk_order(tok_parts[:, 0, :], 1, replicas)
    tok_wide = jnp.broadcast_to(tok_sorted[None], (quarters,) + tok_sorted.shape)
    mixed_sorted = chunk_order(mixed_piece, 1, replicas)
    hidden_sorted = chunk_order(hidden, 1, replicas)
    down_sorted = chunk_order(mixed_down, 1, replicas)
    g_right_one = jnp.einsum("qtb,qnt->qbn", tok_wide, d_up_flat, preferred_element_type=fp)
    g_left_one = jnp.einsum("jbt,jct->jbc", mixed_sorted, d_pre, preferred_element_type=fp)
    g_right_two = jnp.einsum(
        "jbt,jkgt->jbkg", hidden_sorted, d_down_inner, preferred_element_type=fp
    ).reshape(hid_blocks, block_width, block_width)
    g_left_two = jnp.einsum("kwt,tkc->kwc", down_sorted, cot_parts, preferred_element_type=fp)

    def view(g):
        return g.reshape(g.shape[0], replicas, -1, g.shape[-1])

    reduced = dp_reduce_scatter(
        [view(g_right_one), view(g_left_one), view(g_right_two), view(g_left_two)], replicas
    )
    grad_right_one, grad_left_one, grad_right_two, grad_left_two = [r * grad_scale for r in reduced]
    grad_right_one = jnp.transpose(grad_right_one, (1, 0, 2)).reshape(in_blocks, -1, wide_width)
    return (layer_out, grad_tokens, grad_right_one, grad_left_one, grad_right_two, grad_left_two)


def solution(mesh):
    in_specs = (
        P("dp", "tensor"),
        P("tensor", None, None),
        P("tensor", None, None),
        P("tensor", None, None),
        P("tensor", None, None),
        P("dp", "tensor"),
    )
    out_specs = (
        P("dp", "tensor"),
        P("dp", "tensor"),
        P("tensor", "dp", None),
        P("tensor", "dp", None),
        P("tensor", "dp", None),
        P("tensor", "dp", None),
    )
    return jax.shard_map(shards, mesh=mesh, in_specs=in_specs, out_specs=out_specs, check_vma=False)
```

time: 201 us -> 224 us (1.11)
  the two profiles are of different devices: /device:TPU:24 before, /device:TPU:1 now
where the time goes in v4:
time: 224 us; the launch traced here: 222 us
  waiting for transfers between devices  113 us (50%)
  starting transfers between devices  49.9 us (22%)
  local copies, waits for them, and re-layouts  42.7 us (19%)
  matrix products  9.81 us (4%)
  other arithmetic  5.82 us (3%)
    all_to_all x1, waiting for transfers between devices, shards(): lax.all_to_all(first_send, 'tensor', split_axis=0, concat_axis=2, tiled=T...  52.3 us
    all_to_all x1, waiting for transfers between devices, shards(): lax.all_to_all(second_send, 'tensor', split_axis=0, concat_axis=2, tiled=...  40.2 us
    ppermute x4, starting transfers between devices, dp_reduce_scatter(): got = lax.ppermute(packed, 'dp', perm)  29.3 us
    ppermute x4, waiting for transfers between devices, dp_reduce_scatter(): got = lax.ppermute(packed, 'dp', perm)  20.1 us
    all_to_all x1, starting transfers between devices, shards(): lax.all_to_all(first_send, 'tensor', split_axis=0, concat_axis=2, tiled=T...  14.3 us
    unnamed x50, local copies, waits for them, and re-layouts  14 us
    all_to_all x1, starting transfers between devices, shards(): lax.all_to_all(second_send, 'tensor', split_axis=0, concat_axis=2, tiled=...  6.23 us
    another operation x1, local copies, waits for them, and re-layouts, view(): return g.reshape(g.shape[0], replicas, -1, g.shape[-1])  4.72 us
  transfers between devices with their start and end apart: 6, of which 5 were waited for; matrix products, arithmetic and copies ran while one was open for 12% of the time, Pallas kernels for 0%

profile of v4, /device:TPU:1, one launch (start us, length us, event | category | flops | bytes accessed | tf_op | source)
XLA Modules:
  0.0 222.3 jit_solution(7709156537991459656)
XLA Ops:
  0.7 1.7 fusion.11
  2.3 0.3 copy.175
  2.7 0.2 copy.173
  2.9 0.4 copy.188
  3.3 0.5 fusion.10
  3.8 0.2 pad_maximum_fusion
  4.0 2.5 %copy.176 = bf16[128,2,1,8,512]{4,3,2,1,0:T(8,128)(2,1)} copy(bf16[128,2,1,8,512]{4,0,3,2,1:T(8,128)(2,1)S(1)} %pad_maximum_fusion) | data formatting | bytes 4194304 | tf_op jit(solution)/shard_map/stack | solution.py:84
  6.5 14.3 %all-to-all-start = ((bf16[128,2,1,8,512]{4,3,2,1,0:T(8,128)(2,1)}), bf16[128,2,1,8,512]{4,3,2,1,0:T(8,128)(2,1)S(1)}, u32[]{:S(2)}, u32[]{:S(2)}) async-start(bf16[128,2,1,8,512]{4,3,2,1,0:T(8,128)(2,1)} %copy.176), calls=%async_computation | async-start | bytes 4194304 | tf_op jit(solution)/shard_map/all_to_all | solution.py:85
  20.8 2.1 copy.180
  22.9 52.3 %all-to-all-done = bf16[128,2,1,8,512]{4,3,2,1,0:T(8,128)(2,1)S(1)} async-done(((bf16[128,2,1,8,512]{4,3,2,1,0:T(8,128)(2,1)}), bf16[128,2,1,8,512]{4,3,2,1,0:T(8,128)(2,1)S(1)}, u32[]{:S(2)}, u32[]{:S(2)}) %all-to-all-start) | async-done | bytes 2097184 | tf_op jit(solution)/shard_map/all_to_all | solution.py:85
  75.2 1.2 copy.224
  76.4 1.2 slice_bitcast_fusion
  77.5 1.1 fusion.7
  78.6 1.2 fusion.5
  79.9 0.4 fusion.13
  80.3 0.3 copy.225
  80.6 0.2 copy-done.4
  80.8 0.4 fusion.12
  81.3 0.2 pad_maximum_fusion.1
  81.5 2.5 %copy.185 = bf16[32,2,4,8,512]{4,3,2,1,0:T(8,128)(2,1)} copy(bf16[32,2,4,8,512]{4,0,3,2,1:T(8,128)(2,1)S(1)} %pad_maximum_fusion.1) | data formatting | bytes 4194304 | tf_op jit(solution)/shard_map/stack | solution.py:97
  84.0 6.2 %all-to-all-start.1 = ((bf16[32,2,4,8,512]{4,3,2,1,0:T(8,128)(2,1)}), bf16[32,2,4,8,512]{4,3,2,1,0:T(8,128)(2,1)}, u32[]{:S(2)}, u32[]{:S(2)}) async-start(bf16[32,2,4,8,512]{4,3,2,1,0:T(8,128)(2,1)} %copy.185), calls=%async_computation.1 | async-start | bytes 4194304 | tf_op jit(solution)/shard_map/all_to_all | solution.py:98
  90.3 0.1 copy.190
  90.5 1.6 copy.178
  92.1 0.8 fusion.20
  92.9 4.7 %reshape_reshape.3 = f32[4,16,16,256]{2,1,3,0:T(8,128)} reshape(f32[4,256,32,8]{1,3,2,0:T(8,128)S(1)} %fusion.20) | data formatting | bytes 2097152 | tf_op jit(solution)/shard_map/reshape;reshape | solution.py:122
  97.6 2.5 %constant_dynamic-slice_fusion.1 = bf16[4,8,16,256]{2,1,3,0:T(8,128)(2,1)S(1)} fusion(f32[4,16,16,256]{2,1,3,0:T(8,128)} %reshape_reshape.3, s32[]{:T(128)S(6)} %select_n.17), kind=kLoop, calls=%fused_computation.91 | loop fusion | bytes 524292 | tf_op jit(solution)/shard_map/dynamic_slice | solution.py:48
  100.1 1.1 copy.208
  101.2 1.4 copy.193
  102.5 0.2 copy-done.5
  102.7 0.5 fusion.47
  103.2 40.2 %all-to-all-done.1 = bf16[32,2,4,8,512]{4,3,2,1,0:T(8,128)(2,1)} async-done(((bf16[32,2,4,8,512]{4,3,2,1,0:T(8,128)(2,1)}), bf16[32,2,4,8,512]{4,3,2,1,0:T(8,128)(2,1)}, u32[]{:S(2)}, u32[]{:S(2)}) %all-to-all-start.1) | async-done | bytes 2097184 | tf_op jit(solution)/shard_map/all_to_all | solution.py:98
  143.4 1.8 copy.186
  145.2 0.1 fusion.42
  145.4 1.2 copy-done.2
  146.5 0.1 copy.197
  146.6 0.8 copy-done.15
  147.5 0.4 fusion.28
  147.9 1.0 copy-done.6
  148.9 0.5 fusion.24
  149.4 1.0 copy-done.8
  150.5 1.0 pad_maximum_fusion.2
  151.5 5.0 %collective-permute-start = (bf16[2048,256]{1,0:T(8,128)(2,1)}, bf16[2048,256]{1,0:T(8,128)(2,1)}, u32[]{:S(2)}, u32[]{:S(2)}) collective-permute-start(bf16[2048,256]{1,0:T(8,128)(2,1)} %pad_maximum_fusion.2), channel_id=1, source_target_pairs={{0,32},{32,0},{64,96},{96,64},{128,160},{160,128},{192,224},{224,1... | collective-permute-start | bytes 3145736 | tf_op jit(solution)/shard_map/ppermute | solution.py:51
  156.5 4.5 %constant_dynamic-slice_fusion = f32[4,8,16,256]{2,1,3,0:T(8,128)} fusion(f32[4,16,16,256]{2,1,3,0:T(8,128)} %reshape_reshape.3, s32[]{:T(128)S(6)} %select_n.16), kind=kLoop, calls=%fused_computation.90 | loop fusion | bytes 1048580 | tf_op jit(solution)/shard_map/dynamic_slice | solution.py:47
  161.0 2.8 %copy.209 = f32[4,8,16,256]{3,2,1,0:T(8,128)S(1)} copy(f32[4,8,16,256]{2,1,3,0:T(8,128)} %constant_dynamic-slice_fusion) | data formatting | bytes 1048576
  163.8 1.3 fusion.43
  165.1 0.2 copy-done.7
  165.5 0.1 convert_add_fusion.2
  165.7 1.4 copy-done.9
  167.3 0.8 pad_maximum_fusion.3
  168.1 3.1 %collective-permute-start.1 = (bf16[1024,256]{1,0:T(8,128)(2,1)}, bf16[1024,256]{1,0:T(8,128)(2,1)}, u32[]{:S(2)}, u32[]{:S(2)}) collective-permute-start(bf16[1024,256]{1,0:T(8,128)(2,1)} %pad_maximum_fusion.3), channel_id=1, source_target_pairs={{0,128},{32,160},{64,192},{96,224},{128,0},{160,32},{192,64},{224,... | collective-permute-start | bytes 1572872 | tf_op jit(solution)/shard_map/ppermute | solution.py:51
  171.2 1.7 copy.207
  172.9 10.8 %collective-permute-done.1 = bf16[1024,256]{1,0:T(8,128)(2,1)} collective-permute-done((bf16[1024,256]{1,0:T(8,128)(2,1)}, bf16[1024,256]{1,0:T(8,128)(2,1)}, u32[]{:S(2)}, u32[]{:S(2)}) %collective-permute-start.1) | collective-permute-done | bytes 524320 | tf_op jit(solution)/shard_map/ppermute | solution.py:51
  183.8 1.1 fusion.44
  185.0 1.1 convert_add_fusion.5
  186.3 4.8 %collective-permute-start.2 = (bf16[512,256]{1,0:T(8,128)(2,1)S(1)}, bf16[512,256]{1,0:T(8,128)(2,1)S(1)}, u32[]{:S(2)}, u32[]{:S(2)}) collective-permute-start(bf16[512,256]{1,0:T(8,128)(2,1)S(1)} %pad_maximum_fusion.4), channel_id=1, source_target_pairs={{0,256},{32,288},{64,320},{96,352},{128,384},{160,416},{192,448},{... | collective-permute-start | bytes 786440 | tf_op jit(solution)/shard_map/ppermute | solution.py:51
  191.1 1.2 convolution_convert_fusion.4
  192.3 4.5 %collective-permute-done.2 = bf16[512,256]{1,0:T(8,128)(2,1)S(1)} collective-permute-done((bf16[512,256]{1,0:T(8,128)(2,1)S(1)}, bf16[512,256]{1,0:T(8,128)(2,1)S(1)}, u32[]{:S(2)}, u32[]{:S(2)}) %collective-permute-start.2) | collective-permute-done | bytes 262176 | tf_op jit(solution)/shard_map/ppermute | solution.py:51
  197.1 16.5 %collective-permute-start.3 = (bf16[256,256]{1,0:T(8,128)(2,1)S(1)}, bf16[256,256]{1,0:T(8,128)(2,1)S(1)}, u32[]{:S(2)}, u32[]{:S(2)}) collective-permute-start(bf16[256,256]{1,0:T(8,128)(2,1)S(1)} %pad_maximum_fusion.5), channel_id=1, source_target_pairs={{0,64},{32,96},{64,0},{96,32},{128,192},{160,224},{192,128},{224,1... | collective-permute-start | bytes 393224 | tf_op jit(solution)/shard_map/ppermute | solution.py:51
  213.6 1.2 fusion.14
  214.8 4.8 %collective-permute-done.3 = bf16[256,256]{1,0:T(8,128)(2,1)S(1)} collective-permute-done((bf16[256,256]{1,0:T(8,128)(2,1)S(1)}, bf16[256,256]{1,0:T(8,128)(2,1)S(1)}, u32[]{:S(2)}, u32[]{:S(2)}) %collective-permute-start.3) | collective-permute-done | bytes 131104 | tf_op jit(solution)/shard_map/ppermute | solution.py:51
  219.7 0.7 reshape.317
  220.3 0.6 fusion.36
  221.0 0.6 fusion.34
  221.6 0.6 fusion.32
  (69 shorter events, 1.0 us)
Async XLA Ops:
  0.6 76.9 %copy-start = (bf16[4,256,256]{2,1,0:T(8,128)(2,1)S(1)}, bf16[4,256,256]{2,1,0:T(8,128)(2,1)}, u32[]{:S(2)}) copy-start(bf16[4,256,256]{2,1,0:T(8,128)(2,1)} %param.8) | copy-start | bytes 1572868
  0.6 2.0 copy-start.20
  2.3 1.0 copy-start.16
  6.5 68.7 %all-to-all-start = ((bf16[128,2,1,8,512]{4,3,2,1,0:T(8,128)(2,1)}), bf16[128,2,1,8,512]{4,3,2,1,0:T(8,128)(2,1)S(1)}, u32[]{:S(2)}, u32[]{:S(2)}) async-start(bf16[128,2,1,8,512]{4,3,2,1,0:T(8,128)(2,1)} %copy.176), calls=%async_computation | async-start | bytes 4194304 | tf_op jit(solution)/shard_map/all_to_all | solution.py:85
  77.5 1.1 copy-start.21
  79.9 1.0 copy-start.4
  84.0 59.4 %all-to-all-start.1 = ((bf16[32,2,4,8,512]{4,3,2,1,0:T(8,128)(2,1)}), bf16[32,2,4,8,512]{4,3,2,1,0:T(8,128)(2,1)}, u32[]{:S(2)}, u32[]{:S(2)}) async-start(bf16[32,2,4,8,512]{4,3,2,1,0:T(8,128)(2,1)} %copy.185), calls=%async_computation.1 | async-start | bytes 4194304 | tf_op jit(solution)/shard_map/all_to_all | solution.py:98
  90.4 1.7 copy-start.18
  101.2 1.5 copy-start.5
  145.2 1.3 copy-start.2
  146.5 0.9 copy-start.15
  147.9 1.0 copy-start.6
  149.4 1.0 copy-start.8
  151.5 12.3 %collective-permute-start = (bf16[2048,256]{1,0:T(8,128)(2,1)}, bf16[2048,256]{1,0:T(8,128)(2,1)}, u32[]{:S(2)}, u32[]{:S(2)}) collective-permute-start(bf16[2048,256]{1,0:T(8,128)(2,1)} %pad_maximum_fusion.2), channel_id=1, source_target_pairs={{0,32},{32,0},{64,96},{96,64},{128,160},{160,128},{192,224},{224,1... | collective-permute-start | bytes 3145736 | tf_op jit(solution)/shard_map/ppermute | solution.py:51
  163.8 1.5 copy-start.7
  165.3 1.8 copy-start.9
  165.4 1.8 copy-start.10
  165.5 1.7 copy-start.14
  165.6 1.6 copy-start.12
  167.2 17.7 %copy-start.11 = (f32[8,64,256]{2,1,0:T(8,128)S(1)}, f32[8,64,256]{2,1,0:T(8,128)}, u32[]{:S(2)}) copy-start(f32[8,64,256]{2,1,0:T(8,128)} %copy-done.10) | copy-start | bytes 1572868
  168.1 15.7 %collective-permute-start.1 = (bf16[1024,256]{1,0:T(8,128)(2,1)}, bf16[1024,256]{1,0:T(8,128)(2,1)}, u32[]{:S(2)}, u32[]{:S(2)}) collective-permute-start(bf16[1024,256]{1,0:T(8,128)(2,1)} %pad_maximum_fusion.3), channel_id=1, source_target_pairs={{0,128},{32,160},{64,192},{96,224},{128,0},{160,32},{192,64},{224,... | collective-permute-start | bytes 1572872 | tf_op jit(solution)/shard_map/ppermute | solution.py:51
  171.2 14.9 %copy-start.13 = (f32[4,8,16,256]{3,2,1,0:T(8,128)S(1)}, f32[4,8,16,256]{3,2,1,0:T(8,128)}, u32[]{:S(2)}) copy-start(f32[4,8,16,256]{3,2,1,0:T(8,128)} %copy-done.12) | copy-start | bytes 1572868
  184.9 6.2 %copy-start.3 = (bf16[32,2,4,8,512]{4,3,2,0,1:T(8,128)(2,1)S(1)}, bf16[32,2,4,8,512]{4,3,2,0,1:T(8,128)(2,1)}, u32[]{:S(2)}) copy-start(bf16[32,2,4,8,512]{4,3,2,0,1:T(8,128)(2,1)} %copy-done.2) | copy-start | bytes 6291460
  184.9 6.2 %copy-start.19 = (bf16[1,1024,256]{2,1,0:T(8,128)(2,1)S(1)}, bf16[1,1024,256]{2,1,0:T(8,128)(2,1)}, u32[]{:S(2)}) copy-start(bf16[1,1024,256]{2,1,0:T(8,128)(2,1)} %param.10) | copy-start | bytes 1572868
  186.3 27.3 %copy-start.17 = (bf16[1,1,128,8,512]{2,4,3,1,0:T(8,128)(2,1)S(1)}, bf16[1,1,128,8,512]{2,4,3,1,0:T(8,128)(2,1)}, u32[]{:S(2)}) copy-start(bf16[1,1,128,8,512]{2,4,3,1,0:T(8,128)(2,1)} %copy.207) | copy-start | bytes 3145732
  186.3 10.5 %collective-permute-start.2 = (bf16[512,256]{1,0:T(8,128)(2,1)S(1)}, bf16[512,256]{1,0:T(8,128)(2,1)S(1)}, u32[]{:S(2)}, u32[]{:S(2)}) collective-permute-start(bf16[512,256]{1,0:T(8,128)(2,1)S(1)} %pad_maximum_fusion.4), channel_id=1, source_target_pairs={{0,256},{32,288},{64,320},{96,352},{128,384},{160,416},{192,448},{... | collective-permute-start | bytes 786440 | tf_op jit(solution)/shard_map/ppermute | solution.py:51
  196.9 25.3 %copy-start.1 = (bf16[4,256,256]{2,1,0:T(8,128)(2,1)S(1)}, bf16[4,256,256]{2,1,0:T(8,128)(2,1)}, u32[]{:S(2)}) copy-start(bf16[4,256,256]{2,1,0:T(8,128)(2,1)} %param.8) | copy-start | bytes 1572868
  197.1 22.5 %collective-permute-start.3 = (bf16[256,256]{1,0:T(8,128)(2,1)S(1)}, bf16[256,256]{1,0:T(8,128)(2,1)S(1)}, u32[]{:S(2)}, u32[]{:S(2)}) collective-permute-start(bf16[256,256]{1,0:T(8,128)(2,1)S(1)} %pad_maximum_fusion.5), channel_id=1, source_target_pairs={{0,64},{32,96},{64,0},{96,32},{128,192},{160,224},{192,128},{224,1... | collective-permute-start | bytes 393224 | tf_op jit(solution)/shard_map/ppermute | solution.py:51

commit v5 on v3

--- a/solution.py
+++ b/solution.py
@@ -37,27 +37,23 @@
     return jnp.transpose(view, perm).reshape(shape)
 
 
-def dp_reduce_scatter(wide, narrow, replicas):
+def dp_reduce_scatter(arrays, replicas):
     idx = lax.axis_index("dp")
     order = dp_bit_order(replicas)
-    arrays = [wide] + list(narrow)
     size = replicas
     for bit in order:
         half = size // 2
         me = (idx >> bit) & 1
         keeps = [lax.dynamic_slice_in_dim(a, me * half, half, axis=1) for a in arrays]
         sends = [lax.dynamic_slice_in_dim(a, (1 - me) * half, half, axis=1) for a in arrays]
-        sends = [s.astype(jnp.bfloat16) for s in sends]
-        first = sends[0].reshape(-1, sends[0].shape[-1])
-        rest = jnp.concatenate([s.reshape(-1, s.shape[-1]) for s in sends[1:]], axis=0)
+        packed = jnp.concatenate([s.astype(jnp.bfloat16).reshape(-1, s.shape[-1]) for s in sends], axis=0)
         perm = [(i, i ^ (1 << bit)) for i in range(replicas)]
-        got_first, got_rest = lax.ppermute((first, rest), "dp", perm)
-        arrays = [keeps[0] + got_first.reshape(keeps[0].shape).astype(jnp.float32)]
+        got = lax.ppermute(packed, "dp", perm)
+        arrays = []
         offset = 0
-        for k in keeps[1:]:
+        for k in keeps:
             rows = k.size // k.shape[-1]
-            part = got_rest[offset : offset + rows].reshape(k.shape)
-            arrays.append(k + part.astype(jnp.float32))
+            arrays.append(k + got[offset : offset + rows].reshape(k.shape).astype(jnp.float32))
             offset += rows
         size = half
     return [a.reshape(a.shape[:1] + a.shape[2:]) for a in arrays]
@@ -127,9 +123,10 @@
     def view(g):
         return g.reshape(in_blocks if g.ndim == 2 else g.shape[0], replicas, -1, g.shape[-1])
 
-    reduced = dp_reduce_scatter(
-        view(g_right_one), [view(g_left_one), view(g_right_two), view(g_left_two)], replicas
-    )
+    (red_left_two,) = dp_reduce_scatter([view(g_left_two)], replicas)
+    red_left_one, red_right_two = dp_reduce_scatter([view(g_left_one), view(g_right_two)], replicas)
+    (red_right_one,) = dp_reduce_scatter([view(g_right_one)], replicas)
+    reduced = (red_right_one, red_left_one, red_right_two, red_left_two)
     grad_right_one, grad_left_one, grad_right_two, grad_left_two = [r * grad_scale for r in reduced]
     return (layer_out, grad_tokens, grad_right_one, grad_left_one, grad_right_two, grad_left_two)
 

time: 201 us -> 220 us (1.095)
  the two profiles are of different devices: /device:TPU:24 before, /device:TPU:1 now
where the time goes in v5:
time: 220 us; the launch traced here: 217 us
  starting transfers between devices  82.8 us (38%)
  waiting for transfers between devices  66.5 us (30%)
  local copies, waits for them, and re-layouts  37.4 us (17%)
  matrix products  17 us (8%)
  other arithmetic  11.6 us (5%)
    ppermute x12, starting transfers between devices, dp_reduce_scatter(): got = lax.ppermute(packed, 'dp', perm)  45.8 us
    all_to_all x1, waiting for transfers between devices, shards(): lax.all_to_all(up_inner, 'tensor', split_axis=0, concat_axis=1, tiled=True)  24.4 us
    ppermute x12, waiting for transfers between devices, dp_reduce_scatter(): got = lax.ppermute(packed, 'dp', perm)  21.6 us
    all_to_all x1, waiting for transfers between devices, shards(): lax.all_to_all(d_mixed_down, 'tensor', split_axis=1, concat_axis=0, tiled...  20.5 us
    all_to_all x1, starting transfers between devices, shards(): lax.all_to_all(up_inner, 'tensor', split_axis=0, concat_axis=1, tiled=True)  14.3 us
    unnamed x41, local copies, waits for them, and re-layouts  13.9 us
    all_to_all x1, starting transfers between devices, shards(): lax.all_to_all(d_mixed_up, 'tensor', split_axis=1, concat_axis=0, tiled=T...  9.29 us
    all_to_all x1, starting transfers between devices, shards(): lax.all_to_all(d_mixed_down, 'tensor', split_axis=1, concat_axis=0, tiled...  7.69 us
  transfers between devices with their start and end apart: 16, of which 7 were waited for; matrix products, arithmetic and copies ran while one was open for 18% of the time, Pallas kernels for 0%

profile of v5, /device:TPU:1, one launch (start us, length us, event | category | flops | bytes accessed | tf_op | source)
XLA Modules:
  0.0 216.6 jit_solution(8892521751515061065)
XLA Ops:
  0.6 1.3 copy.167
  2.0 1.4 fusion.10
  3.4 1.6 copy.169
  5.0 14.3 %all-to-all-start = ((bf16[128,1,8,512]{3,2,1,0:T(8,128)(2,1)}), bf16[128,1,8,512]{3,2,1,0:T(8,128)(2,1)S(1)}, u32[]{:S(2)}, u32[]{:S(2)}) async-start(bf16[128,1,8,512]{3,2,1,0:T(8,128)(2,1)} %copy.169), calls=%async_computation | async-start | bytes 2097152 | tf_op jit(solution)/shard_map/all_to_all | solution.py:83
  19.3 1.5 fusion.11
  20.7 24.4 %all-to-all-done = bf16[128,1,8,512]{3,2,1,0:T(8,128)(2,1)S(1)} async-done(((bf16[128,1,8,512]{3,2,1,0:T(8,128)(2,1)}), bf16[128,1,8,512]{3,2,1,0:T(8,128)(2,1)S(1)}, u32[]{:S(2)}, u32[]{:S(2)}) %all-to-all-start) | async-done | bytes 1048608 | tf_op jit(solution)/shard_map/all_to_all | solution.py:83
  45.1 7.7 %all-to-all-start.2 = ((bf16[1,128,8,512]{3,2,0,1:T(8,128)(2,1)}), bf16[1,128,8,512]{3,2,0,1:T(8,128)(2,1)}, u32[]{:S(2)}, u32[]{:S(2)}) async-start(bf16[1,128,8,512]{3,2,0,1:T(8,128)(2,1)} %fusion.11), calls=%async_computation.2 | async-start | bytes 2097152 | tf_op jit(solution)/shard_map/all_to_all | solution.py:101
  52.8 1.0 copy.172
  54.0 2.0 fusion.7
  56.0 1.0 copy-done.3
  57.0 1.0 copy.183
  58.0 20.5 %all-to-all-done.2 = bf16[1,128,8,512]{3,2,0,1:T(8,128)(2,1)} async-done(((bf16[1,128,8,512]{3,2,0,1:T(8,128)(2,1)}), bf16[1,128,8,512]{3,2,0,1:T(8,128)(2,1)}, u32[]{:S(2)}, u32[]{:S(2)}) %all-to-all-start.2) | async-done | bytes 1048608 | tf_op jit(solution)/shard_map/all_to_all | solution.py:101
  78.5 2.0 fusion.16
  80.5 4.7 %reshape_reshape.10 = f32[4,16,16,256]{2,1,3,0:T(8,128)} reshape(f32[4,256,32,8]{1,3,2,0:T(8,128)S(1)} %fusion.16) | data formatting | bytes 2097152 | tf_op jit(solution)/shard_map/reshape;reshape | solution.py:124
  85.2 3.1 %fusion.5 = bf16[4,256,512]{2,1,0:T(8,128)(2,1)S(1)} fusion(f32[4,512,256]{1,2,0:T(8,128)} %get-tuple-element.39, bf16[32,4,8,512]{3,2,1,0:T(8,128)(2,1)} %bitcast.15, bf16[4,256,256]{1,2,0:T(8,128)(2,1)} %copy.172), kind=kOutput, calls=%fused_computation.6 | convolution fusion | flops 273678336 | bytes 4718592 | tf_op jit(solution)/shard_map/kjgt,jbkg->jbt/dot_general | solution.py:102
  89.9 0.7 dynamic-slice_convert_fusion.1
  90.6 2.5 %constant_dynamic-slice_fusion.1 = bf16[4,8,16,256]{2,1,3,0:T(8,128)(2,1)S(1)} fusion(f32[4,16,16,256]{2,1,3,0:T(8,128)} %reshape_reshape.10, s32[]{:T(128)S(6)} %select_n.17), kind=kLoop, calls=%fused_computation.83 | loop fusion | bytes 524292 | tf_op jit(solution)/shard_map/dynamic_slice | solution.py:48
  93.1 1.8 copy.199
  94.8 1.9 pad_maximum_fusion
  96.7 4.6 %collective-permute-start.4 = (bf16[1024,256]{1,0:T(8,128)(2,1)}, bf16[1024,256]{1,0:T(8,128)(2,1)}, u32[]{:S(2)}, u32[]{:S(2)}) collective-permute-start(bf16[1024,256]{1,0:T(8,128)(2,1)} %pad_maximum_fusion), channel_id=1, source_target_pairs={{0,32},{32,0},{64,96},{96,64},{128,160},{160,128},{192,224},{224,1... | collective-permute-start | bytes 1572872 | tf_op jit(solution)/shard_map/ppermute | solution.py:51
  101.3 1.8 fusion.12
  103.1 1.5 copy.174
  104.7 5.7 %all-to-all-start.1 = ((bf16[32,4,8,512]{3,2,1,0:T(8,128)(2,1)}), bf16[32,4,8,512]{3,2,1,0:T(8,128)(2,1)S(1)}, u32[]{:S(2)}, u32[]{:S(2)}) async-start(bf16[32,4,8,512]{3,2,1,0:T(8,128)(2,1)} %copy.174), calls=%async_computation.1 | async-start | bytes 2097152 | tf_op jit(solution)/shard_map/all_to_all | solution.py:90
  110.4 4.5 %constant_dynamic-slice_fusion = f32[4,8,16,256]{2,1,3,0:T(8,128)} fusion(f32[4,16,16,256]{2,1,3,0:T(8,128)} %reshape_reshape.10, s32[]{:T(128)S(6)} %select_n.16), kind=kLoop, calls=%fused_computation.82 | loop fusion | bytes 1048580 | tf_op jit(solution)/shard_map/dynamic_slice | solution.py:47
  114.9 3.6 %copy.200 = f32[4,8,16,256]{3,2,1,0:T(8,128)} copy(f32[4,8,16,256]{2,1,3,0:T(8,128)} %constant_dynamic-slice_fusion) | data formatting | bytes 1048576
  118.5 1.1 fusion.40
  119.8 0.7 copy-done.9
  120.6 0.7 copy-done.10
  121.3 0.7 pad_maximum_fusion.1
  122.0 3.1 %collective-permute-start.5 = (bf16[512,256]{1,0:T(8,128)(2,1)}, bf16[512,256]{1,0:T(8,128)(2,1)}, u32[]{:S(2)}, u32[]{:S(2)}) collective-permute-start(bf16[512,256]{1,0:T(8,128)(2,1)} %pad_maximum_fusion.1), channel_id=1, source_target_pairs={{0,128},{32,160},{64,192},{96,224},{128,0},{160,32},{192,64},{224,... | collective-permute-start | bytes 786440 | tf_op jit(solution)/shard_map/ppermute | solution.py:51
  125.2 6.6 %collective-permute-done.5 = bf16[512,256]{1,0:T(8,128)(2,1)} collective-permute-done((bf16[512,256]{1,0:T(8,128)(2,1)}, bf16[512,256]{1,0:T(8,128)(2,1)}, u32[]{:S(2)}, u32[]{:S(2)}) %collective-permute-start.5) | collective-permute-done | bytes 262176 | tf_op jit(solution)/shard_map/ppermute | solution.py:51
  131.8 1.0 fusion.41
  132.8 1.0 convert_add_fusion.6
  133.8 1.1 convert_add_fusion.5
  134.9 0.7 pad_maximum_fusion.2
  135.7 4.6 %collective-permute-start.6 = (bf16[256,256]{1,0:T(8,128)(2,1)}, bf16[256,256]{1,0:T(8,128)(2,1)S(1)}, u32[]{:S(2)}, u32[]{:S(2)}) collective-permute-start(bf16[256,256]{1,0:T(8,128)(2,1)} %pad_maximum_fusion.2), channel_id=1, source_target_pairs={{0,256},{32,288},{64,320},{96,352},{128,384},{160,416},{192,448},{... | collective-permute-start | bytes 393224 | tf_op jit(solution)/shard_map/ppermute | solution.py:51
  140.8 1.1 copy.178
  141.9 9.3 %all-to-all-start.3 = ((bf16[4,32,8,512]{3,2,0,1:T(8,128)(2,1)}), bf16[4,32,8,512]{3,2,0,1:T(8,128)(2,1)S(1)}, u32[]{:S(2)}, u32[]{:S(2)}) async-start(bf16[4,32,8,512]{3,2,0,1:T(8,128)(2,1)} %copy.178), calls=%async_computation.3 | async-start | bytes 2097152 | tf_op jit(solution)/shard_map/all_to_all | solution.py:106
  151.2 0.9 convert_add_fusion.10
  152.2 0.9 convert_add_fusion.9
  153.1 0.7 copy-done.17
  154.4 4.9 %collective-permute-start.7 = (bf16[128,256]{1,0:T(8,128)(2,1)}, bf16[128,256]{1,0:T(8,128)(2,1)}, u32[]{:S(2)}, u32[]{:S(2)}) collective-permute-start(bf16[128,256]{1,0:T(8,128)(2,1)} %pad_maximum_fusion.3), channel_id=1, source_target_pairs={{0,64},{32,96},{64,0},{96,32},{128,192},{160,224},{192,128},{224,1... | collective-permute-start | bytes 196616 | tf_op jit(solution)/shard_map/ppermute | solution.py:51
  159.3 1.8 copy.179
  161.1 1.7 copy.180
  162.8 9.5 %collective-permute-done.7 = bf16[128,256]{1,0:T(8,128)(2,1)} collective-permute-done((bf16[128,256]{1,0:T(8,128)(2,1)}, bf16[128,256]{1,0:T(8,128)(2,1)}, u32[]{:S(2)}, u32[]{:S(2)}) %collective-permute-start.7) | collective-permute-done | bytes 65568 | tf_op jit(solution)/shard_map/ppermute | solution.py:51
  172.3 0.8 fusion.43
  173.1 1.5 fusion.31
  174.6 0.6 fusion.33
  175.8 0.8 dynamic-slice_convert_fusion
  176.8 5.4 %collective-permute-start.8 = (bf16[512,256]{1,0:T(8,128)(2,1)}, bf16[512,256]{1,0:T(8,128)(2,1)S(1)}, u32[]{:S(2)}, u32[]{:S(2)}) collective-permute-start(bf16[512,256]{1,0:T(8,128)(2,1)} %bitcast.75), channel_id=1, source_target_pairs={{0,32},{32,0},{64,96},{96,64},{128,160},{160,128},{192,224},{224,1... | collective-permute-start | bytes 786440 | tf_op jit(solution)/shard_map/ppermute | solution.py:51
  182.2 1.4 fusion.44
  183.7 2.1 collective-permute-start
  185.8 1.2 fusion.14
  187.0 1.2 convolution_convert_fusion.4
  188.4 2.3 %collective-permute-start.9 = (bf16[256,256]{1,0:T(8,128)(2,1)S(1)}, bf16[256,256]{1,0:T(8,128)(2,1)S(1)}, u32[]{:S(2)}, u32[]{:S(2)}) collective-permute-start(bf16[256,256]{1,0:T(8,128)(2,1)S(1)} %bitcast.219), channel_id=1, source_target_pairs={{0,128},{32,160},{64,192},{96,224},{128,0},{160,32},{192,64},{224,... | collective-permute-start | bytes 393224 | tf_op jit(solution)/shard_map/ppermute | solution.py:51
  190.7 3.0 %collective-permute-start.1 = (bf16[64,1024]{1,0:T(8,128)(2,1)S(1)}, bf16[64,1024]{1,0:T(8,128)(2,1)S(1)}, u32[]{:S(2)}, u32[]{:S(2)}) collective-permute-start(bf16[64,1024]{1,0:T(8,128)(2,1)S(1)} %bitcast.220), channel_id=1, source_target_pairs={{0,128},{32,160},{64,192},{96,224},{128,0},{160,32},{192,64},{224,... | collective-permute-start | bytes 393224 | tf_op jit(solution)/shard_map/ppermute | solution.py:51
  193.8 1.2 collective-permute-done.9
  195.0 2.7 %collective-permute-start.10 = (bf16[128,256]{1,0:T(8,128)(2,1)S(1)}, bf16[128,256]{1,0:T(8,128)(2,1)S(1)}, u32[]{:S(2)}, u32[]{:S(2)}) collective-permute-start(bf16[128,256]{1,0:T(8,128)(2,1)S(1)} %bitcast.229), channel_id=1, source_target_pairs={{0,256},{32,288},{64,320},{96,352},{128,384},{160,416},{192,448},{... | collective-permute-start | bytes 196616 | tf_op jit(solution)/shard_map/ppermute | solution.py:51
  198.0 3.9 %collective-permute-start.2 = (bf16[32,1024]{1,0:T(8,128)(2,1)S(1)}, bf16[32,1024]{1,0:T(8,128)(2,1)S(1)}, u32[]{:S(2)}, u32[]{:S(2)}) collective-permute-start(bf16[32,1024]{1,0:T(8,128)(2,1)S(1)} %bitcast.230), channel_id=1, source_target_pairs={{0,256},{32,288},{64,320},{96,352},{128,384},{160,416},{192,448},{... | collective-permute-start | bytes 196616 | tf_op jit(solution)/shard_map/ppermute | solution.py:51
  202.0 5.0 %collective-permute-start.11 = (bf16[64,256]{1,0:T(8,128)(2,1)S(1)}, bf16[64,256]{1,0:T(8,128)(2,1)S(1)}, u32[]{:S(2)}, u32[]{:S(2)}) collective-permute-start(bf16[64,256]{1,0:T(8,128)(2,1)S(1)} %fusion.37), channel_id=1, source_target_pairs={{0,64},{32,96},{64,0},{96,32},{128,192},{160,224},{192,128},{224,1... | collective-permute-start | bytes 98312 | tf_op jit(solution)/shard_map/ppermute | solution.py:51
  207.0 4.2 %collective-permute-start.3 = (bf16[16,1024]{1,0:T(8,128)(2,1)S(1)}, bf16[16,1024]{1,0:T(8,128)(2,1)S(1)}, u32[]{:S(2)}, u32[]{:S(2)}) collective-permute-start(bf16[16,1024]{1,0:T(8,128)(2,1)S(1)} %fusion.36), channel_id=1, source_target_pairs={{0,64},{32,96},{64,0},{96,32},{128,192},{160,224},{192,128},{224,1... | collective-permute-start | bytes 98312 | tf_op jit(solution)/shard_map/ppermute | solution.py:51
  211.2 0.6 fusion.29
  211.9 4.0 %collective-permute-done.3 = bf16[16,1024]{1,0:T(8,128)(2,1)S(1)} collective-permute-done((bf16[16,1024]{1,0:T(8,128)(2,1)S(1)}, bf16[16,1024]{1,0:T(8,128)(2,1)S(1)}, u32[]{:S(2)}, u32[]{:S(2)}) %collective-permute-start.3) | collective-permute-done | bytes 32800 | tf_op jit(solution)/shard_map/ppermute | solution.py:51
  215.9 0.6 fusion.35
  (70 shorter events, 4.4 us)
Async XLA Ops:
  0.6 53.4 %copy-start = (bf16[4,256,256]{2,1,0:T(8,128)(2,1)S(1)}, bf16[4,256,256]{2,1,0:T(8,128)(2,1)}, u32[]{:S(2)}) copy-start(bf16[4,256,256]{2,1,0:T(8,128)(2,1)} %param.8) | copy-start | bytes 1572868
  3.4 15.9 %copy-start.11 = (bf16[512,256]{1,0:T(8,128)(2,1)S(1)}, bf16[512,256]{1,0:T(8,128)(2,1)}, u32[]{:S(2)}) copy-start(bf16[512,256]{1,0:T(8,128)(2,1)} %param.11) | copy-start | bytes 786436
  3.4 15.9 %copy-start.14 = (bf16[1,1024,256]{2,1,0:T(8,128)(2,1)S(1)}, bf16[1,1024,256]{2,1,0:T(8,128)(2,1)}, u32[]{:S(2)}) copy-start(bf16[1,1024,256]{2,1,0:T(8,128)(2,1)} %param.10) | copy-start | bytes 1572868
  5.0 40.2 %all-to-all-start = ((bf16[128,1,8,512]{3,2,1,0:T(8,128)(2,1)}), bf16[128,1,8,512]{3,2,1,0:T(8,128)(2,1)S(1)}, u32[]{:S(2)}, u32[]{:S(2)}) async-start(bf16[128,1,8,512]{3,2,1,0:T(8,128)(2,1)} %copy.169), calls=%async_computation | async-start | bytes 2097152 | tf_op jit(solution)/shard_map/all_to_all | solution.py:83
  19.3 33.6 %copy-start.16 = (bf16[4,256,256]{2,1,0:T(8,128)(2,1)S(1)}, bf16[4,256,256]{2,1,0:T(8,128)(2,1)}, u32[]{:S(2)}) copy-start(bf16[4,256,256]{2,1,0:T(8,128)(2,1)} %param.9) | copy-start | bytes 1572868
  45.1 33.4 %all-to-all-start.2 = ((bf16[1,128,8,512]{3,2,0,1:T(8,128)(2,1)}), bf16[1,128,8,512]{3,2,0,1:T(8,128)(2,1)}, u32[]{:S(2)}, u32[]{:S(2)}) async-start(bf16[1,128,8,512]{3,2,0,1:T(8,128)(2,1)} %fusion.11), calls=%async_computation.2 | async-start | bytes 2097152 | tf_op jit(solution)/shard_map/all_to_all | solution.py:101
  56.0 1.0 copy-start.3
  88.4 1.0 copy-start.1
  88.9 1.0 copy-start.4
  96.7 21.8 %collective-permute-start.4 = (bf16[1024,256]{1,0:T(8,128)(2,1)}, bf16[1024,256]{1,0:T(8,128)(2,1)}, u32[]{:S(2)}, u32[]{:S(2)}) collective-permute-start(bf16[1024,256]{1,0:T(8,128)(2,1)} %pad_maximum_fusion), channel_id=1, source_target_pairs={{0,32},{32,0},{64,96},{96,64},{128,160},{160,128},{192,224},{224,1... | collective-permute-start | bytes 1572872 | tf_op jit(solution)/shard_map/ppermute | solution.py:51
  104.7 37.2 %all-to-all-start.1 = ((bf16[32,4,8,512]{3,2,1,0:T(8,128)(2,1)}), bf16[32,4,8,512]{3,2,1,0:T(8,128)(2,1)S(1)}, u32[]{:S(2)}, u32[]{:S(2)}) async-start(bf16[32,4,8,512]{3,2,1,0:T(8,128)(2,1)} %copy.174), calls=%async_computation.1 | async-start | bytes 2097152 | tf_op jit(solution)/shard_map/all_to_all | solution.py:90
  114.9 4.7 %copy-start.5 = (f32[4,256,256]{2,1,0:T(8,128)S(1)}, f32[4,256,256]{2,1,0:T(8,128)}, u32[]{:S(2)}) copy-start(f32[4,256,256]{2,1,0:T(8,128)} %copy-done.4) | copy-start | bytes 3145732
  118.5 1.2 copy-start.8
  119.7 0.8 copy-start.9
  119.7 20.6 %copy-start.2 = (bf16[4,256,512]{2,1,0:T(8,128)(2,1)S(1)}, bf16[4,256,512]{2,1,0:T(8,128)(2,1)}, u32[]{:S(2)}) copy-start(bf16[4,256,512]{2,1,0:T(8,128)(2,1)} %copy-done.1) | copy-start | bytes 3145732
  120.5 0.8 copy-start.10
  122.0 9.8 %collective-permute-start.5 = (bf16[512,256]{1,0:T(8,128)(2,1)}, bf16[512,256]{1,0:T(8,128)(2,1)}, u32[]{:S(2)}, u32[]{:S(2)}) collective-permute-start(bf16[512,256]{1,0:T(8,128)(2,1)} %pad_maximum_fusion.1), channel_id=1, source_target_pairs={{0,128},{32,160},{64,192},{96,224},{128,0},{160,32},{192,64},{224,... | collective-permute-start | bytes 786440 | tf_op jit(solution)/shard_map/ppermute | solution.py:51
  133.8 1.9 copy-start.12
  134.9 0.8 copy-start.13
  135.7 15.5 %collective-permute-start.6 = (bf16[256,256]{1,0:T(8,128)(2,1)}, bf16[256,256]{1,0:T(8,128)(2,1)S(1)}, u32[]{:S(2)}, u32[]{:S(2)}) collective-permute-start(bf16[256,256]{1,0:T(8,128)(2,1)} %pad_maximum_fusion.2), channel_id=1, source_target_pairs={{0,256},{32,288},{64,320},{96,352},{128,384},{160,416},{192,448},{... | collective-permute-start | bytes 393224 | tf_op jit(solution)/shard_map/ppermute | solution.py:51
  141.9 40.3 %all-to-all-start.3 = ((bf16[4,32,8,512]{3,2,0,1:T(8,128)(2,1)}), bf16[4,32,8,512]{3,2,0,1:T(8,128)(2,1)S(1)}, u32[]{:S(2)}, u32[]{:S(2)}) async-start(bf16[4,32,8,512]{3,2,0,1:T(8,128)(2,1)} %copy.178), calls=%async_computation.3 | async-start | bytes 2097152 | tf_op jit(solution)/shard_map/all_to_all | solution.py:106
  153.1 0.7 copy-start.17
  154.4 17.9 %collective-permute-start.7 = (bf16[128,256]{1,0:T(8,128)(2,1)}, bf16[128,256]{1,0:T(8,128)(2,1)}, u32[]{:S(2)}, u32[]{:S(2)}) collective-permute-start(bf16[128,256]{1,0:T(8,128)(2,1)} %pad_maximum_fusion.3), channel_id=1, source_target_pairs={{0,64},{32,96},{64,0},{96,32},{128,192},{160,224},{192,128},{224,1... | collective-permute-start | bytes 196616 | tf_op jit(solution)/shard_map/ppermute | solution.py:51
  175.8 1.1 copy-start.6
  176.8 11.4 %collective-permute-start.8 = (bf16[512,256]{1,0:T(8,128)(2,1)}, bf16[512,256]{1,0:T(8,128)(2,1)S(1)}, u32[]{:S(2)}, u32[]{:S(2)}) collective-permute-start(bf16[512,256]{1,0:T(8,128)(2,1)} %bitcast.75), channel_id=1, source_target_pairs={{0,32},{32,0},{64,96},{96,64},{128,160},{160,128},{192,224},{224,1... | collective-permute-start | bytes 786440 | tf_op jit(solution)/shard_map/ppermute | solution.py:51
  183.7 6.9 %collective-permute-start = (bf16[128,1024]{1,0:T(8,128)(2,1)S(1)}, bf16[128,1024]{1,0:T(8,128)(2,1)S(1)}, u32[]{:S(2)}, u32[]{:S(2)}) collective-permute-start(bf16[128,1024]{1,0:T(8,128)(2,1)S(1)} %bitcast.214), channel_id=1, source_target_pairs={{0,32},{32,0},{64,96},{96,64},{128,160},{160,128},{192,224},{224,1... | collective-permute-start | bytes 786440 | tf_op jit(solution)/shard_map/ppermute | solution.py:51
  185.8 1.3 copy-start.15
  187.0 1.2 copy-start.7
  188.4 6.6 %collective-permute-start.9 = (bf16[256,256]{1,0:T(8,128)(2,1)S(1)}, bf16[256,256]{1,0:T(8,128)(2,1)S(1)}, u32[]{:S(2)}, u32[]{:S(2)}) collective-permute-start(bf16[256,256]{1,0:T(8,128)(2,1)S(1)} %bitcast.219), channel_id=1, source_target_pairs={{0,128},{32,160},{64,192},{96,224},{128,0},{160,32},{192,64},{224,... | collective-permute-start | bytes 393224 | tf_op jit(solution)/shard_map/ppermute | solution.py:51
  190.7 7.2 %collective-permute-start.1 = (bf16[64,1024]{1,0:T(8,128)(2,1)S(1)}, bf16[64,1024]{1,0:T(8,128)(2,1)S(1)}, u32[]{:S(2)}, u32[]{:S(2)}) collective-permute-start(bf16[64,1024]{1,0:T(8,128)(2,1)S(1)} %bitcast.220), channel_id=1, source_target_pairs={{0,128},{32,160},{64,192},{96,224},{128,0},{160,32},{192,64},{224,... | collective-permute-start | bytes 393224 | tf_op jit(solution)/shard_map/ppermute | solution.py:51
  195.0 6.9 %collective-permute-start.10 = (bf16[128,256]{1,0:T(8,128)(2,1)S(1)}, bf16[128,256]{1,0:T(8,128)(2,1)S(1)}, u32[]{:S(2)}, u32[]{:S(2)}) collective-permute-start(bf16[128,256]{1,0:T(8,128)(2,1)S(1)} %bitcast.229), channel_id=1, source_target_pairs={{0,256},{32,288},{64,320},{96,352},{128,384},{160,416},{192,448},{... | collective-permute-start | bytes 196616 | tf_op jit(solution)/shard_map/ppermute | solution.py:51
  198.0 8.9 %collective-permute-start.2 = (bf16[32,1024]{1,0:T(8,128)(2,1)S(1)}, bf16[32,1024]{1,0:T(8,128)(2,1)S(1)}, u32[]{:S(2)}, u32[]{:S(2)}) collective-permute-start(bf16[32,1024]{1,0:T(8,128)(2,1)S(1)} %bitcast.230), channel_id=1, source_target_pairs={{0,256},{32,288},{64,320},{96,352},{128,384},{160,416},{192,448},{... | collective-permute-start | bytes 196616 | tf_op jit(solution)/shard_map/ppermute | solution.py:51
  202.0 9.3 %collective-permute-start.11 = (bf16[64,256]{1,0:T(8,128)(2,1)S(1)}, bf16[64,256]{1,0:T(8,128)(2,1)S(1)}, u32[]{:S(2)}, u32[]{:S(2)}) collective-permute-start(bf16[64,256]{1,0:T(8,128)(2,1)S(1)} %fusion.37), channel_id=1, source_target_pairs={{0,64},{32,96},{64,0},{96,32},{128,192},{160,224},{192,128},{224,1... | collective-permute-start | bytes 98312 | tf_op jit(solution)/shard_map/ppermute | solution.py:51
  207.0 8.9 %collective-permute-start.3 = (bf16[16,1024]{1,0:T(8,128)(2,1)S(1)}, bf16[16,1024]{1,0:T(8,128)(2,1)S(1)}, u32[]{:S(2)}, u32[]{:S(2)}) collective-permute-start(bf16[16,1024]{1,0:T(8,128)(2,1)S(1)} %fusion.36), channel_id=1, source_target_pairs={{0,64},{32,96},{64,0},{96,32},{128,192},{160,224},{192,128},{224,1... | collective-permute-start | bytes 98312 | tf_op jit(solution)/shard_map/ppermute | solution.py:51

commit v6 on v5

--- a/solution.py
+++ b/solution.py
@@ -104,16 +104,9 @@
     d_mixed_up = jnp.einsum("jct,jbc->jbt", d_pre, first_left, preferred_element_type=fp).astype(bf)
     d_mixed_up = d_mixed_up.reshape(hid_blocks, all_in, sub_width, tok_rows)
     d_up_inner = lax.all_to_all(d_mixed_up, "tensor", split_axis=1, concat_axis=0, tiled=True)
-    grad_tokens = jnp.einsum(
-        "jkgt,kbjg->tkb", d_up_inner, right_one, preferred_element_type=fp
-    ).astype(bf)
-    grad_tokens = grad_tokens.reshape(tok_rows, in_blocks * block_width)
-    d_up_flat = d_up_inner.reshape(all_hid * in_blocks * sub_width, tok_rows)
-    tok_sorted = chunk_order(tok_parts[:, 0, :], 1, replicas)
     mixed_sorted = chunk_order(mixed_piece, 1, replicas)
     hidden_sorted = chunk_order(hidden, 1, replicas)
     down_sorted = chunk_order(mixed_down, 1, replicas)
-    g_right_one = jnp.einsum("tb,nt->bn", tok_sorted, d_up_flat, preferred_element_type=fp)
     g_left_one = jnp.einsum("jbt,jct->jbc", mixed_sorted, d_pre, preferred_element_type=fp)
     g_right_two = jnp.einsum(
         "jbt,kjgt->jbkg", hidden_sorted, d_down_inner, preferred_element_type=fp
@@ -123,8 +116,17 @@
     def view(g):
         return g.reshape(in_blocks if g.ndim == 2 else g.shape[0], replicas, -1, g.shape[-1])
 
-    (red_left_two,) = dp_reduce_scatter([view(g_left_two)], replicas)
-    red_left_one, red_right_two = dp_reduce_scatter([view(g_left_one), view(g_right_two)], replicas)
+    early = dp_reduce_scatter([view(g_left_two), view(g_left_one), view(g_right_two)], replicas)
+    d_up_inner, *early = lax.optimization_barrier((d_up_inner, *early))
+    red_left_two, red_left_one, red_right_two = early
+
+    grad_tokens = jnp.einsum(
+        "jkgt,kbjg->tkb", d_up_inner, right_one, preferred_element_type=fp
+    ).astype(bf)
+    grad_tokens = grad_tokens.reshape(tok_rows, in_blocks * block_width)
+    d_up_flat = d_up_inner.reshape(all_hid * in_blocks * sub_width, tok_rows)
+    tok_sorted = chunk_order(tok_parts[:, 0, :], 1, replicas)
+    g_right_one = jnp.einsum("tb,nt->bn", tok_sorted, d_up_flat, preferred_element_type=fp)
     (red_right_one,) = dp_reduce_scatter([view(g_right_one)], replicas)
     reduced = (red_right_one, red_left_one, red_right_two, red_left_two)
     grad_right_one, grad_left_one, grad_right_two, grad_left_two = [r * grad_scale for r in reduced]

time: 220 us -> 221 us (level)
  waiting for transfers between devices: 66.5 us -> 93.9 us
  starting transfers between devices: 82.8 us -> 67.6 us
  local copies, waits for them, and re-layouts: 37.4 us -> 32 us
  other arithmetic: 11.6 us -> 6.85 us
    ppermute x12 -> x8, starting transfers between devices: 45.8 us -> 31.9 us  [dp_reduce_scatter(): got = lax.ppermute(packed, 'dp', perm)]
    ppermute x12 -> x8, waiting for transfers between devices: 21.6 us -> 33.6 us  [dp_reduce_scatter(): got = lax.ppermute(packed, 'dp', perm)]
    all_to_all x1, waiting for transfers between devices: 0.01 us -> 9.29 us  [shards(): lax.all_to_all(down_inner, 'tensor', split_axis=0, concat_axis=1, tiled=T...]
    all_to_all x1, waiting for transfers between devices: 0.01 us -> 5.96 us  [shards(): lax.all_to_all(d_mixed_up, 'tensor', split_axis=1, concat_axis=0, tiled=T...]
    unnamed x41 -> x43, local copies, waits for them, and re-layouts: 13.9 us -> 10.2 us
    all_to_all x1, starting transfers between devices: 9.29 us -> 5.76 us  [shards(): lax.all_to_all(d_mixed_up, 'tensor', split_axis=1, concat_axis=0, tiled=T...]
    add x12, other arithmetic: 4.29 us -> 1.43 us  [dp_reduce_scatter(): k + got[offset:offset + rows].reshape(k.shape).astype(jnp.float32)]
  transfers between devices with their start and end apart: 16 -> 12, of which waited for: 7 -> 9; matrix products, arithmetic and copies ran while one was open for 18% -> 18% of each run, Pallas kernels for 0% -> 0%
where the time goes in v6:
time: 221 us; the launch traced here: 217 us
  waiting for transfers between devices  93.9 us (42%)
  starting transfers between devices  67.6 us (31%)
  local copies, waits for them, and re-layouts  32 us (14%)
  matrix products  15.7 us (7%)
  other arithmetic  6.85 us (3%)
    ppermute x8, waiting for transfers between devices, dp_reduce_scatter(): got = lax.ppermute(packed, 'dp', perm)  33.6 us
    ppermute x8, starting transfers between devices, dp_reduce_scatter(): got = lax.ppermute(packed, 'dp', perm)  31.9 us
    all_to_all x1, waiting for transfers between devices, shards(): lax.all_to_all(up_inner, 'tensor', split_axis=0, concat_axis=1, tiled=True)  24.4 us
    all_to_all x1, waiting for transfers between devices, shards(): lax.all_to_all(d_mixed_down, 'tensor', split_axis=1, concat_axis=0, tiled...  20.7 us
    all_to_all x1, starting transfers between devices, shards(): lax.all_to_all(up_inner, 'tensor', split_axis=0, concat_axis=1, tiled=True)  14.3 us
    unnamed x43, local copies, waits for them, and re-layouts  10.2 us
    all_to_all x1, waiting for transfers between devices, shards(): lax.all_to_all(down_inner, 'tensor', split_axis=0, concat_axis=1, tiled=T...  9.29 us
    all_to_all x1, starting transfers between devices, shards(): lax.all_to_all(down_inner, 'tensor', split_axis=0, concat_axis=1, tiled=T...  7.88 us
  transfers between devices with their start and end apart: 12, of which 9 were waited for; matrix products, arithmetic and copies ran while one was open for 18% of the time, Pallas kernels for 0%

profile of v6, /device:TPU:1, one launch (start us, length us, event | category | flops | bytes accessed | tf_op | source)
XLA Modules:
  0.0 217.3 jit_solution(11438501234739311443)
XLA Ops:
  0.6 1.3 copy.135
  2.0 1.4 fusion.10
  3.4 1.6 copy.137
  5.0 14.3 %all-to-all-start = ((bf16[128,1,8,512]{3,2,1,0:T(8,128)(2,1)}), bf16[128,1,8,512]{3,2,1,0:T(8,128)(2,1)S(1)}, u32[]{:S(2)}, u32[]{:S(2)}) async-start(bf16[128,1,8,512]{3,2,1,0:T(8,128)(2,1)} %copy.137), calls=%async_computation | async-start | bytes 2097152 | tf_op jit(solution)/shard_map/all_to_all | solution.py:83
  19.3 1.4 fusion.11
  20.7 24.4 %all-to-all-done = bf16[128,1,8,512]{3,2,1,0:T(8,128)(2,1)S(1)} async-done(((bf16[128,1,8,512]{3,2,1,0:T(8,128)(2,1)}), bf16[128,1,8,512]{3,2,1,0:T(8,128)(2,1)S(1)}, u32[]{:S(2)}, u32[]{:S(2)}) %all-to-all-start) | async-done | bytes 1048608 | tf_op jit(solution)/shard_map/all_to_all | solution.py:83
  45.1 7.7 %all-to-all-start.2 = ((bf16[1,128,8,512]{3,2,0,1:T(8,128)(2,1)}), bf16[1,128,8,512]{3,2,0,1:T(8,128)(2,1)}, u32[]{:S(2)}, u32[]{:S(2)}) async-start(bf16[1,128,8,512]{3,2,0,1:T(8,128)(2,1)} %fusion.11), calls=%async_computation.2 | async-start | bytes 2097152 | tf_op jit(solution)/shard_map/all_to_all | solution.py:101
  52.8 1.0 copy.140
  53.8 2.0 fusion.7
  55.8 0.4 fusion.12
  56.3 1.6 copy.142
  57.8 20.7 %all-to-all-done.2 = bf16[1,128,8,512]{3,2,0,1:T(8,128)(2,1)} async-done(((bf16[1,128,8,512]{3,2,0,1:T(8,128)(2,1)}), bf16[1,128,8,512]{3,2,0,1:T(8,128)(2,1)}, u32[]{:S(2)}, u32[]{:S(2)}) %all-to-all-start.2) | async-done | bytes 1048608 | tf_op jit(solution)/shard_map/all_to_all | solution.py:101
  78.5 7.9 %all-to-all-start.1 = ((bf16[32,4,8,512]{3,2,1,0:T(8,128)(2,1)}), bf16[32,4,8,512]{3,2,1,0:T(8,128)(2,1)}, u32[]{:S(2)}, u32[]{:S(2)}) async-start(bf16[32,4,8,512]{3,2,1,0:T(8,128)(2,1)} %copy.142), calls=%async_computation.1 | async-start | bytes 2097152 | tf_op jit(solution)/shard_map/all_to_all | solution.py:90
  86.4 0.1 copy.138
  86.5 1.1 copy.149
  87.6 1.7 fusion.19
  89.4 4.7 %reshape_reshape.11 = f32[4,16,16,256]{2,1,3,0:T(8,128)} reshape(f32[4,256,32,8]{1,3,2,0:T(8,128)S(1)} %fusion.19) | data formatting | bytes 2097152 | tf_op jit(solution)/shard_map/reshape;reshape | solution.py:117
  94.1 2.5 %constant_dynamic-slice_fusion.1 = bf16[4,8,16,256]{2,1,3,0:T(8,128)(2,1)S(1)} fusion(f32[4,16,16,256]{2,1,3,0:T(8,128)} %reshape_reshape.11, s32[]{:T(128)S(6)} %select_n.17), kind=kLoop, calls=%fused_computation.87 | loop fusion | bytes 524292 | tf_op jit(solution)/shard_map/dynamic_slice | solution.py:48
  96.6 1.8 copy.170
  98.3 3.2 %fusion.5 = bf16[4,256,512]{2,1,0:T(8,128)(2,1)S(1)} fusion(f32[4,512,256]{1,2,0:T(8,128)} %get-tuple-element.44, bf16[32,4,8,512]{3,2,1,0:T(8,128)(2,1)} %bitcast.15, bf16[4,256,256]{1,2,0:T(8,128)(2,1)} %copy.140), kind=kOutput, calls=%fused_computation.6 | convolution fusion | flops 273678336 | bytes 4718592 | tf_op jit(solution)/shard_map/kjgt,jbkg->jbt/dot_general | solution.py:102
  101.6 0.5 fusion.44
  102.0 0.7 dynamic-slice_convert_fusion.1
  102.8 9.3 %all-to-all-done.1 = bf16[32,4,8,512]{3,2,1,0:T(8,128)(2,1)} async-done(((bf16[32,4,8,512]{3,2,1,0:T(8,128)(2,1)}), bf16[32,4,8,512]{3,2,1,0:T(8,128)(2,1)}, u32[]{:S(2)}, u32[]{:S(2)}) %all-to-all-start.1) | async-done | bytes 1048608 | tf_op jit(solution)/shard_map/all_to_all | solution.py:90
  112.1 1.4 copy.147
  113.4 0.4 fusion.28
  113.9 1.0 copy-done.2
  114.9 1.0 pad_maximum_fusion
  115.9 4.6 %collective-permute-start = (bf16[1536,256]{1,0:T(8,128)(2,1)}, bf16[1536,256]{1,0:T(8,128)(2,1)}, u32[]{:S(2)}, u32[]{:S(2)}) collective-permute-start(bf16[1536,256]{1,0:T(8,128)(2,1)} %pad_maximum_fusion), channel_id=1, source_target_pairs={{0,32},{32,0},{64,96},{96,64},{128,160},{160,128},{192,224},{224,1... | collective-permute-start | bytes 2359304 | tf_op jit(solution)/shard_map/ppermute | solution.py:51
  120.5 4.5 %constant_dynamic-slice_fusion = f32[4,8,16,256]{2,1,3,0:T(8,128)} fusion(f32[4,16,16,256]{2,1,3,0:T(8,128)} %reshape_reshape.11, s32[]{:T(128)S(6)} %select_n.16), kind=kLoop, calls=%fused_computation.86 | loop fusion | bytes 1048580 | tf_op jit(solution)/shard_map/dynamic_slice | solution.py:47
  125.0 3.5 %copy.171 = f32[4,8,16,256]{3,2,0,1:T(8,128)} copy(f32[4,8,16,256]{2,1,3,0:T(8,128)} %constant_dynamic-slice_fusion) | data formatting | bytes 1048576
  128.5 1.3 fusion.40
  129.8 0.1 convert_add_fusion.1
  129.9 0.1 copy-done.3
  130.1 0.1 copy_add_fusion
  130.3 0.8 pad_maximum_fusion.1
  131.0 3.1 %collective-permute-start.1 = (bf16[768,256]{1,0:T(8,128)(2,1)}, bf16[768,256]{1,0:T(8,128)(2,1)S(1)}, u32[]{:S(2)}, u32[]{:S(2)}) collective-permute-start(bf16[768,256]{1,0:T(8,128)(2,1)} %pad_maximum_fusion.1), channel_id=1, source_target_pairs={{0,128},{32,160},{64,192},{96,224},{128,0},{160,32},{192,64},{224,... | collective-permute-start | bytes 1179656 | tf_op jit(solution)/shard_map/ppermute | solution.py:51
  134.2 9.6 %collective-permute-done.1 = bf16[768,256]{1,0:T(8,128)(2,1)S(1)} collective-permute-done((bf16[768,256]{1,0:T(8,128)(2,1)}, bf16[768,256]{1,0:T(8,128)(2,1)S(1)}, u32[]{:S(2)}, u32[]{:S(2)}) %collective-permute-start.1) | collective-permute-done | bytes 393248 | tf_op jit(solution)/shard_map/ppermute | solution.py:51
  143.9 1.0 convert_add_fusion.4
  145.0 4.6 %collective-permute-start.2 = (bf16[384,256]{1,0:T(8,128)(2,1)S(1)}, bf16[384,256]{1,0:T(8,128)(2,1)}, u32[]{:S(2)}, u32[]{:S(2)}) collective-permute-start(bf16[384,256]{1,0:T(8,128)(2,1)S(1)} %pad_maximum_fusion.2), channel_id=1, source_target_pairs={{0,256},{32,288},{64,320},{96,352},{128,384},{160,416},{192,448},{... | collective-permute-start | bytes 589832 | tf_op jit(solution)/shard_map/ppermute | solution.py:51
  149.7 0.4 fusion.13
  150.1 1.1 copy.146
  151.3 5.8 %all-to-all-start.3 = ((bf16[4,32,8,512]{3,2,0,1:T(8,128)(2,1)}), bf16[4,32,8,512]{3,2,0,1:T(8,128)(2,1)S(1)}, u32[]{:S(2)}, u32[]{:S(2)}) async-start(bf16[4,32,8,512]{3,2,0,1:T(8,128)(2,1)} %copy.146), calls=%async_computation.3 | async-start | bytes 2097152 | tf_op jit(solution)/shard_map/all_to_all | solution.py:106
  157.0 0.9 fusion.42
  158.1 0.6 copy-done.17
  158.8 4.8 %collective-permute-start.3 = (bf16[192,256]{1,0:T(8,128)(2,1)S(1)}, bf16[192,256]{1,0:T(8,128)(2,1)S(1)}, u32[]{:S(2)}, u32[]{:S(2)}) collective-permute-start(bf16[192,256]{1,0:T(8,128)(2,1)S(1)} %pad_maximum_fusion.3), channel_id=1, source_target_pairs={{0,64},{32,96},{64,0},{96,32},{128,192},{160,224},{192,128},{224,1... | collective-permute-start | bytes 294920 | tf_op jit(solution)/shard_map/ppermute | solution.py:51
  163.6 0.1 copy.160
  163.7 14.4 %collective-permute-done.3 = bf16[192,256]{1,0:T(8,128)(2,1)S(1)} collective-permute-done((bf16[192,256]{1,0:T(8,128)(2,1)S(1)}, bf16[192,256]{1,0:T(8,128)(2,1)S(1)}, u32[]{:S(2)}, u32[]{:S(2)}) %collective-permute-start.3) | collective-permute-done | bytes 98336 | tf_op jit(solution)/shard_map/ppermute | solution.py:51
  178.2 0.6 copy-done.18
  178.8 0.8 fusion.33
  179.7 0.9 fusion.35
  180.5 6.0 %all-to-all-done.3 = bf16[4,32,8,512]{3,2,0,1:T(8,128)(2,1)S(1)} async-done(((bf16[4,32,8,512]{3,2,0,1:T(8,128)(2,1)}), bf16[4,32,8,512]{3,2,0,1:T(8,128)(2,1)S(1)}, u32[]{:S(2)}, u32[]{:S(2)}) %all-to-all-start.3) | async-done | bytes 1048608 | tf_op jit(solution)/shard_map/all_to_all | solution.py:106
  186.5 0.5 fusion.16
  187.0 4.9 %collective-permute-start.4 = (bf16[128,1024]{1,0:T(8,128)(2,1)S(1)}, bf16[128,1024]{1,0:T(8,128)(2,1)S(1)}, u32[]{:S(2)}, u32[]{:S(2)}) collective-permute-start(bf16[128,1024]{1,0:T(8,128)(2,1)S(1)} %bitcast.213), channel_id=1, source_target_pairs={{0,32},{32,0},{64,96},{96,64},{128,160},{160,128},{192,224},{224,1... | collective-permute-start | bytes 786440 | tf_op jit(solution)/shard_map/ppermute | solution.py:51
  191.9 2.4 %convolution_convert_fusion.4 = bf16[512,256]{1,0:T(8,128)(2,1)} fusion(bf16[1024,512]{1,0:T(8,128)(2,1)} %bitcast.11, bf16[1,1024,256]{2,1,0:T(8,128)(2,1)S(1)} %copy-done.13), kind=kOutput, calls=%fused_computation.23 | convolution fusion | flops 268566528 | bytes 1835008 | tf_op jit(solution)/shard_map/kwt,kwc->tkc/dot_general | solution.py:92
  194.4 2.2 %collective-permute-start.5 = (bf16[64,1024]{1,0:T(8,128)(2,1)S(1)}, bf16[64,1024]{1,0:T(8,128)(2,1)S(1)}, u32[]{:S(2)}, u32[]{:S(2)}) collective-permute-start(bf16[64,1024]{1,0:T(8,128)(2,1)S(1)} %bitcast.220), channel_id=1, source_target_pairs={{0,128},{32,160},{64,192},{96,224},{128,0},{160,32},{192,64},{224,... | collective-permute-start | bytes 393224 | tf_op jit(solution)/shard_map/ppermute | solution.py:51
  196.6 1.2 fusion.14
  197.9 3.5 %collective-permute-done.5 = bf16[64,1024]{1,0:T(8,128)(2,1)S(1)} collective-permute-done((bf16[64,1024]{1,0:T(8,128)(2,1)S(1)}, bf16[64,1024]{1,0:T(8,128)(2,1)S(1)}, u32[]{:S(2)}, u32[]{:S(2)}) %collective-permute-start.5) | collective-permute-done | bytes 131104 | tf_op jit(solution)/shard_map/ppermute | solution.py:51
  201.4 2.8 %collective-permute-start.6 = (bf16[32,1024]{1,0:T(8,128)(2,1)S(1)}, bf16[32,1024]{1,0:T(8,128)(2,1)S(1)}, u32[]{:S(2)}, u32[]{:S(2)}) collective-permute-start(bf16[32,1024]{1,0:T(8,128)(2,1)S(1)} %bitcast.227), channel_id=1, source_target_pairs={{0,256},{32,288},{64,320},{96,352},{128,384},{160,416},{192,448},{... | collective-permute-start | bytes 196616 | tf_op jit(solution)/shard_map/ppermute | solution.py:51
  204.2 0.7 broadcast_multiply_fusion.1
  204.8 3.1 %collective-permute-done.6 = bf16[32,1024]{1,0:T(8,128)(2,1)S(1)} collective-permute-done((bf16[32,1024]{1,0:T(8,128)(2,1)S(1)}, bf16[32,1024]{1,0:T(8,128)(2,1)S(1)}, u32[]{:S(2)}, u32[]{:S(2)}) %collective-permute-start.6) | collective-permute-done | bytes 65568 | tf_op jit(solution)/shard_map/ppermute | solution.py:51
  207.9 4.9 %collective-permute-start.7 = (bf16[16,1024]{1,0:T(8,128)(2,1)S(1)}, bf16[16,1024]{1,0:T(8,128)(2,1)S(1)}, u32[]{:S(2)}, u32[]{:S(2)}) collective-permute-start(bf16[16,1024]{1,0:T(8,128)(2,1)S(1)} %fusion.37), channel_id=1, source_target_pairs={{0,64},{32,96},{64,0},{96,32},{128,192},{160,224},{192,128},{224,1... | collective-permute-start | bytes 98312 | tf_op jit(solution)/shard_map/ppermute | solution.py:51
  212.9 0.6 broadcast_multiply_fusion
  213.5 3.1 %collective-permute-done.7 = bf16[16,1024]{1,0:T(8,128)(2,1)S(1)} collective-permute-done((bf16[16,1024]{1,0:T(8,128)(2,1)S(1)}, bf16[16,1024]{1,0:T(8,128)(2,1)S(1)}, u32[]{:S(2)}, u32[]{:S(2)}) %collective-permute-start.7) | collective-permute-done | bytes 32800 | tf_op jit(solution)/shard_map/ppermute | solution.py:51
  216.6 0.6 fusion.32
  (69 shorter events, 0.8 us)
Async XLA Ops:
  0.6 53.2 %copy-start = (bf16[4,256,256]{2,1,0:T(8,128)(2,1)S(1)}, bf16[4,256,256]{2,1,0:T(8,128)(2,1)}, u32[]{:S(2)}) copy-start(bf16[4,256,256]{2,1,0:T(8,128)(2,1)} %param.8) | copy-start | bytes 1572868
  3.4 15.9 %copy-start.6 = (bf16[512,256]{1,0:T(8,128)(2,1)S(1)}, bf16[512,256]{1,0:T(8,128)(2,1)}, u32[]{:S(2)}) copy-start(bf16[512,256]{1,0:T(8,128)(2,1)} %param.11) | copy-start | bytes 786436
  3.4 15.9 %copy-start.12 = (bf16[1,1024,256]{2,1,0:T(8,128)(2,1)S(1)}, bf16[1,1024,256]{2,1,0:T(8,128)(2,1)}, u32[]{:S(2)}) copy-start(bf16[1,1024,256]{2,1,0:T(8,128)(2,1)} %param.10) | copy-start | bytes 1572868
  5.0 40.1 %all-to-all-start = ((bf16[128,1,8,512]{3,2,1,0:T(8,128)(2,1)}), bf16[128,1,8,512]{3,2,1,0:T(8,128)(2,1)S(1)}, u32[]{:S(2)}, u32[]{:S(2)}) async-start(bf16[128,1,8,512]{3,2,1,0:T(8,128)(2,1)} %copy.137), calls=%async_computation | async-start | bytes 2097152 | tf_op jit(solution)/shard_map/all_to_all | solution.py:83
  19.3 33.6 %copy-start.14 = (bf16[4,256,256]{2,1,0:T(8,128)(2,1)S(1)}, bf16[4,256,256]{2,1,0:T(8,128)(2,1)}, u32[]{:S(2)}) copy-start(bf16[4,256,256]{2,1,0:T(8,128)(2,1)} %param.9) | copy-start | bytes 1572868
  45.1 33.4 %all-to-all-start.2 = ((bf16[1,128,8,512]{3,2,0,1:T(8,128)(2,1)}), bf16[1,128,8,512]{3,2,0,1:T(8,128)(2,1)}, u32[]{:S(2)}, u32[]{:S(2)}) async-start(bf16[1,128,8,512]{3,2,0,1:T(8,128)(2,1)} %fusion.11), calls=%async_computation.2 | async-start | bytes 2097152 | tf_op jit(solution)/shard_map/all_to_all | solution.py:101
  53.8 2.0 copy-start.15
  78.5 33.6 %all-to-all-start.1 = ((bf16[32,4,8,512]{3,2,1,0:T(8,128)(2,1)}), bf16[32,4,8,512]{3,2,1,0:T(8,128)(2,1)}, u32[]{:S(2)}, u32[]{:S(2)}) async-start(bf16[32,4,8,512]{3,2,1,0:T(8,128)(2,1)} %copy.142), calls=%async_computation.1 | async-start | bytes 2097152 | tf_op jit(solution)/shard_map/all_to_all | solution.py:90
  98.3 3.2 %copy-start.1 = (bf16[4,2,2,2,2,16,512]{6,5,4,3,2,1,0:T(8,128)(2,1)S(1)}, bf16[4,2,2,2,2,16,512]{6,5,4,3,2,1,0:T(8,128)(2,1)}, u32[]{:S(2)}) copy-start(bf16[4,2,2,2,2,16,512]{6,5,4,3,2,1,0:T(8,128)(2,1)} %copy.149) | copy-start | bytes 3145732
  112.1 2.9 %copy-start.8 = (bf16[4,8,16,256]{3,2,1,0:T(8,128)(2,1)S(1)}, bf16[4,8,16,256]{3,2,1,0:T(8,128)(2,1)}, u32[]{:S(2)}) copy-start(bf16[4,8,16,256]{3,2,1,0:T(8,128)(2,1)} %copy.170) | copy-start | bytes 786436
  112.1 2.9 %copy-start.9 = (bf16[4,8,16,256]{3,2,1,0:T(8,128)(2,1)S(1)}, bf16[4,8,16,256]{3,2,1,0:T(8,128)(2,1)}, u32[]{:S(2)}) copy-start(bf16[4,8,16,256]{3,2,1,0:T(8,128)(2,1)} %dynamic-slice_convert_fusion.1) | copy-start | bytes 786436
  113.9 1.0 copy-start.2
  115.9 12.6 %collective-permute-start = (bf16[1536,256]{1,0:T(8,128)(2,1)}, bf16[1536,256]{1,0:T(8,128)(2,1)}, u32[]{:S(2)}, u32[]{:S(2)}) collective-permute-start(bf16[1536,256]{1,0:T(8,128)(2,1)} %pad_maximum_fusion), channel_id=1, source_target_pairs={{0,32},{32,0},{64,96},{96,64},{128,160},{160,128},{192,224},{224,1... | collective-permute-start | bytes 2359304 | tf_op jit(solution)/shard_map/ppermute | solution.py:51
  128.5 1.5 copy-start.3
  128.5 1.6 copy-start.4
  129.9 1.2 copy-start.5
  131.0 12.8 %collective-permute-start.1 = (bf16[768,256]{1,0:T(8,128)(2,1)}, bf16[768,256]{1,0:T(8,128)(2,1)S(1)}, u32[]{:S(2)}, u32[]{:S(2)}) collective-permute-start(bf16[768,256]{1,0:T(8,128)(2,1)} %pad_maximum_fusion.1), channel_id=1, source_target_pairs={{0,128},{32,160},{64,192},{96,224},{128,0},{160,32},{192,64},{224,... | collective-permute-start | bytes 1179656 | tf_op jit(solution)/shard_map/ppermute | solution.py:51
  145.0 5.2 %copy-start.10 = (f32[4,4,16,256]{3,2,0,1:T(8,128)}, f32[4,4,16,256]{3,2,0,1:T(8,128)S(1)}, u32[]{:S(2)}) copy-start(f32[4,4,16,256]{3,2,0,1:T(8,128)S(1)} %copy_add_fusion.1) | copy-start | bytes 786436
  145.0 12.0 %collective-permute-start.2 = (bf16[384,256]{1,0:T(8,128)(2,1)S(1)}, bf16[384,256]{1,0:T(8,128)(2,1)}, u32[]{:S(2)}, u32[]{:S(2)}) collective-permute-start(bf16[384,256]{1,0:T(8,128)(2,1)S(1)} %pad_maximum_fusion.2), channel_id=1, source_target_pairs={{0,256},{32,288},{64,320},{96,352},{128,384},{160,416},{192,448},{... | collective-permute-start | bytes 589832 | tf_op jit(solution)/shard_map/ppermute | solution.py:51
  151.3 6.8 %copy-start.11 = (f32[4,4,16,256]{3,2,0,1:T(8,128)S(1)}, f32[4,4,16,256]{3,2,0,1:T(8,128)}, u32[]{:S(2)}) copy-start(f32[4,4,16,256]{3,2,0,1:T(8,128)} %copy-done.10) | copy-start | bytes 786436
  151.3 12.3 %copy-start.7 = (bf16[512,256]{1,0:T(8,128)(2,1)S(1)}, bf16[512,256]{1,0:T(8,128)(2,1)}, u32[]{:S(2)}) copy-start(bf16[512,256]{1,0:T(8,128)(2,1)} %param.6) | copy-start | bytes 786436
  151.3 35.2 %all-to-all-start.3 = ((bf16[4,32,8,512]{3,2,0,1:T(8,128)(2,1)}), bf16[4,32,8,512]{3,2,0,1:T(8,128)(2,1)S(1)}, u32[]{:S(2)}, u32[]{:S(2)}) async-start(bf16[4,32,8,512]{3,2,0,1:T(8,128)(2,1)} %copy.146), calls=%async_computation.3 | async-start | bytes 2097152 | tf_op jit(solution)/shard_map/all_to_all | solution.py:106
  158.1 0.7 copy-start.17
  158.7 4.8 %copy-start.16 = (f32[2,64,256]{2,1,0:T(8,128)}, f32[2,64,256]{2,1,0:T(8,128)S(1)}, u32[]{:S(2)}) copy-start(f32[2,64,256]{2,1,0:T(8,128)S(1)} %convert_add_fusion.8) | copy-start | bytes 393220
  158.8 19.4 %collective-permute-start.3 = (bf16[192,256]{1,0:T(8,128)(2,1)S(1)}, bf16[192,256]{1,0:T(8,128)(2,1)S(1)}, u32[]{:S(2)}, u32[]{:S(2)}) collective-permute-start(bf16[192,256]{1,0:T(8,128)(2,1)S(1)} %pad_maximum_fusion.3), channel_id=1, source_target_pairs={{0,64},{32,96},{64,0},{96,32},{128,192},{160,224},{192,128},{224,1... | collective-permute-start | bytes 294920 | tf_op jit(solution)/shard_map/ppermute | solution.py:51
  163.7 28.2 %copy-start.13 = (bf16[1,1024,256]{2,1,0:T(8,128)(2,1)S(1)}, bf16[1,1024,256]{2,1,0:T(8,128)(2,1)}, u32[]{:S(2)}) copy-start(bf16[1,1024,256]{2,1,0:T(8,128)(2,1)} %param.10) | copy-start | bytes 1572868
  178.1 0.6 copy-start.18
  187.0 7.3 %collective-permute-start.4 = (bf16[128,1024]{1,0:T(8,128)(2,1)S(1)}, bf16[128,1024]{1,0:T(8,128)(2,1)S(1)}, u32[]{:S(2)}, u32[]{:S(2)}) collective-permute-start(bf16[128,1024]{1,0:T(8,128)(2,1)S(1)} %bitcast.213), channel_id=1, source_target_pairs={{0,32},{32,0},{64,96},{96,64},{128,160},{160,128},{192,224},{224,1... | collective-permute-start | bytes 786440 | tf_op jit(solution)/shard_map/ppermute | solution.py:51
  194.4 6.9 %collective-permute-start.5 = (bf16[64,1024]{1,0:T(8,128)(2,1)S(1)}, bf16[64,1024]{1,0:T(8,128)(2,1)S(1)}, u32[]{:S(2)}, u32[]{:S(2)}) collective-permute-start(bf16[64,1024]{1,0:T(8,128)(2,1)S(1)} %bitcast.220), channel_id=1, source_target_pairs={{0,128},{32,160},{64,192},{96,224},{128,0},{160,32},{192,64},{224,... | collective-permute-start | bytes 393224 | tf_op jit(solution)/shard_map/ppermute | solution.py:51
  201.4 6.5 %collective-permute-start.6 = (bf16[32,1024]{1,0:T(8,128)(2,1)S(1)}, bf16[32,1024]{1,0:T(8,128)(2,1)S(1)}, u32[]{:S(2)}, u32[]{:S(2)}) collective-permute-start(bf16[32,1024]{1,0:T(8,128)(2,1)S(1)} %bitcast.227), channel_id=1, source_target_pairs={{0,256},{32,288},{64,320},{96,352},{128,384},{160,416},{192,448},{... | collective-permute-start | bytes 196616 | tf_op jit(solution)/shard_map/ppermute | solution.py:51
  207.9 8.7 %collective-permute-start.7 = (bf16[16,1024]{1,0:T(8,128)(2,1)S(1)}, bf16[16,1024]{1,0:T(8,128)(2,1)S(1)}, u32[]{:S(2)}, u32[]{:S(2)}) collective-permute-start(bf16[16,1024]{1,0:T(8,128)(2,1)S(1)} %fusion.37), channel_id=1, source_target_pairs={{0,64},{32,96},{64,0},{96,32},{128,192},{160,224},{192,128},{224,1... | collective-permute-start | bytes 98312 | tf_op jit(solution)/shard_map/ppermute | solution.py:51

commit v7 on v4

--- a/solution.py
+++ b/solution.py
@@ -37,23 +37,27 @@
     return jnp.transpose(view, perm).reshape(shape)
 
 
-def dp_reduce_scatter(arrays, replicas):
+def dp_reduce_scatter(wide, narrow, replicas):
     idx = lax.axis_index("dp")
     order = dp_bit_order(replicas)
+    arrays = [wide] + list(narrow)
     size = replicas
     for bit in order:
         half = size // 2
         me = (idx >> bit) & 1
         keeps = [lax.dynamic_slice_in_dim(a, me * half, half, axis=1) for a in arrays]
         sends = [lax.dynamic_slice_in_dim(a, (1 - me) * half, half, axis=1) for a in arrays]
-        packed = jnp.concatenate([s.astype(jnp.bfloat16).reshape(-1, s.shape[-1]) for s in sends], axis=0)
+        sends = [s.astype(jnp.bfloat16) for s in sends]
+        first = sends[0].reshape(-1, sends[0].shape[-1])
+        rest = jnp.concatenate([s.reshape(-1, s.shape[-1]) for s in sends[1:]], axis=0)
         perm = [(i, i ^ (1 << bit)) for i in range(replicas)]
-        got = lax.ppermute(packed, "dp", perm)
-        arrays = []
+        got_first, got_rest = lax.ppermute((first, rest), "dp", perm)
+        arrays = [keeps[0] + got_first.reshape(keeps[0].shape).astype(jnp.float32)]
         offset = 0
-        for k in keeps:
+        for k in keeps[1:]:
             rows = k.size // k.shape[-1]
-            arrays.append(k + got[offset : offset + rows].reshape(k.shape).astype(jnp.float32))
+            part = got_rest[offset : offset + rows].reshape(k.shape)
+            arrays.append(k + part.astype(jnp.float32))
             offset += rows
         size = half
     return [a.reshape(a.shape[:1] + a.shape[2:]) for a in arrays]
@@ -104,14 +108,12 @@
     grad_tokens = jnp.einsum("kjgt,kbjg->tkb", d_up_inner, right_one, preferred_element_type=fp).astype(bf)
     grad_tokens = grad_tokens.reshape(tok_rows, in_blocks * block_width)
 
-    quarters = wide_width // block_width
-    d_up_flat = d_up_inner.reshape(quarters, block_width, tok_rows)
+    d_up_flat = d_up_inner.reshape(all_hid * in_blocks * sub_width, tok_rows)
     tok_sorted = chunk_order(tok_parts[:, 0, :], 1, replicas)
-    tok_wide = jnp.broadcast_to(tok_sorted[None], (quarters,) + tok_sorted.shape)
     mixed_sorted = chunk_order(mixed_piece, 1, replicas)
     hidden_sorted = chunk_order(hidden, 1, replicas)
     down_sorted = chunk_order(mixed_down, 1, replicas)
-    g_right_one = jnp.einsum("qtb,qnt->qbn", tok_wide, d_up_flat, preferred_element_type=fp)
+    g_right_one = jnp.einsum("tb,nt->bn", tok_sorted, d_up_flat, preferred_element_type=fp)
     g_left_one = jnp.einsum("jbt,jct->jbc", mixed_sorted, d_pre, preferred_element_type=fp)
     g_right_two = jnp.einsum(
         "jbt,jkgt->jbkg", hidden_sorted, d_down_inner, preferred_element_type=fp
@@ -119,13 +121,12 @@
     g_left_two = jnp.einsum("kwt,tkc->kwc", down_sorted, cot_parts, preferred_element_type=fp)
 
     def view(g):
-        return g.reshape(g.shape[0], replicas, -1, g.shape[-1])
+        return g.reshape(in_blocks if g.ndim == 2 else g.shape[0], replicas, -1, g.shape[-1])
 
     reduced = dp_reduce_scatter(
-        [view(g_right_one), view(g_left_one), view(g_right_two), view(g_left_two)], replicas
+        view(g_right_one), [view(g_left_one), view(g_right_two), view(g_left_two)], replicas
     )
     grad_right_one, grad_left_one, grad_right_two, grad_left_two = [r * grad_scale for r in reduced]
-    grad_right_one = jnp.transpose(grad_right_one, (1, 0, 2)).reshape(in_blocks, -1, wide_width)
     return (layer_out, grad_tokens, grad_right_one, grad_left_one, grad_right_two, grad_left_two)
 
 

time: 224 us -> 219 us (0.978)
  the two profiles are of different devices: /device:TPU:1 before, /device:TPU:72 now
where the time goes in v7:
time: 219 us; the launch traced here: 218 us
  waiting for transfers between devices  96.5 us (44%)
  starting transfers between devices  62.1 us (28%)
  local copies, waits for them, and re-layouts  42 us (19%)
  matrix products  11.9 us (5%)
  other arithmetic  4.44 us (2%)
    all_to_all x1, waiting for transfers between devices, shards(): lax.all_to_all(first_send, 'tensor', split_axis=0, concat_axis=2, tiled=T...  54.3 us
    ppermute x8, starting transfers between devices, dp_reduce_scatter(): got_first, got_rest = lax.ppermute((first, rest), 'dp', perm)  43.9 us
    all_to_all x1, waiting for transfers between devices, shards(): lax.all_to_all(second_send, 'tensor', split_axis=0, concat_axis=2, tiled=...  32.1 us
    all_to_all x1, starting transfers between devices, shards(): lax.all_to_all(first_send, 'tensor', split_axis=0, concat_axis=2, tiled=T...  13.1 us
    unnamed x40, local copies, waits for them, and re-layouts  12.7 us
    ppermute x8, waiting for transfers between devices, dp_reduce_scatter(): got_first, got_rest = lax.ppermute((first, rest), 'dp', perm)  10.2 us
    all_to_all x1, starting transfers between devices, shards(): lax.all_to_all(second_send, 'tensor', split_axis=0, concat_axis=2, tiled=...  5.13 us
    another operation x1, local copies, waits for them, and re-layouts, view(): g.reshape(in_blocks if g.ndim == 2 else g.shape[0], replicas, -1, g.shape...  4.71 us
  transfers between devices with their start and end apart: 10, of which 4 were waited for; matrix products, arithmetic and copies ran while one was open for 16% of the time, Pallas kernels for 0%

profile of v7, /device:TPU:72, one launch (start us, length us, event | category | flops | bytes accessed | tf_op | source)
XLA Modules:
  0.0 218.2 jit_solution(9135881584257746591)
XLA Ops:
  0.7 1.7 fusion.11
  2.3 0.3 copy.147
  2.7 0.2 copy.145
  2.9 0.4 copy.160
  3.3 0.5 fusion.10
  3.8 0.2 pad_maximum_fusion
  4.0 2.5 %copy.148 = bf16[128,2,1,8,512]{4,3,2,1,0:T(8,128)(2,1)} copy(bf16[128,2,1,8,512]{4,0,3,2,1:T(8,128)(2,1)S(1)} %pad_maximum_fusion) | data formatting | bytes 4194304 | tf_op jit(solution)/shard_map/stack | solution.py:88
  6.5 13.1 %all-to-all-start = ((bf16[128,2,1,8,512]{4,3,2,1,0:T(8,128)(2,1)}), bf16[128,2,1,8,512]{4,3,2,1,0:T(8,128)(2,1)S(1)}, u32[]{:S(2)}, u32[]{:S(2)}) async-start(bf16[128,2,1,8,512]{4,3,2,1,0:T(8,128)(2,1)} %copy.148), calls=%async_computation | async-start | bytes 4194304 | tf_op jit(solution)/shard_map/all_to_all | solution.py:89
  19.6 2.1 copy.152
  21.6 54.3 %all-to-all-done = bf16[128,2,1,8,512]{4,3,2,1,0:T(8,128)(2,1)S(1)} async-done(((bf16[128,2,1,8,512]{4,3,2,1,0:T(8,128)(2,1)}), bf16[128,2,1,8,512]{4,3,2,1,0:T(8,128)(2,1)S(1)}, u32[]{:S(2)}, u32[]{:S(2)}) %all-to-all-start) | async-done | bytes 2097184 | tf_op jit(solution)/shard_map/all_to_all | solution.py:89
  75.9 1.2 copy.195
  77.1 1.2 slice_bitcast_fusion
  78.3 1.1 fusion.7
  79.3 1.2 fusion.5
  80.6 0.4 fusion.13
  81.0 0.3 copy.196
  81.3 0.2 copy-done.2
  81.5 0.4 fusion.12
  82.0 0.2 pad_maximum_fusion.1
  82.2 2.5 %copy.157 = bf16[32,2,4,8,512]{4,3,2,1,0:T(8,128)(2,1)} copy(bf16[32,2,4,8,512]{4,0,3,2,1:T(8,128)(2,1)S(1)} %pad_maximum_fusion.1) | data formatting | bytes 4194304 | tf_op jit(solution)/shard_map/stack | solution.py:101
  84.7 5.1 %all-to-all-start.1 = ((bf16[32,2,4,8,512]{4,3,2,1,0:T(8,128)(2,1)}), bf16[32,2,4,8,512]{4,3,2,1,0:T(8,128)(2,1)}, u32[]{:S(2)}, u32[]{:S(2)}) async-start(bf16[32,2,4,8,512]{4,3,2,1,0:T(8,128)(2,1)} %copy.157), calls=%async_computation.1 | async-start | bytes 4194304 | tf_op jit(solution)/shard_map/all_to_all | solution.py:102
  89.8 0.1 copy.162
  90.0 1.6 copy.150
  91.6 0.1 copy.166
  91.7 0.8 fusion.22
  92.4 4.7 %reshape_reshape.3 = f32[4,16,16,256]{2,1,3,0:T(8,128)} reshape(f32[4,256,32,8]{1,3,2,0:T(8,128)S(1)} %fusion.22) | data formatting | bytes 2097152 | tf_op jit(solution)/shard_map/reshape;reshape | solution.py:124
  97.2 2.5 %constant_dynamic-slice_fusion.1 = bf16[4,8,16,256]{2,1,3,0:T(8,128)(2,1)S(1)} fusion(f32[4,16,16,256]{2,1,3,0:T(8,128)} %reshape_reshape.3, s32[]{:T(128)S(6)} %select_n.17), kind=kLoop, calls=%fused_computation.92 | loop fusion | bytes 524292 | tf_op jit(solution)/shard_map/dynamic_slice | solution.py:49
  99.6 1.8 copy.179
  101.4 1.3 copy.165
  102.7 4.5 %constant_dynamic-slice_fusion = f32[4,8,16,256]{2,1,3,0:T(8,128)} fusion(f32[4,16,16,256]{2,1,3,0:T(8,128)} %reshape_reshape.3, s32[]{:T(128)S(6)} %select_n.16), kind=kLoop, calls=%fused_computation.91 | loop fusion | bytes 1048580 | tf_op jit(solution)/shard_map/dynamic_slice | solution.py:48
  107.2 2.9 %copy.180 = f32[4,8,16,256]{3,2,1,0:T(8,128)S(1)} copy(f32[4,8,16,256]{2,1,3,0:T(8,128)} %constant_dynamic-slice_fusion) | data formatting | bytes 1048576
  110.1 0.5 fusion.49
  110.5 1.0 copy-done.4
  111.5 0.7 dynamic-slice_convert_fusion.1
  112.2 32.1 %all-to-all-done.1 = bf16[32,2,4,8,512]{4,3,2,1,0:T(8,128)(2,1)} async-done(((bf16[32,2,4,8,512]{4,3,2,1,0:T(8,128)(2,1)}), bf16[32,2,4,8,512]{4,3,2,1,0:T(8,128)(2,1)}, u32[]{:S(2)}, u32[]{:S(2)}) %all-to-all-start.1) | async-done | bytes 2097184 | tf_op jit(solution)/shard_map/all_to_all | solution.py:102
  144.3 1.7 copy.158
  146.0 1.1 fusion.44
  147.2 0.1 copy.169
  147.2 0.8 copy-done.9
  148.1 0.4 fusion.28
  148.5 0.9 copy-done.6
  149.5 0.9 pad_maximum_fusion.2
  150.5 1.9 collective-permute-start.4
  152.4 1.5 fusion.16
  153.9 2.7 %copy.178 = bf16[1,1,128,8,512]{2,4,3,1,0:T(8,128)(2,1)} copy(bf16[1,1,128,8,512]{4,3,2,1,0:T(8,128)(2,1)} %get-tuple-element.27) | data formatting | bytes 2097152
  156.6 1.2 dynamic-slice_convert_fusion.2
  157.7 2.4 %collective-permute-start = (bf16[128,1024]{1,0:T(8,128)(2,1)S(1)}, bf16[128,1024]{1,0:T(8,128)(2,1)S(1)}, u32[]{:S(2)}, u32[]{:S(2)}) collective-permute-start(bf16[128,1024]{1,0:T(8,128)(2,1)S(1)} %bitcast.225), channel_id=1, source_target_pairs={{0,32},{32,0},{64,96},{96,64},{128,160},{160,128},{192,224},{224,1... | collective-permute-start | bytes 786440 | tf_op jit(solution)/shard_map/ppermute | solution.py:54
  160.2 2.2 %convolution_convert_fusion.4 = bf16[512,256]{1,0:T(8,128)(2,1)} fusion(bf16[1,1024,256]{2,1,0:T(8,128)(2,1)} %param.10, bf16[1,2,128,8,512]{4,3,2,1,0:T(8,128)(2,1)S(1)} %bitcast.192), kind=kOutput, calls=%fused_computation.25 | convolution fusion | flops 268566528 | bytes 1835008 | tf_op jit(solution)/shard_map/kwt,kwc->tkc/dot_general | solution.py:106
  162.5 3.5 %collective-permute-start.1 = (bf16[64,1024]{1,0:T(8,128)(2,1)S(1)}, bf16[64,1024]{1,0:T(8,128)(2,1)S(1)}, u32[]{:S(2)}, u32[]{:S(2)}) collective-permute-start(bf16[64,1024]{1,0:T(8,128)(2,1)S(1)} %bitcast.232), channel_id=1, source_target_pairs={{0,128},{32,160},{64,192},{96,224},{128,0},{160,32},{192,64},{224,... | collective-permute-start | bytes 393224 | tf_op jit(solution)/shard_map/ppermute | solution.py:54
  166.1 1.2 fusion.45
  167.3 0.1 convert_add_fusion.2
  167.4 0.1 convert_add_fusion.1
  167.6 2.4 %collective-permute-start.5 = (bf16[768,256]{1,0:T(8,128)(2,1)S(1)}, bf16[768,256]{1,0:T(8,128)(2,1)S(1)}, u32[]{:S(2)}, u32[]{:S(2)}) collective-permute-start(bf16[768,256]{1,0:T(8,128)(2,1)S(1)} %pad_maximum_fusion.3), channel_id=1, source_target_pairs={{0,128},{32,160},{64,192},{96,224},{128,0},{160,32},{192,64},{224,... | collective-permute-start | bytes 1179656 | tf_op jit(solution)/shard_map/ppermute | solution.py:54
  170.1 1.2 fusion.14
  171.3 4.9 %collective-permute-start.2 = (bf16[32,1024]{1,0:T(8,128)(2,1)S(1)}, bf16[32,1024]{1,0:T(8,128)(2,1)S(1)}, u32[]{:S(2)}, u32[]{:S(2)}) collective-permute-start(bf16[32,1024]{1,0:T(8,128)(2,1)S(1)} %bitcast.239), channel_id=1, source_target_pairs={{0,256},{32,288},{64,320},{96,352},{128,384},{160,416},{192,448},{... | collective-permute-start | bytes 196616 | tf_op jit(solution)/shard_map/ppermute | solution.py:54
  176.2 4.7 %collective-permute-done.5 = bf16[768,256]{1,0:T(8,128)(2,1)S(1)} collective-permute-done((bf16[768,256]{1,0:T(8,128)(2,1)S(1)}, bf16[768,256]{1,0:T(8,128)(2,1)S(1)}, u32[]{:S(2)}, u32[]{:S(2)}) %collective-permute-start.5) | collective-permute-done | bytes 393248 | tf_op jit(solution)/shard_map/ppermute | solution.py:54
  181.2 4.8 %collective-permute-start.6 = (bf16[384,256]{1,0:T(8,128)(2,1)S(1)}, bf16[384,256]{1,0:T(8,128)(2,1)S(1)}, u32[]{:S(2)}, u32[]{:S(2)}) collective-permute-start(bf16[384,256]{1,0:T(8,128)(2,1)S(1)} %pad_maximum_fusion.4), channel_id=1, source_target_pairs={{0,256},{32,288},{64,320},{96,352},{128,384},{160,416},{192,448},{... | collective-permute-start | bytes 589832 | tf_op jit(solution)/shard_map/ppermute | solution.py:54
  186.1 19.5 %collective-permute-start.3 = (bf16[16,1024]{1,0:T(8,128)(2,1)S(1)}, bf16[16,1024]{1,0:T(8,128)(2,1)S(1)}, u32[]{:S(2)}, u32[]{:S(2)}) collective-permute-start(bf16[16,1024]{1,0:T(8,128)(2,1)S(1)} %fusion.39), channel_id=1, source_target_pairs={{0,64},{32,96},{64,0},{96,32},{128,192},{160,224},{192,128},{224,1... | collective-permute-start | bytes 98312 | tf_op jit(solution)/shard_map/ppermute | solution.py:54
  205.8 4.3 %collective-permute-start.7 = (bf16[192,256]{1,0:T(8,128)(2,1)S(1)}, bf16[192,256]{1,0:T(8,128)(2,1)S(1)}, u32[]{:S(2)}, u32[]{:S(2)}) collective-permute-start(bf16[192,256]{1,0:T(8,128)(2,1)S(1)} %pad_maximum_fusion.5), channel_id=1, source_target_pairs={{0,64},{32,96},{64,0},{96,32},{128,192},{160,224},{192,128},{224,1... | collective-permute-start | bytes 294920 | tf_op jit(solution)/shard_map/ppermute | solution.py:54
  210.2 0.6 fusion.38
  210.8 5.4 %collective-permute-done.7 = bf16[192,256]{1,0:T(8,128)(2,1)S(1)} collective-permute-done((bf16[192,256]{1,0:T(8,128)(2,1)S(1)}, bf16[192,256]{1,0:T(8,128)(2,1)S(1)}, u32[]{:S(2)}, u32[]{:S(2)}) %collective-permute-start.7) | collective-permute-done | bytes 98336 | tf_op jit(solution)/shard_map/ppermute | solution.py:54
  216.2 0.6 fusion.36
  216.9 0.6 fusion.34
  217.5 0.6 fusion.32
  (65 shorter events, 0.8 us)
Async XLA Ops:
  0.6 77.6 %copy-start = (bf16[4,256,256]{2,1,0:T(8,128)(2,1)S(1)}, bf16[4,256,256]{2,1,0:T(8,128)(2,1)}, u32[]{:S(2)}) copy-start(bf16[4,256,256]{2,1,0:T(8,128)(2,1)} %param.8) | copy-start | bytes 1572868
  0.6 2.0 copy-start.15
  2.3 1.0 copy-start.10
  6.5 69.4 %all-to-all-start = ((bf16[128,2,1,8,512]{4,3,2,1,0:T(8,128)(2,1)}), bf16[128,2,1,8,512]{4,3,2,1,0:T(8,128)(2,1)S(1)}, u32[]{:S(2)}, u32[]{:S(2)}) async-start(bf16[128,2,1,8,512]{4,3,2,1,0:T(8,128)(2,1)} %copy.148), calls=%async_computation | async-start | bytes 4194304 | tf_op jit(solution)/shard_map/all_to_all | solution.py:89
  78.3 1.1 copy-start.16
  80.6 1.0 copy-start.2
  84.7 59.6 %all-to-all-start.1 = ((bf16[32,2,4,8,512]{4,3,2,1,0:T(8,128)(2,1)}), bf16[32,2,4,8,512]{4,3,2,1,0:T(8,128)(2,1)}, u32[]{:S(2)}, u32[]{:S(2)}) async-start(bf16[32,2,4,8,512]{4,3,2,1,0:T(8,128)(2,1)} %copy.157), calls=%async_computation.1 | async-start | bytes 4194304 | tf_op jit(solution)/shard_map/all_to_all | solution.py:102
  90.0 1.7 copy-start.14
  107.2 2.9 %copy-start.3 = (bf16[4,256,512]{2,1,0:T(8,128)(2,1)S(1)}, bf16[4,256,512]{2,1,0:T(8,128)(2,1)}, u32[]{:S(2)}) copy-start(bf16[4,256,512]{2,1,0:T(8,128)(2,1)} %copy-done.2) | copy-start | bytes 3145732
  110.5 1.0 copy-start.4
  147.1 0.9 copy-start.9
  147.1 2.4 %copy-start.12 = (bf16[4,8,16,256]{3,2,1,0:T(8,128)(2,1)S(1)}, bf16[4,8,16,256]{3,2,1,0:T(8,128)(2,1)}, u32[]{:S(2)}) copy-start(bf16[4,8,16,256]{3,2,1,0:T(8,128)(2,1)} %copy.179) | copy-start | bytes 786436
  147.1 2.4 %copy-start.13 = (bf16[4,8,16,256]{3,2,1,0:T(8,128)(2,1)S(1)}, bf16[4,8,16,256]{3,2,1,0:T(8,128)(2,1)}, u32[]{:S(2)}) copy-start(bf16[4,8,16,256]{3,2,1,0:T(8,128)(2,1)} %dynamic-slice_convert_fusion.1) | copy-start | bytes 786436
  148.5 1.0 copy-start.6
  150.5 15.6 %collective-permute-start.4 = (bf16[1536,256]{1,0:T(8,128)(2,1)}, bf16[1536,256]{1,0:T(8,128)(2,1)}, u32[]{:S(2)}, u32[]{:S(2)}) collective-permute-start(bf16[1536,256]{1,0:T(8,128)(2,1)} %pad_maximum_fusion.2), channel_id=1, source_target_pairs={{0,32},{32,0},{64,96},{96,64},{128,160},{160,128},{192,224},{224,1... | collective-permute-start | bytes 2359304 | tf_op jit(solution)/shard_map/ppermute | solution.py:54
  156.6 5.8 %copy-start.8 = (f32[1024,256]{0,1:T(8,128)S(1)}, f32[1024,256]{0,1:T(8,128)}, u32[]{:S(2)}) copy-start(f32[1024,256]{0,1:T(8,128)} %fusion.16) | copy-start | bytes 3145732
  157.7 4.6 %collective-permute-start = (bf16[128,1024]{1,0:T(8,128)(2,1)S(1)}, bf16[128,1024]{1,0:T(8,128)(2,1)S(1)}, u32[]{:S(2)}, u32[]{:S(2)}) collective-permute-start(bf16[128,1024]{1,0:T(8,128)(2,1)S(1)} %bitcast.225), channel_id=1, source_target_pairs={{0,32},{32,0},{64,96},{96,64},{128,160},{160,128},{192,224},{224,1... | collective-permute-start | bytes 786440 | tf_op jit(solution)/shard_map/ppermute | solution.py:54
  162.4 4.8 %copy-start.7 = (f32[16,64,256]{2,1,0:T(8,128)S(1)}, f32[16,64,256]{2,1,0:T(8,128)}, u32[]{:S(2)}) copy-start(f32[16,64,256]{2,1,0:T(8,128)} %copy-done.6) | copy-start | bytes 3145732
  162.4 4.9 %copy-start.5 = (f32[4,256,256]{2,1,0:T(8,128)S(1)}, f32[4,256,256]{2,1,0:T(8,128)}, u32[]{:S(2)}) copy-start(f32[4,256,256]{2,1,0:T(8,128)} %copy-done.4) | copy-start | bytes 3145732
  162.5 8.7 %collective-permute-start.1 = (bf16[64,1024]{1,0:T(8,128)(2,1)S(1)}, bf16[64,1024]{1,0:T(8,128)(2,1)S(1)}, u32[]{:S(2)}, u32[]{:S(2)}) collective-permute-start(bf16[64,1024]{1,0:T(8,128)(2,1)S(1)} %bitcast.232), channel_id=1, source_target_pairs={{0,128},{32,160},{64,192},{96,224},{128,0},{160,32},{192,64},{224,... | collective-permute-start | bytes 393224 | tf_op jit(solution)/shard_map/ppermute | solution.py:54
  167.3 2.8 %copy-start.11 = (bf16[1,1,128,8,512]{2,4,3,1,0:T(8,128)(2,1)S(1)}, bf16[1,1,128,8,512]{2,4,3,1,0:T(8,128)(2,1)}, u32[]{:S(2)}) copy-start(bf16[1,1,128,8,512]{2,4,3,1,0:T(8,128)(2,1)} %copy.178) | copy-start | bytes 3145732
  167.6 13.4 %collective-permute-start.5 = (bf16[768,256]{1,0:T(8,128)(2,1)S(1)}, bf16[768,256]{1,0:T(8,128)(2,1)S(1)}, u32[]{:S(2)}, u32[]{:S(2)}) collective-permute-start(bf16[768,256]{1,0:T(8,128)(2,1)S(1)} %pad_maximum_fusion.3), channel_id=1, source_target_pairs={{0,128},{32,160},{64,192},{96,224},{128,0},{160,32},{192,64},{224,... | collective-permute-start | bytes 1179656 | tf_op jit(solution)/shard_map/ppermute | solution.py:54
  171.3 14.7 %collective-permute-start.2 = (bf16[32,1024]{1,0:T(8,128)(2,1)S(1)}, bf16[32,1024]{1,0:T(8,128)(2,1)S(1)}, u32[]{:S(2)}, u32[]{:S(2)}) collective-permute-start(bf16[32,1024]{1,0:T(8,128)(2,1)S(1)} %bitcast.239), channel_id=1, source_target_pairs={{0,256},{32,288},{64,320},{96,352},{128,384},{160,416},{192,448},{... | collective-permute-start | bytes 196616 | tf_op jit(solution)/shard_map/ppermute | solution.py:54
  181.1 37.1 %copy-start.1 = (bf16[4,256,256]{2,1,0:T(8,128)(2,1)S(1)}, bf16[4,256,256]{2,1,0:T(8,128)(2,1)}, u32[]{:S(2)}) copy-start(bf16[4,256,256]{2,1,0:T(8,128)(2,1)} %param.8) | copy-start | bytes 1572868
  181.2 24.4 %collective-permute-start.6 = (bf16[384,256]{1,0:T(8,128)(2,1)S(1)}, bf16[384,256]{1,0:T(8,128)(2,1)S(1)}, u32[]{:S(2)}, u32[]{:S(2)}) collective-permute-start(bf16[384,256]{1,0:T(8,128)(2,1)S(1)} %pad_maximum_fusion.4), channel_id=1, source_target_pairs={{0,256},{32,288},{64,320},{96,352},{128,384},{160,416},{192,448},{... | collective-permute-start | bytes 589832 | tf_op jit(solution)/shard_map/ppermute | solution.py:54
  186.1 24.1 %collective-permute-start.3 = (bf16[16,1024]{1,0:T(8,128)(2,1)S(1)}, bf16[16,1024]{1,0:T(8,128)(2,1)S(1)}, u32[]{:S(2)}, u32[]{:S(2)}) collective-permute-start(bf16[16,1024]{1,0:T(8,128)(2,1)S(1)} %fusion.39), channel_id=1, source_target_pairs={{0,64},{32,96},{64,0},{96,32},{128,192},{160,224},{192,128},{224,1... | collective-permute-start | bytes 98312 | tf_op jit(solution)/shard_map/ppermute | solution.py:54
  205.8 10.4 %collective-permute-start.7 = (bf16[192,256]{1,0:T(8,128)(2,1)S(1)}, bf16[192,256]{1,0:T(8,128)(2,1)S(1)}, u32[]{:S(2)}, u32[]{:S(2)}) collective-permute-start(bf16[192,256]{1,0:T(8,128)(2,1)S(1)} %pad_maximum_fusion.5), channel_id=1, source_target_pairs={{0,64},{32,96},{64,0},{96,32},{128,192},{160,224},{192,128},{224,1... | collective-permute-start | bytes 294920 | tf_op jit(solution)/shard_map/ppermute | solution.py:54

commit v8 on v6

--- a/solution.py
+++ b/solution.py
@@ -2,6 +2,7 @@
 import jax.numpy as jnp
 from jax import lax
 from jax.sharding import PartitionSpec as P
+
 
 half_root = 0.7071067811865476
 inv_root_two_pi = 0.3989422804014327
@@ -37,11 +38,12 @@
     return jnp.transpose(view, perm).reshape(shape)
 
 
-def dp_reduce_scatter(arrays, replicas):
+def dp_reduce_scatter(arrays, replicas, first=0, last=None):
     idx = lax.axis_index("dp")
     order = dp_bit_order(replicas)
-    size = replicas
-    for bit in order:
+    last = len(order) if last is None else last
+    size = replicas >> first
+    for bit in order[first:last]:
         half = size // 2
         me = (idx >> bit) & 1
         keeps = [lax.dynamic_slice_in_dim(a, me * half, half, axis=1) for a in arrays]
@@ -56,10 +58,10 @@
             arrays.append(k + got[offset : offset + rows].reshape(k.shape).astype(jnp.float32))
             offset += rows
         size = half
-    return [a.reshape(a.shape[:1] + a.shape[2:]) for a in arrays]
+    return arrays
 
 
-def shards(tokens, first_right, first_left, second_right, second_left, cotangent):
+def layer(tokens, first_right, first_left, second_right, second_left, cotangent):
     fp = jnp.float32
     bf = jnp.bfloat16
     tok_rows = tokens.shape[0]
@@ -116,9 +118,11 @@
     def view(g):
         return g.reshape(in_blocks if g.ndim == 2 else g.shape[0], replicas, -1, g.shape[-1])
 
-    early = dp_reduce_scatter([view(g_left_two), view(g_left_one), view(g_right_two)], replicas)
+    early_stages = 2
+    early = dp_reduce_scatter(
+        [view(g_left_two), view(g_left_one), view(g_right_two)], replicas, 0, early_stages
+    )
     d_up_inner, *early = lax.optimization_barrier((d_up_inner, *early))
-    red_left_two, red_left_one, red_right_two = early
 
     grad_tokens = jnp.einsum(
         "jkgt,kbjg->tkb", d_up_inner, right_one, preferred_element_type=fp
@@ -127,7 +131,14 @@
     d_up_flat = d_up_inner.reshape(all_hid * in_blocks * sub_width, tok_rows)
     tok_sorted = chunk_order(tok_parts[:, 0, :], 1, replicas)
     g_right_one = jnp.einsum("tb,nt->bn", tok_sorted, d_up_flat, preferred_element_type=fp)
-    (red_right_one,) = dp_reduce_scatter([view(g_right_one)], replicas)
+    late = [view(g_right_one)]
+    stages = len(dp_bit_order(replicas))
+    for stage in range(stages):
+        late = dp_reduce_scatter(late, replicas, stage, stage + 1)
+        if early_stages + stage < stages:
+            early = dp_reduce_scatter(early, replicas, early_stages + stage, early_stages + stage + 1)
+    red_right_one = late[0][:, 0]
+    red_left_two, red_left_one, red_right_two = [e[:, 0] for e in early]
     reduced = (red_right_one, red_left_one, red_right_two, red_left_two)
     grad_right_one, grad_left_one, grad_right_two, grad_left_two = [r * grad_scale for r in reduced]
     return (layer_out, grad_tokens, grad_right_one, grad_left_one, grad_right_two, grad_left_two)
@@ -150,4 +161,4 @@
         P("tensor", "dp", None),
         P("tensor", "dp", None),
     )
-    return jax.shard_map(shards, mesh=mesh, in_specs=in_specs, out_specs=out_specs, check_vma=False)
+    return jax.shard_map(layer, mesh=mesh, in_specs=in_specs, out_specs=out_specs, check_vma=False)

time: 221 us -> 208 us (0.941)
  the two profiles are of different devices: /device:TPU:1 before, /device:TPU:76 now
where the time goes in v8:
time: 208 us; the launch traced here: 206 us
  waiting for transfers between devices  91.7 us (44%)
  starting transfers between devices  54.5 us (26%)
  local copies, waits for them, and re-layouts  34 us (16%)
  matrix products  16.9 us (8%)
  other arithmetic  8.17 us (4%)
    all_to_all x1, waiting for transfers between devices, layer(): lax.all_to_all(up_inner, 'tensor', split_axis=0, concat_axis=1, tiled=True)  26.6 us
    ppermute x8, starting transfers between devices, dp_reduce_scatter(): got = lax.ppermute(packed, 'dp', perm)  25.2 us
    ppermute x8, waiting for transfers between devices, dp_reduce_scatter(): got = lax.ppermute(packed, 'dp', perm)  23.1 us
    all_to_all x1, waiting for transfers between devices, layer(): lax.all_to_all(d_mixed_down, 'tensor', split_axis=1, concat_axis=0, tiled...  23 us
    all_to_all x1, starting transfers between devices, layer(): lax.all_to_all(up_inner, 'tensor', split_axis=0, concat_axis=1, tiled=True)  13.1 us
    all_to_all x1, waiting for transfers between devices, layer(): lax.all_to_all(down_inner, 'tensor', split_axis=0, concat_axis=1, tiled=T...  11.6 us
    unnamed x39, local copies, waits for them, and re-layouts  9.3 us
    all_to_all x1, waiting for transfers between devices, layer(): lax.all_to_all(d_mixed_up, 'tensor', split_axis=1, concat_axis=0, tiled=T...  7.32 us
  transfers between devices with their start and end apart: 12, of which 9 were waited for; matrix products, arithmetic and copies ran while one was open for 22% of the time, Pallas kernels for 0%

profile of v8, /device:TPU:76, one launch (start us, length us, event | category | flops | bytes accessed | tf_op | source)
XLA Modules:
  0.0 206.4 jit_solution(5180590669145996256)
XLA Ops:
  0.6 1.3 copy.135
  2.0 1.4 fusion.10
  3.4 1.6 copy.137
  5.0 13.1 %all-to-all-start = ((bf16[128,1,8,512]{3,2,1,0:T(8,128)(2,1)}), bf16[128,1,8,512]{3,2,1,0:T(8,128)(2,1)S(1)}, u32[]{:S(2)}, u32[]{:S(2)}) async-start(bf16[128,1,8,512]{3,2,1,0:T(8,128)(2,1)} %copy.137), calls=%async_computation | async-start | bytes 2097152 | tf_op jit(solution)/shard_map/all_to_all | solution.py:85
  18.1 1.4 fusion.11
  19.5 26.6 %all-to-all-done = bf16[128,1,8,512]{3,2,1,0:T(8,128)(2,1)S(1)} async-done(((bf16[128,1,8,512]{3,2,1,0:T(8,128)(2,1)}), bf16[128,1,8,512]{3,2,1,0:T(8,128)(2,1)S(1)}, u32[]{:S(2)}, u32[]{:S(2)}) %all-to-all-start) | async-done | bytes 1048608 | tf_op jit(solution)/shard_map/all_to_all | solution.py:85
  46.1 5.4 %all-to-all-start.2 = ((bf16[1,128,8,512]{3,2,0,1:T(8,128)(2,1)}), bf16[1,128,8,512]{3,2,0,1:T(8,128)(2,1)}, u32[]{:S(2)}, u32[]{:S(2)}) async-start(bf16[1,128,8,512]{3,2,0,1:T(8,128)(2,1)} %fusion.11), calls=%async_computation.2 | async-start | bytes 2097152 | tf_op jit(solution)/shard_map/all_to_all | solution.py:103
  51.5 1.0 copy.140
  52.5 2.0 fusion.7
  54.5 0.4 fusion.12
  54.9 1.6 copy.142
  56.5 23.0 %all-to-all-done.2 = bf16[1,128,8,512]{3,2,0,1:T(8,128)(2,1)} async-done(((bf16[1,128,8,512]{3,2,0,1:T(8,128)(2,1)}), bf16[1,128,8,512]{3,2,0,1:T(8,128)(2,1)}, u32[]{:S(2)}, u32[]{:S(2)}) %all-to-all-start.2) | async-done | bytes 1048608 | tf_op jit(solution)/shard_map/all_to_all | solution.py:103
  79.5 5.6 %all-to-all-start.1 = ((bf16[32,4,8,512]{3,2,1,0:T(8,128)(2,1)}), bf16[32,4,8,512]{3,2,1,0:T(8,128)(2,1)}, u32[]{:S(2)}, u32[]{:S(2)}) async-start(bf16[32,4,8,512]{3,2,1,0:T(8,128)(2,1)} %copy.142), calls=%async_computation.1 | async-start | bytes 2097152 | tf_op jit(solution)/shard_map/all_to_all | solution.py:92
  85.1 0.1 copy.138
  85.2 1.1 copy.149
  86.4 1.7 fusion.19
  88.1 4.7 %reshape_reshape.11 = f32[4,16,16,256]{2,1,3,0:T(8,128)} reshape(f32[4,256,32,8]{1,3,2,0:T(8,128)S(1)} %fusion.19) | data formatting | bytes 2097152 | tf_op jit(solution)/shard_map/reshape;reshape | solution.py:119
  92.8 2.5 %constant_dynamic-slice_fusion.1 = bf16[4,8,16,256]{2,1,3,0:T(8,128)(2,1)S(1)} fusion(f32[4,16,16,256]{2,1,3,0:T(8,128)} %reshape_reshape.11, s32[]{:T(128)S(6)} %select_n.17), kind=kLoop, calls=%fused_computation.88 | loop fusion | bytes 524292 | tf_op jit(solution)/shard_map/dynamic_slice | solution.py:50
  95.3 1.8 copy.165
  97.1 3.2 %fusion.5 = bf16[4,256,512]{2,1,0:T(8,128)(2,1)S(1)} fusion(f32[4,512,256]{1,2,0:T(8,128)} %get-tuple-element.44, bf16[32,4,8,512]{3,2,1,0:T(8,128)(2,1)} %bitcast.15, bf16[4,256,256]{1,2,0:T(8,128)(2,1)} %copy.140), kind=kOutput, calls=%fused_computation.6 | convolution fusion | flops 273678336 | bytes 4718592 | tf_op jit(solution)/shard_map/kjgt,jbkg->jbt/dot_general | solution.py:104
  100.3 0.5 fusion.48
  100.8 0.7 dynamic-slice_convert_fusion.1
  101.5 11.6 %all-to-all-done.1 = bf16[32,4,8,512]{3,2,1,0:T(8,128)(2,1)} async-done(((bf16[32,4,8,512]{3,2,1,0:T(8,128)(2,1)}), bf16[32,4,8,512]{3,2,1,0:T(8,128)(2,1)}, u32[]{:S(2)}, u32[]{:S(2)}) %all-to-all-start.1) | async-done | bytes 1048608 | tf_op jit(solution)/shard_map/all_to_all | solution.py:92
  113.2 1.4 copy.147
  114.5 1.4 fusion.29
  116.0 1.1 dynamic-slice_convert_fusion.2
  117.1 1.0 pad_maximum_fusion
  118.0 1.9 collective-permute-start
  119.9 4.5 %constant_dynamic-slice_fusion = f32[4,8,16,256]{2,1,3,0:T(8,128)} fusion(f32[4,16,16,256]{2,1,3,0:T(8,128)} %reshape_reshape.11, s32[]{:T(128)S(6)} %select_n.16), kind=kLoop, calls=%fused_computation.87 | loop fusion | bytes 1048580 | tf_op jit(solution)/shard_map/dynamic_slice | solution.py:49
  124.4 3.5 %copy.166 = f32[4,8,16,256]{3,2,1,0:T(8,128)} copy(f32[4,8,16,256]{2,1,3,0:T(8,128)} %constant_dynamic-slice_fusion) | data formatting | bytes 1048576
  127.9 0.4 fusion.13
  128.4 1.1 copy.146
  129.5 5.3 %all-to-all-start.3 = ((bf16[4,32,8,512]{3,2,0,1:T(8,128)(2,1)}), bf16[4,32,8,512]{3,2,0,1:T(8,128)(2,1)S(1)}, u32[]{:S(2)}, u32[]{:S(2)}) async-start(bf16[4,32,8,512]{3,2,0,1:T(8,128)(2,1)} %copy.146), calls=%async_computation.3 | async-start | bytes 2097152 | tf_op jit(solution)/shard_map/all_to_all | solution.py:108
  134.8 1.2 fusion.44
  136.1 1.1 convert_add_fusion.3
  137.4 0.7 copy-done.5
  138.1 0.8 copy-done.7
  138.9 0.8 pad_maximum_fusion.1
  139.7 3.3 %collective-permute-start.1 = (bf16[768,256]{1,0:T(8,128)(2,1)}, bf16[768,256]{1,0:T(8,128)(2,1)}, u32[]{:S(2)}, u32[]{:S(2)}) collective-permute-start(bf16[768,256]{1,0:T(8,128)(2,1)} %pad_maximum_fusion.1), channel_id=1, source_target_pairs={{0,128},{32,160},{64,192},{96,224},{128,0},{160,32},{192,64},{224,... | collective-permute-start | bytes 1179656 | tf_op jit(solution)/shard_map/ppermute | solution.py:53
  143.0 0.1 copy.155
  143.2 2.6 %convolution_convert_fusion.4 = bf16[512,256]{1,0:T(8,128)(2,1)} fusion(bf16[1024,512]{1,0:T(8,128)(2,1)} %bitcast.11, bf16[1,1024,256]{2,1,0:T(8,128)(2,1)} %param.10), kind=kOutput, calls=%fused_computation.23 | convolution fusion | flops 268566528 | bytes 1835008 | tf_op jit(solution)/shard_map/kwt,kwc->tkc/dot_general | solution.py:94
  145.8 7.0 %collective-permute-done.1 = bf16[768,256]{1,0:T(8,128)(2,1)} collective-permute-done((bf16[768,256]{1,0:T(8,128)(2,1)}, bf16[768,256]{1,0:T(8,128)(2,1)}, u32[]{:S(2)}, u32[]{:S(2)}) %collective-permute-start.1) | collective-permute-done | bytes 393248 | tf_op jit(solution)/shard_map/ppermute | solution.py:53
  152.8 1.1 fusion.45
  153.9 1.7 convert_add_fusion.5
  155.6 0.7 convert_add_fusion.6
  156.4 7.3 %all-to-all-done.3 = bf16[4,32,8,512]{3,2,0,1:T(8,128)(2,1)S(1)} async-done(((bf16[4,32,8,512]{3,2,0,1:T(8,128)(2,1)}), bf16[4,32,8,512]{3,2,0,1:T(8,128)(2,1)S(1)}, u32[]{:S(2)}, u32[]{:S(2)}) %all-to-all-start.3) | async-done | bytes 1048608 | tf_op jit(solution)/shard_map/all_to_all | solution.py:108
  163.7 0.9 dynamic-slice_convert_fusion.8
  164.6 0.9 dynamic-slice_convert_fusion.7
  165.6 2.4 %collective-permute-start.6 = (bf16[384,256]{1,0:T(8,128)(2,1)S(1)}, bf16[384,256]{1,0:T(8,128)(2,1)S(1)}, u32[]{:S(2)}, u32[]{:S(2)}) collective-permute-start(bf16[384,256]{1,0:T(8,128)(2,1)S(1)} %pad_maximum_fusion.2), channel_id=1, source_target_pairs={{0,256},{32,288},{64,320},{96,352},{128,384},{160,416},{192,448},{... | collective-permute-start | bytes 589832 | tf_op jit(solution)/shard_map/ppermute | solution.py:53
  168.0 1.2 fusion.14
  169.2 0.5 fusion.16
  169.8 1.9 collective-permute-start.2
  171.7 2.9 %collective-permute-done.6 = bf16[384,256]{1,0:T(8,128)(2,1)S(1)} collective-permute-done((bf16[384,256]{1,0:T(8,128)(2,1)S(1)}, bf16[384,256]{1,0:T(8,128)(2,1)S(1)}, u32[]{:S(2)}, u32[]{:S(2)}) %collective-permute-start.6) | collective-permute-done | bytes 196640 | tf_op jit(solution)/shard_map/ppermute | solution.py:53
  174.8 4.9 %collective-permute-start.7 = (bf16[192,256]{1,0:T(8,128)(2,1)S(1)}, bf16[192,256]{1,0:T(8,128)(2,1)S(1)}, u32[]{:S(2)}, u32[]{:S(2)}) collective-permute-start(bf16[192,256]{1,0:T(8,128)(2,1)S(1)} %pad_maximum_fusion.3), channel_id=1, source_target_pairs={{0,64},{32,96},{64,0},{96,32},{128,192},{160,224},{192,128},{224,1... | collective-permute-start | bytes 294920 | tf_op jit(solution)/shard_map/ppermute | solution.py:53
  179.9 3.1 %collective-permute-start.3 = (bf16[64,1024]{1,0:T(8,128)(2,1)S(1)}, bf16[64,1024]{1,0:T(8,128)(2,1)S(1)}, u32[]{:S(2)}, u32[]{:S(2)}) collective-permute-start(bf16[64,1024]{1,0:T(8,128)(2,1)S(1)} %bitcast.220), channel_id=1, source_target_pairs={{0,128},{32,160},{64,192},{96,224},{128,0},{160,32},{192,64},{224,... | collective-permute-start | bytes 393224 | tf_op jit(solution)/shard_map/ppermute | solution.py:53
  183.0 4.3 %collective-permute-done.7 = bf16[192,256]{1,0:T(8,128)(2,1)S(1)} collective-permute-done((bf16[192,256]{1,0:T(8,128)(2,1)S(1)}, bf16[192,256]{1,0:T(8,128)(2,1)S(1)}, u32[]{:S(2)}, u32[]{:S(2)}) %collective-permute-start.7) | collective-permute-done | bytes 98336 | tf_op jit(solution)/shard_map/ppermute | solution.py:53
  187.3 0.6 fusion.35
  188.0 2.6 %collective-permute-start.4 = (bf16[32,1024]{1,0:T(8,128)(2,1)S(1)}, bf16[32,1024]{1,0:T(8,128)(2,1)S(1)}, u32[]{:S(2)}, u32[]{:S(2)}) collective-permute-start(bf16[32,1024]{1,0:T(8,128)(2,1)S(1)} %bitcast.227), channel_id=1, source_target_pairs={{0,256},{32,288},{64,320},{96,352},{128,384},{160,416},{192,448},{... | collective-permute-start | bytes 196616 | tf_op jit(solution)/shard_map/ppermute | solution.py:53
  190.6 0.6 fusion.37
  191.3 4.4 %collective-permute-done.4 = bf16[32,1024]{1,0:T(8,128)(2,1)S(1)} collective-permute-done((bf16[32,1024]{1,0:T(8,128)(2,1)S(1)}, bf16[32,1024]{1,0:T(8,128)(2,1)S(1)}, u32[]{:S(2)}, u32[]{:S(2)}) %collective-permute-start.4) | collective-permute-done | bytes 65568 | tf_op jit(solution)/shard_map/ppermute | solution.py:53
  195.7 5.0 %collective-permute-start.5 = (bf16[16,1024]{1,0:T(8,128)(2,1)S(1)}, bf16[16,1024]{1,0:T(8,128)(2,1)S(1)}, u32[]{:S(2)}, u32[]{:S(2)}) collective-permute-start(bf16[16,1024]{1,0:T(8,128)(2,1)S(1)} %fusion.40), channel_id=1, source_target_pairs={{0,64},{32,96},{64,0},{96,32},{128,192},{160,224},{192,128},{224,1... | collective-permute-start | bytes 98312 | tf_op jit(solution)/shard_map/ppermute | solution.py:53
  200.7 0.6 fusion.33
  201.3 4.5 %collective-permute-done.5 = bf16[16,1024]{1,0:T(8,128)(2,1)S(1)} collective-permute-done((bf16[16,1024]{1,0:T(8,128)(2,1)S(1)}, bf16[16,1024]{1,0:T(8,128)(2,1)S(1)}, u32[]{:S(2)}, u32[]{:S(2)}) %collective-permute-start.5) | collective-permute-done | bytes 32800 | tf_op jit(solution)/shard_map/ppermute | solution.py:53
  205.8 0.6 fusion.39
  (60 shorter events, 0.7 us)
Async XLA Ops:
  0.6 51.9 %copy-start = (bf16[4,256,256]{2,1,0:T(8,128)(2,1)S(1)}, bf16[4,256,256]{2,1,0:T(8,128)(2,1)}, u32[]{:S(2)}) copy-start(bf16[4,256,256]{2,1,0:T(8,128)(2,1)} %param.8) | copy-start | bytes 1572868
  3.4 14.7 %copy-start.8 = (bf16[512,256]{1,0:T(8,128)(2,1)S(1)}, bf16[512,256]{1,0:T(8,128)(2,1)}, u32[]{:S(2)}) copy-start(bf16[512,256]{1,0:T(8,128)(2,1)} %param.11) | copy-start | bytes 786436
  3.4 14.6 %copy-start.14 = (bf16[1,1024,256]{2,1,0:T(8,128)(2,1)S(1)}, bf16[1,1024,256]{2,1,0:T(8,128)(2,1)}, u32[]{:S(2)}) copy-start(bf16[1,1024,256]{2,1,0:T(8,128)(2,1)} %param.10) | copy-start | bytes 1572868
  5.0 41.1 %all-to-all-start = ((bf16[128,1,8,512]{3,2,1,0:T(8,128)(2,1)}), bf16[128,1,8,512]{3,2,1,0:T(8,128)(2,1)S(1)}, u32[]{:S(2)}, u32[]{:S(2)}) async-start(bf16[128,1,8,512]{3,2,1,0:T(8,128)(2,1)} %copy.137), calls=%async_computation | async-start | bytes 2097152 | tf_op jit(solution)/shard_map/all_to_all | solution.py:85
  18.0 33.4 %copy-start.15 = (bf16[4,256,256]{2,1,0:T(8,128)(2,1)S(1)}, bf16[4,256,256]{2,1,0:T(8,128)(2,1)}, u32[]{:S(2)}) copy-start(bf16[4,256,256]{2,1,0:T(8,128)(2,1)} %param.9) | copy-start | bytes 1572868
  46.1 33.5 %all-to-all-start.2 = ((bf16[1,128,8,512]{3,2,0,1:T(8,128)(2,1)}), bf16[1,128,8,512]{3,2,0,1:T(8,128)(2,1)}, u32[]{:S(2)}, u32[]{:S(2)}) async-start(bf16[1,128,8,512]{3,2,0,1:T(8,128)(2,1)} %fusion.11), calls=%async_computation.2 | async-start | bytes 2097152 | tf_op jit(solution)/shard_map/all_to_all | solution.py:103
  52.5 2.0 copy-start.16
  79.5 33.6 %all-to-all-start.1 = ((bf16[32,4,8,512]{3,2,1,0:T(8,128)(2,1)}), bf16[32,4,8,512]{3,2,1,0:T(8,128)(2,1)}, u32[]{:S(2)}, u32[]{:S(2)}) async-start(bf16[32,4,8,512]{3,2,1,0:T(8,128)(2,1)} %copy.142), calls=%async_computation.1 | async-start | bytes 2097152 | tf_op jit(solution)/shard_map/all_to_all | solution.py:92
  97.0 3.2 %copy-start.1 = (bf16[4,2,2,2,2,16,512]{6,5,4,3,2,1,0:T(8,128)(2,1)S(1)}, bf16[4,2,2,2,2,16,512]{6,5,4,3,2,1,0:T(8,128)(2,1)}, u32[]{:S(2)}) copy-start(bf16[4,2,2,2,2,16,512]{6,5,4,3,2,1,0:T(8,128)(2,1)} %copy.149) | copy-start | bytes 3145732
  113.2 3.9 %copy-start.10 = (bf16[4,8,16,256]{3,2,1,0:T(8,128)(2,1)S(1)}, bf16[4,8,16,256]{3,2,1,0:T(8,128)(2,1)}, u32[]{:S(2)}) copy-start(bf16[4,8,16,256]{3,2,1,0:T(8,128)(2,1)} %copy.165) | copy-start | bytes 786436
  113.2 3.9 %copy-start.11 = (bf16[4,8,16,256]{3,2,1,0:T(8,128)(2,1)S(1)}, bf16[4,8,16,256]{3,2,1,0:T(8,128)(2,1)}, u32[]{:S(2)}) copy-start(bf16[4,8,16,256]{3,2,1,0:T(8,128)(2,1)} %dynamic-slice_convert_fusion.1) | copy-start | bytes 786436
  118.0 16.8 %collective-permute-start = (bf16[1536,256]{1,0:T(8,128)(2,1)}, bf16[1536,256]{1,0:T(8,128)(2,1)}, u32[]{:S(2)}, u32[]{:S(2)}) collective-permute-start(bf16[1536,256]{1,0:T(8,128)(2,1)} %pad_maximum_fusion), channel_id=1, source_target_pairs={{0,32},{32,0},{64,96},{96,64},{128,160},{160,128},{192,224},{224,1... | collective-permute-start | bytes 2359304 | tf_op jit(solution)/shard_map/ppermute | solution.py:53
  129.5 34.2 %all-to-all-start.3 = ((bf16[4,32,8,512]{3,2,0,1:T(8,128)(2,1)}), bf16[4,32,8,512]{3,2,0,1:T(8,128)(2,1)S(1)}, u32[]{:S(2)}, u32[]{:S(2)}) async-start(bf16[4,32,8,512]{3,2,0,1:T(8,128)(2,1)} %copy.146), calls=%async_computation.3 | async-start | bytes 2097152 | tf_op jit(solution)/shard_map/all_to_all | solution.py:108
  134.8 2.5 %copy-start.2 = (f32[4,8,16,256]{3,2,1,0:T(8,128)S(1)}, f32[4,8,16,256]{3,2,1,0:T(8,128)}, u32[]{:S(2)}) copy-start(f32[4,8,16,256]{3,2,1,0:T(8,128)} %copy.166) | copy-start | bytes 1572868
  137.2 2.5 %copy-start.3 = (f32[8,64,256]{2,1,0:T(8,128)}, f32[8,64,256]{2,1,0:T(8,128)S(1)}, u32[]{:S(2)}) copy-start(f32[8,64,256]{2,1,0:T(8,128)S(1)} %convert_add_fusion.3) | copy-start | bytes 1572868
  137.2 5.8 %copy-start.9 = (bf16[512,256]{1,0:T(8,128)(2,1)S(1)}, bf16[512,256]{1,0:T(8,128)(2,1)}, u32[]{:S(2)}) copy-start(bf16[512,256]{1,0:T(8,128)(2,1)} %param.6) | copy-start | bytes 786436
  137.3 0.8 copy-start.5
  138.1 0.8 copy-start.7
  139.7 13.2 %collective-permute-start.1 = (bf16[768,256]{1,0:T(8,128)(2,1)}, bf16[768,256]{1,0:T(8,128)(2,1)}, u32[]{:S(2)}, u32[]{:S(2)}) collective-permute-start(bf16[768,256]{1,0:T(8,128)(2,1)} %pad_maximum_fusion.1), channel_id=1, source_target_pairs={{0,128},{32,160},{64,192},{96,224},{128,0},{160,32},{192,64},{224,... | collective-permute-start | bytes 1179656 | tf_op jit(solution)/shard_map/ppermute | solution.py:53
  143.1 12.5 %copy-start.6 = (f32[4,8,16,256]{3,2,1,0:T(8,128)S(1)}, f32[4,8,16,256]{3,2,1,0:T(8,128)}, u32[]{:S(2)}) copy-start(f32[4,8,16,256]{3,2,1,0:T(8,128)} %copy-done.5) | copy-start | bytes 1572868
  143.2 13.2 %copy-start.4 = (f32[8,64,256]{2,1,0:T(8,128)S(1)}, f32[8,64,256]{2,1,0:T(8,128)}, u32[]{:S(2)}) copy-start(f32[8,64,256]{2,1,0:T(8,128)} %copy-done.3) | copy-start | bytes 1572868
  165.6 9.1 %collective-permute-start.6 = (bf16[384,256]{1,0:T(8,128)(2,1)S(1)}, bf16[384,256]{1,0:T(8,128)(2,1)S(1)}, u32[]{:S(2)}, u32[]{:S(2)}) collective-permute-start(bf16[384,256]{1,0:T(8,128)(2,1)S(1)} %pad_maximum_fusion.2), channel_id=1, source_target_pairs={{0,256},{32,288},{64,320},{96,352},{128,384},{160,416},{192,448},{... | collective-permute-start | bytes 589832 | tf_op jit(solution)/shard_map/ppermute | solution.py:53
  169.2 5.4 %copy-start.13 = (f32[4,4,16,256]{3,2,1,0:T(8,128)S(1)}, f32[4,4,16,256]{3,2,1,0:T(8,128)}, u32[]{:S(2)}) copy-start(f32[4,4,16,256]{3,2,1,0:T(8,128)} %convert_add_fusion.6) | copy-start | bytes 786436
  169.2 5.5 %copy-start.12 = (f32[4,4,16,256]{3,2,1,0:T(8,128)S(1)}, f32[4,4,16,256]{3,2,1,0:T(8,128)}, u32[]{:S(2)}) copy-start(f32[4,4,16,256]{3,2,1,0:T(8,128)} %convert_add_fusion.5) | copy-start | bytes 786436
  169.8 10.0 %collective-permute-start.2 = (bf16[128,1024]{1,0:T(8,128)(2,1)S(1)}, bf16[128,1024]{1,0:T(8,128)(2,1)S(1)}, u32[]{:S(2)}, u32[]{:S(2)}) collective-permute-start(bf16[128,1024]{1,0:T(8,128)(2,1)S(1)} %bitcast.213), channel_id=1, source_target_pairs={{0,32},{32,0},{64,96},{96,64},{128,160},{160,128},{192,224},{224,1... | collective-permute-start | bytes 786440 | tf_op jit(solution)/shard_map/ppermute | solution.py:53
  174.8 12.5 %collective-permute-start.7 = (bf16[192,256]{1,0:T(8,128)(2,1)S(1)}, bf16[192,256]{1,0:T(8,128)(2,1)S(1)}, u32[]{:S(2)}, u32[]{:S(2)}) collective-permute-start(bf16[192,256]{1,0:T(8,128)(2,1)S(1)} %pad_maximum_fusion.3), channel_id=1, source_target_pairs={{0,64},{32,96},{64,0},{96,32},{128,192},{160,224},{192,128},{224,1... | collective-permute-start | bytes 294920 | tf_op jit(solution)/shard_map/ppermute | solution.py:53
  179.9 8.0 %collective-permute-start.3 = (bf16[64,1024]{1,0:T(8,128)(2,1)S(1)}, bf16[64,1024]{1,0:T(8,128)(2,1)S(1)}, u32[]{:S(2)}, u32[]{:S(2)}) collective-permute-start(bf16[64,1024]{1,0:T(8,128)(2,1)S(1)} %bitcast.220), channel_id=1, source_target_pairs={{0,128},{32,160},{64,192},{96,224},{128,0},{160,32},{192,64},{224,... | collective-permute-start | bytes 393224 | tf_op jit(solution)/shard_map/ppermute | solution.py:53
  188.0 7.7 %collective-permute-start.4 = (bf16[32,1024]{1,0:T(8,128)(2,1)S(1)}, bf16[32,1024]{1,0:T(8,128)(2,1)S(1)}, u32[]{:S(2)}, u32[]{:S(2)}) collective-permute-start(bf16[32,1024]{1,0:T(8,128)(2,1)S(1)} %bitcast.227), channel_id=1, source_target_pairs={{0,256},{32,288},{64,320},{96,352},{128,384},{160,416},{192,448},{... | collective-permute-start | bytes 196616 | tf_op jit(solution)/shard_map/ppermute | solution.py:53
  195.7 10.1 %collective-permute-start.5 = (bf16[16,1024]{1,0:T(8,128)(2,1)S(1)}, bf16[16,1024]{1,0:T(8,128)(2,1)S(1)}, u32[]{:S(2)}, u32[]{:S(2)}) collective-permute-start(bf16[16,1024]{1,0:T(8,128)(2,1)S(1)} %fusion.40), channel_id=1, source_target_pairs={{0,64},{32,96},{64,0},{96,32},{128,192},{160,224},{192,128},{224,1... | collective-permute-start | bytes 98312 | tf_op jit(solution)/shard_map/ppermute | solution.py:53

commit v9 on v8

--- a/solution.py
+++ b/solution.py
@@ -101,6 +101,15 @@
     ).astype(bf)
     d_mixed_down = d_mixed_down.reshape(in_blocks, all_hid, sub_width, tok_rows)
     d_down_inner = lax.all_to_all(d_mixed_down, "tensor", split_axis=1, concat_axis=0, tiled=True)
+
+    def view(g):
+        return g.reshape(in_blocks if g.ndim == 2 else g.shape[0], replicas, -1, g.shape[-1])
+
+    down_sorted = chunk_order(mixed_down, 1, replicas)
+    g_left_two = jnp.einsum("kwt,tkc->kwc", down_sorted, cot_parts, preferred_element_type=fp)
+    (mid,) = dp_reduce_scatter([view(g_left_two)], replicas)
+    d_down_inner, mid = lax.optimization_barrier((d_down_inner, mid))
+    red_left_two = mid[:, 0]
     d_hidden = jnp.einsum("kjgt,jbkg->jbt", d_down_inner, right_two, preferred_element_type=fp)
     d_pre = (d_hidden * gelu_slope(pre_piece)).astype(bf)
     d_mixed_up = jnp.einsum("jct,jbc->jbt", d_pre, first_left, preferred_element_type=fp).astype(bf)
@@ -108,19 +117,13 @@
     d_up_inner = lax.all_to_all(d_mixed_up, "tensor", split_axis=1, concat_axis=0, tiled=True)
     mixed_sorted = chunk_order(mixed_piece, 1, replicas)
     hidden_sorted = chunk_order(hidden, 1, replicas)
-    down_sorted = chunk_order(mixed_down, 1, replicas)
     g_left_one = jnp.einsum("jbt,jct->jbc", mixed_sorted, d_pre, preferred_element_type=fp)
-    g_right_two = jnp.einsum(
-        "jbt,kjgt->jbkg", hidden_sorted, d_down_inner, preferred_element_type=fp
-    ).reshape(hid_blocks, block_width, block_width)
-    g_left_two = jnp.einsum("kwt,tkc->kwc", down_sorted, cot_parts, preferred_element_type=fp)
-
-    def view(g):
-        return g.reshape(in_blocks if g.ndim == 2 else g.shape[0], replicas, -1, g.shape[-1])
+    d_down_rows = jnp.transpose(d_down_inner, (1, 0, 2, 3)).reshape(hid_blocks, all_in * sub_width, tok_rows)
+    g_right_two = jnp.einsum("jbt,jnt->jbn", hidden_sorted, d_down_rows, preferred_element_type=fp)
 
     early_stages = 2
     early = dp_reduce_scatter(
-        [view(g_left_two), view(g_left_one), view(g_right_two)], replicas, 0, early_stages
+        [view(g_left_one), view(g_right_two)], replicas, 0, early_stages
     )
     d_up_inner, *early = lax.optimization_barrier((d_up_inner, *early))
 
@@ -138,7 +141,7 @@
         if early_stages + stage < stages:
             early = dp_reduce_scatter(early, replicas, early_stages + stage, early_stages + stage + 1)
     red_right_one = late[0][:, 0]
-    red_left_two, red_left_one, red_right_two = [e[:, 0] for e in early]
+    red_left_one, red_right_two = [e[:, 0] for e in early]
     reduced = (red_right_one, red_left_one, red_right_two, red_left_two)
     grad_right_one, grad_left_one, grad_right_two, grad_left_two = [r * grad_scale for r in reduced]
     return (layer_out, grad_tokens, grad_right_one, grad_left_one, grad_right_two, grad_left_two)

time: 208 us -> 217 us (1.043)
  the two profiles are of different devices: /device:TPU:76 before, /device:TPU:1 now
where the time goes in v9:
time: 217 us; the launch traced here: 214 us
  waiting for transfers between devices  88.1 us (41%)
  starting transfers between devices  85.1 us (39%)
  local copies, waits for them, and re-layouts  17.8 us (8%)
  matrix products  13.7 us (6%)
  other arithmetic  8.51 us (4%)
    ppermute x12, starting transfers between devices, dp_reduce_scatter(): got = lax.ppermute(packed, 'dp', perm)  45.5 us
    all_to_all x1, waiting for transfers between devices, layer(): lax.all_to_all(up_inner, 'tensor', split_axis=0, concat_axis=1, tiled=True)  24.8 us
    ppermute x12, waiting for transfers between devices, dp_reduce_scatter(): got = lax.ppermute(packed, 'dp', perm)  24.8 us
    all_to_all x1, waiting for transfers between devices, layer(): lax.all_to_all(down_inner, 'tensor', split_axis=0, concat_axis=1, tiled=T...  23.2 us
    all_to_all x1, waiting for transfers between devices, layer(): lax.all_to_all(d_mixed_up, 'tensor', split_axis=1, concat_axis=0, tiled=T...  15.2 us
    all_to_all x1, starting transfers between devices, layer(): lax.all_to_all(up_inner, 'tensor', split_axis=0, concat_axis=1, tiled=True)  14.3 us
    all_to_all x1, starting transfers between devices, layer(): lax.all_to_all(d_mixed_up, 'tensor', split_axis=1, concat_axis=0, tiled=T...  9.99 us
    unnamed x43, local copies, waits for them, and re-layouts  8.78 us
  transfers between devices with their start and end apart: 16, of which 12 were waited for; matrix products, arithmetic and copies ran while one was open for 9% of the time, Pallas kernels for 0%

profile of v9, /device:TPU:1, one launch (start us, length us, event | category | flops | bytes accessed | tf_op | source)
XLA Modules:
  0.0 214.5 jit_solution(15978020996816488748)
XLA Ops:
  0.6 1.3 copy.77
  2.0 1.4 fusion.10
  3.4 1.6 copy.79
  5.0 14.3 %all-to-all-start = ((bf16[128,1,8,512]{3,2,1,0:T(8,128)(2,1)}), bf16[128,1,8,512]{3,2,1,0:T(8,128)(2,1)S(1)}, u32[]{:S(2)}, u32[]{:S(2)}) async-start(bf16[128,1,8,512]{3,2,1,0:T(8,128)(2,1)} %copy.79), calls=%async_computation | async-start | bytes 2097152 | tf_op jit(solution)/shard_map/all_to_all | solution.py:85
  19.3 1.0 copy.82
  20.3 24.8 %all-to-all-done = bf16[128,1,8,512]{3,2,1,0:T(8,128)(2,1)S(1)} async-done(((bf16[128,1,8,512]{3,2,1,0:T(8,128)(2,1)}), bf16[128,1,8,512]{3,2,1,0:T(8,128)(2,1)S(1)}, u32[]{:S(2)}, u32[]{:S(2)}) %all-to-all-start) | async-done | bytes 1048608 | tf_op jit(solution)/shard_map/all_to_all | solution.py:85
  45.1 1.9 fusion.7
  47.1 1.0 copy-done.6
  48.5 1.6 copy.84
  50.1 7.6 %all-to-all-start.1 = ((bf16[32,4,8,512]{3,2,1,0:T(8,128)(2,1)}), bf16[32,4,8,512]{3,2,1,0:T(8,128)(2,1)S(1)}, u32[]{:S(2)}, u32[]{:S(2)}) async-start(bf16[32,4,8,512]{3,2,1,0:T(8,128)(2,1)} %copy.84), calls=%async_computation.1 | async-start | bytes 2097152 | tf_op jit(solution)/shard_map/all_to_all | solution.py:92
  57.7 2.5 %fusion.11 = bf16[1,128,8,512]{3,2,0,1:T(8,128)(2,1)} fusion(bf16[512,256]{1,0:T(8,128)(2,1)S(1)} %copy-done.13, bf16[1,1024,256]{2,1,0:T(8,128)(2,1)} %param.10), kind=kOutput, calls=%fused_computation.18 | convolution fusion | flops 268959744 | bytes 1835008 | tf_op jit(solution)/shard_map/tkc,kwc->kwt/dot_general | solution.py:99
  60.2 23.2 %all-to-all-done.1 = bf16[32,4,8,512]{3,2,1,0:T(8,128)(2,1)S(1)} async-done(((bf16[32,4,8,512]{3,2,1,0:T(8,128)(2,1)}), bf16[32,4,8,512]{3,2,1,0:T(8,128)(2,1)S(1)}, u32[]{:S(2)}, u32[]{:S(2)}) %all-to-all-start.1) | async-done | bytes 1048608 | tf_op jit(solution)/shard_map/all_to_all | solution.py:92
  83.4 1.0 copy-done.4
  84.4 7.7 %all-to-all-start.2 = ((bf16[1,128,8,512]{3,2,0,1:T(8,128)(2,1)}), bf16[1,128,8,512]{3,2,0,1:T(8,128)(2,1)S(1)}, u32[]{:S(2)}, u32[]{:S(2)}) async-start(bf16[1,128,8,512]{3,2,0,1:T(8,128)(2,1)} %fusion.11), calls=%async_computation.2 | async-start | bytes 2097152 | tf_op jit(solution)/shard_map/all_to_all | solution.py:103
  92.1 1.3 copy.86
  93.9 1.0 copy-done.11
  94.8 0.7 dynamic-slice_convert_fusion.3
  95.6 2.9 %collective-permute-start = (bf16[512,256]{1,0:T(8,128)(2,1)}, bf16[512,256]{1,0:T(8,128)(2,1)S(1)}, u32[]{:S(2)}, u32[]{:S(2)}) collective-permute-start(bf16[512,256]{1,0:T(8,128)(2,1)} %bitcast.20), channel_id=1, source_target_pairs={{0,32},{32,0},{64,96},{96,64},{128,160},{160,128},{192,224},{224,1... | collective-permute-start | bytes 786440 | tf_op jit(solution)/shard_map/ppermute | solution.py:53
  98.5 1.3 collective-permute-done
  99.8 1.1 convert_add_fusion.3
  100.9 0.8 copy-done.12
  101.7 3.1 %collective-permute-start.1 = (bf16[256,256]{1,0:T(8,128)(2,1)S(1)}, bf16[256,256]{1,0:T(8,128)(2,1)S(1)}, u32[]{:S(2)}, u32[]{:S(2)}) collective-permute-start(bf16[256,256]{1,0:T(8,128)(2,1)S(1)} %bitcast.219), channel_id=1, source_target_pairs={{0,128},{32,160},{64,192},{96,224},{128,0},{160,32},{192,64},{224,... | collective-permute-start | bytes 393224 | tf_op jit(solution)/shard_map/ppermute | solution.py:53
  104.9 3.4 %collective-permute-done.1 = bf16[256,256]{1,0:T(8,128)(2,1)S(1)} collective-permute-done((bf16[256,256]{1,0:T(8,128)(2,1)S(1)}, bf16[256,256]{1,0:T(8,128)(2,1)S(1)}, u32[]{:S(2)}, u32[]{:S(2)}) %collective-permute-start.1) | collective-permute-done | bytes 131104 | tf_op jit(solution)/shard_map/ppermute | solution.py:53
  108.3 1.0 convert_add_fusion.7
  109.3 4.7 %collective-permute-start.2 = (bf16[128,256]{1,0:T(8,128)(2,1)S(1)}, bf16[128,256]{1,0:T(8,128)(2,1)S(1)}, u32[]{:S(2)}, u32[]{:S(2)}) collective-permute-start(bf16[128,256]{1,0:T(8,128)(2,1)S(1)} %bitcast.229), channel_id=1, source_target_pairs={{0,256},{32,288},{64,320},{96,352},{128,384},{160,416},{192,448},{... | collective-permute-start | bytes 196616 | tf_op jit(solution)/shard_map/ppermute | solution.py:53
  114.0 2.1 collective-permute-done.2
  116.1 0.6 copy-done.19
  116.7 0.9 convert_add_fusion.11
  117.6 4.8 %collective-permute-start.3 = (bf16[64,256]{1,0:T(8,128)(2,1)S(1)}, bf16[64,256]{1,0:T(8,128)(2,1)S(1)}, u32[]{:S(2)}, u32[]{:S(2)}) collective-permute-start(bf16[64,256]{1,0:T(8,128)(2,1)S(1)} %fusion.38), channel_id=1, source_target_pairs={{0,64},{32,96},{64,0},{96,32},{128,192},{160,224},{192,128},{224,1... | collective-permute-start | bytes 98312 | tf_op jit(solution)/shard_map/ppermute | solution.py:53
  122.6 1.0 copy-done.7
  123.6 1.1 copy.92
  124.7 1.5 collective-permute-done.3
  126.2 0.6 convert_add_fusion.15
  126.8 2.7 %fusion.5 = bf16[4,256,512]{2,1,0:T(8,128)(2,1)S(1)} fusion(f32[4,512,256]{1,2,0:T(8,128)} %get-tuple-element.25, bf16[32,4,8,512]{3,2,1,0:T(8,128)(2,1)S(1)} %bitcast.183, bf16[4,256,256]{1,2,0:T(8,128)(2,1)} %copy.82), kind=kOutput, calls=%fused_computation.6 | convolution fusion | flops 273678336 | bytes 4718592 | tf_op jit(solution)/shard_map/kjgt,jbkg->jbt/dot_general | solution.py:113
  129.6 0.5 fusion.19
  130.1 0.5 fusion.46
  131.0 0.5 copy-done.10
  131.5 0.8 pad_maximum_fusion
  132.4 5.1 %collective-permute-start.4 = (bf16[1024,256]{1,0:T(8,128)(2,1)}, bf16[1024,256]{1,0:T(8,128)(2,1)}, u32[]{:S(2)}, u32[]{:S(2)}) collective-permute-start(bf16[1024,256]{1,0:T(8,128)(2,1)} %pad_maximum_fusion), channel_id=1, source_target_pairs={{0,32},{32,0},{64,96},{96,64},{128,160},{160,128},{192,224},{224,1... | collective-permute-start | bytes 1572872 | tf_op jit(solution)/shard_map/ppermute | solution.py:53
  137.7 0.4 fusion.13
  138.1 1.1 copy.89
  139.2 10.0 %all-to-all-start.3 = ((bf16[4,32,8,512]{3,2,0,1:T(8,128)(2,1)}), bf16[4,32,8,512]{3,2,0,1:T(8,128)(2,1)S(1)}, u32[]{:S(2)}, u32[]{:S(2)}) async-start(bf16[4,32,8,512]{3,2,0,1:T(8,128)(2,1)} %copy.89), calls=%async_computation.3 | async-start | bytes 2097152 | tf_op jit(solution)/shard_map/all_to_all | solution.py:117
  149.2 1.1 fusion.42
  150.3 1.2 convert_add_fusion.2
  151.8 3.1 %collective-permute-start.5 = (bf16[512,256]{1,0:T(8,128)(2,1)S(1)}, bf16[512,256]{1,0:T(8,128)(2,1)S(1)}, u32[]{:S(2)}, u32[]{:S(2)}) collective-permute-start(bf16[512,256]{1,0:T(8,128)(2,1)S(1)} %pad_maximum_fusion.1), channel_id=1, source_target_pairs={{0,128},{32,160},{64,192},{96,224},{128,0},{160,32},{192,64},{224,... | collective-permute-start | bytes 786440 | tf_op jit(solution)/shard_map/ppermute | solution.py:53
  154.9 1.2 convolution_convert_fusion.4
  156.1 0.6 multiply_bitcast_fusion
  156.8 4.5 %collective-permute-done.5 = bf16[512,256]{1,0:T(8,128)(2,1)S(1)} collective-permute-done((bf16[512,256]{1,0:T(8,128)(2,1)S(1)}, bf16[512,256]{1,0:T(8,128)(2,1)S(1)}, u32[]{:S(2)}, u32[]{:S(2)}) %collective-permute-start.5) | collective-permute-done | bytes 262176 | tf_op jit(solution)/shard_map/ppermute | solution.py:53
  161.4 15.2 %all-to-all-done.3 = bf16[4,32,8,512]{3,2,0,1:T(8,128)(2,1)S(1)} async-done(((bf16[4,32,8,512]{3,2,0,1:T(8,128)(2,1)}), bf16[4,32,8,512]{3,2,0,1:T(8,128)(2,1)S(1)}, u32[]{:S(2)}, u32[]{:S(2)}) %all-to-all-start.3) | async-done | bytes 1048608 | tf_op jit(solution)/shard_map/all_to_all | solution.py:117
  176.6 4.7 %collective-permute-start.10 = (bf16[256,256]{1,0:T(8,128)(2,1)S(1)}, bf16[256,256]{1,0:T(8,128)(2,1)S(1)}, u32[]{:S(2)}, u32[]{:S(2)}) collective-permute-start(bf16[256,256]{1,0:T(8,128)(2,1)S(1)} %pad_maximum_fusion.2), channel_id=1, source_target_pairs={{0,256},{32,288},{64,320},{96,352},{128,384},{160,416},{192,448},{... | collective-permute-start | bytes 393224 | tf_op jit(solution)/shard_map/ppermute | solution.py:53
  181.3 1.2 fusion.14
  182.5 0.5 fusion.16
  183.0 3.9 %collective-permute-start.6 = (bf16[128,1024]{1,0:T(8,128)(2,1)S(1)}, bf16[128,1024]{1,0:T(8,128)(2,1)S(1)}, u32[]{:S(2)}, u32[]{:S(2)}) collective-permute-start(bf16[128,1024]{1,0:T(8,128)(2,1)S(1)} %bitcast.214), channel_id=1, source_target_pairs={{0,32},{32,0},{64,96},{96,64},{128,160},{160,128},{192,224},{224,1... | collective-permute-start | bytes 786440 | tf_op jit(solution)/shard_map/ppermute | solution.py:53
  187.1 4.8 %collective-permute-start.11 = (bf16[128,256]{1,0:T(8,128)(2,1)S(1)}, bf16[128,256]{1,0:T(8,128)(2,1)S(1)}, u32[]{:S(2)}, u32[]{:S(2)}) collective-permute-start(bf16[128,256]{1,0:T(8,128)(2,1)S(1)} %pad_maximum_fusion.3), channel_id=1, source_target_pairs={{0,64},{32,96},{64,0},{96,32},{128,192},{160,224},{192,128},{224,1... | collective-permute-start | bytes 196616 | tf_op jit(solution)/shard_map/ppermute | solution.py:53
  192.0 2.1 collective-permute-start.7
  194.2 2.4 %collective-permute-done.11 = bf16[128,256]{1,0:T(8,128)(2,1)S(1)} collective-permute-done((bf16[128,256]{1,0:T(8,128)(2,1)S(1)}, bf16[128,256]{1,0:T(8,128)(2,1)S(1)}, u32[]{:S(2)}, u32[]{:S(2)}) %collective-permute-start.11) | collective-permute-done | bytes 65568 | tf_op jit(solution)/shard_map/ppermute | solution.py:53
  196.6 2.1 collective-permute-done.7
  198.7 1.9 collective-permute-start.8
  200.7 0.6 fusion.33
  201.3 3.9 %collective-permute-done.8 = bf16[32,1024]{1,0:T(8,128)(2,1)S(1)} collective-permute-done((bf16[32,1024]{1,0:T(8,128)(2,1)S(1)}, bf16[32,1024]{1,0:T(8,128)(2,1)S(1)}, u32[]{:S(2)}, u32[]{:S(2)}) %collective-permute-start.8) | collective-permute-done | bytes 65568 | tf_op jit(solution)/shard_map/ppermute | solution.py:53
  205.3 4.4 %collective-permute-start.9 = (bf16[16,1024]{1,0:T(8,128)(2,1)S(1)}, bf16[16,1024]{1,0:T(8,128)(2,1)S(1)}, u32[]{:S(2)}, u32[]{:S(2)}) collective-permute-start(bf16[16,1024]{1,0:T(8,128)(2,1)S(1)} %fusion.39), channel_id=1, source_target_pairs={{0,64},{32,96},{64,0},{96,32},{128,192},{160,224},{192,128},{224,1... | collective-permute-start | bytes 98312 | tf_op jit(solution)/shard_map/ppermute | solution.py:53
  209.7 0.6 fusion.35
  210.3 3.5 %collective-permute-done.9 = bf16[16,1024]{1,0:T(8,128)(2,1)S(1)} collective-permute-done((bf16[16,1024]{1,0:T(8,128)(2,1)S(1)}, bf16[16,1024]{1,0:T(8,128)(2,1)S(1)}, u32[]{:S(2)}, u32[]{:S(2)}) %collective-permute-start.9) | collective-permute-done | bytes 32800 | tf_op jit(solution)/shard_map/ppermute | solution.py:53
  213.9 0.6 fusion.37
  (71 shorter events, 2.4 us)
Async XLA Ops:
  0.6 44.5 %copy-start = (bf16[4,256,256]{2,1,0:T(8,128)(2,1)S(1)}, bf16[4,256,256]{2,1,0:T(8,128)(2,1)}, u32[]{:S(2)}) copy-start(bf16[4,256,256]{2,1,0:T(8,128)(2,1)} %param.8) | copy-start | bytes 1572868
  3.4 15.9 %copy-start.16 = (bf16[4,256,256]{2,1,0:T(8,128)(2,1)S(1)}, bf16[4,256,256]{2,1,0:T(8,128)(2,1)}, u32[]{:S(2)}) copy-start(bf16[4,256,256]{2,1,0:T(8,128)(2,1)} %param.9) | copy-start | bytes 1572868
  5.0 40.1 %all-to-all-start = ((bf16[128,1,8,512]{3,2,1,0:T(8,128)(2,1)}), bf16[128,1,8,512]{3,2,1,0:T(8,128)(2,1)S(1)}, u32[]{:S(2)}, u32[]{:S(2)}) async-start(bf16[128,1,8,512]{3,2,1,0:T(8,128)(2,1)} %copy.79), calls=%async_computation | async-start | bytes 2097152 | tf_op jit(solution)/shard_map/all_to_all | solution.py:85
  45.1 3.0 %copy-start.17 = (bf16[4,256,256]{1,2,0:T(8,128)(2,1)S(1)}, bf16[4,256,256]{1,2,0:T(8,128)(2,1)}, u32[]{:S(2)}) copy-start(bf16[4,256,256]{1,2,0:T(8,128)(2,1)} %copy.82) | copy-start | bytes 1572868
  47.1 1.0 copy-start.6
  48.5 9.2 %copy-start.13 = (bf16[512,256]{1,0:T(8,128)(2,1)S(1)}, bf16[512,256]{1,0:T(8,128)(2,1)}, u32[]{:S(2)}) copy-start(bf16[512,256]{1,0:T(8,128)(2,1)} %param.11) | copy-start | bytes 786436
  50.1 33.3 %all-to-all-start.1 = ((bf16[32,4,8,512]{3,2,1,0:T(8,128)(2,1)}), bf16[32,4,8,512]{3,2,1,0:T(8,128)(2,1)S(1)}, u32[]{:S(2)}, u32[]{:S(2)}) async-start(bf16[32,4,8,512]{3,2,1,0:T(8,128)(2,1)} %copy.84), calls=%async_computation.1 | async-start | bytes 2097152 | tf_op jit(solution)/shard_map/all_to_all | solution.py:92
  83.4 1.0 copy-start.4
  84.4 42.5 %all-to-all-start.2 = ((bf16[1,128,8,512]{3,2,0,1:T(8,128)(2,1)}), bf16[1,128,8,512]{3,2,0,1:T(8,128)(2,1)S(1)}, u32[]{:S(2)}, u32[]{:S(2)}) async-start(bf16[1,128,8,512]{3,2,0,1:T(8,128)(2,1)} %fusion.11), calls=%async_computation.2 | async-start | bytes 2097152 | tf_op jit(solution)/shard_map/all_to_all | solution.py:103
  93.9 1.0 copy-start.11
  95.6 4.2 %collective-permute-start = (bf16[512,256]{1,0:T(8,128)(2,1)}, bf16[512,256]{1,0:T(8,128)(2,1)S(1)}, u32[]{:S(2)}, u32[]{:S(2)}) collective-permute-start(bf16[512,256]{1,0:T(8,128)(2,1)} %bitcast.20), channel_id=1, source_target_pairs={{0,32},{32,0},{64,96},{96,64},{128,160},{160,128},{192,224},{224,1... | collective-permute-start | bytes 786440 | tf_op jit(solution)/shard_map/ppermute | solution.py:53
  100.9 0.8 copy-start.12
  101.7 6.6 %collective-permute-start.1 = (bf16[256,256]{1,0:T(8,128)(2,1)S(1)}, bf16[256,256]{1,0:T(8,128)(2,1)S(1)}, u32[]{:S(2)}, u32[]{:S(2)}) collective-permute-start(bf16[256,256]{1,0:T(8,128)(2,1)S(1)} %bitcast.219), channel_id=1, source_target_pairs={{0,128},{32,160},{64,192},{96,224},{128,0},{160,32},{192,64},{224,... | collective-permute-start | bytes 393224 | tf_op jit(solution)/shard_map/ppermute | solution.py:53
  109.3 6.8 %collective-permute-start.2 = (bf16[128,256]{1,0:T(8,128)(2,1)S(1)}, bf16[128,256]{1,0:T(8,128)(2,1)S(1)}, u32[]{:S(2)}, u32[]{:S(2)}) collective-permute-start(bf16[128,256]{1,0:T(8,128)(2,1)S(1)} %bitcast.229), channel_id=1, source_target_pairs={{0,256},{32,288},{64,320},{96,352},{128,384},{160,416},{192,448},{... | collective-permute-start | bytes 196616 | tf_op jit(solution)/shard_map/ppermute | solution.py:53
  116.1 0.6 copy-start.19
  117.6 8.6 %collective-permute-start.3 = (bf16[64,256]{1,0:T(8,128)(2,1)S(1)}, bf16[64,256]{1,0:T(8,128)(2,1)S(1)}, u32[]{:S(2)}, u32[]{:S(2)}) collective-permute-start(bf16[64,256]{1,0:T(8,128)(2,1)S(1)} %fusion.38), channel_id=1, source_target_pairs={{0,64},{32,96},{64,0},{96,32},{128,192},{160,224},{192,128},{224,1... | collective-permute-start | bytes 98312 | tf_op jit(solution)/shard_map/ppermute | solution.py:53
  122.4 1.2 copy-start.7
  126.8 2.7 %copy-start.3 = (bf16[4,2,2,2,2,16,512]{6,5,4,3,2,1,0:T(8,128)(2,1)S(1)}, bf16[4,2,2,2,2,16,512]{6,5,4,3,2,1,0:T(8,128)(2,1)}, u32[]{:S(2)}) copy-start(bf16[4,2,2,2,2,16,512]{6,5,4,3,2,1,0:T(8,128)(2,1)} %copy.92) | copy-start | bytes 3145732
  129.5 1.0 copy-start.1
  130.0 1.0 copy-start.8
  130.0 7.4 %copy-start.14 = (bf16[512,256]{1,0:T(8,128)(2,1)S(1)}, bf16[512,256]{1,0:T(8,128)(2,1)}, u32[]{:S(2)}) copy-start(bf16[512,256]{1,0:T(8,128)(2,1)} %param.6) | copy-start | bytes 786436
  130.5 1.0 copy-start.10
  130.6 7.1 %copy-start.2 = (bf16[4,256,512]{2,1,0:T(8,128)(2,1)S(1)}, bf16[4,256,512]{2,1,0:T(8,128)(2,1)}, u32[]{:S(2)}) copy-start(bf16[4,256,512]{2,1,0:T(8,128)(2,1)} %copy-done.1) | copy-start | bytes 3145732
  132.4 16.9 %collective-permute-start.4 = (bf16[1024,256]{1,0:T(8,128)(2,1)}, bf16[1024,256]{1,0:T(8,128)(2,1)}, u32[]{:S(2)}, u32[]{:S(2)}) collective-permute-start(bf16[1024,256]{1,0:T(8,128)(2,1)} %pad_maximum_fusion), channel_id=1, source_target_pairs={{0,32},{32,0},{64,96},{96,64},{128,160},{160,128},{192,224},{224,1... | collective-permute-start | bytes 1572872 | tf_op jit(solution)/shard_map/ppermute | solution.py:53
  139.2 12.4 %copy-start.9 = (f32[4,256,256]{2,1,0:T(8,128)S(1)}, f32[4,256,256]{2,1,0:T(8,128)}, u32[]{:S(2)}) copy-start(f32[4,256,256]{2,1,0:T(8,128)} %copy-done.8) | copy-start | bytes 3145732
  139.2 37.3 %all-to-all-start.3 = ((bf16[4,32,8,512]{3,2,0,1:T(8,128)(2,1)}), bf16[4,32,8,512]{3,2,0,1:T(8,128)(2,1)S(1)}, u32[]{:S(2)}, u32[]{:S(2)}) async-start(bf16[4,32,8,512]{3,2,0,1:T(8,128)(2,1)} %copy.89), calls=%async_computation.3 | async-start | bytes 2097152 | tf_op jit(solution)/shard_map/all_to_all | solution.py:117
  150.3 4.6 %copy-start.5 = (bf16[32,4,8,512]{3,2,1,0:T(8,128)(2,1)S(1)}, bf16[32,4,8,512]{3,2,1,0:T(8,128)(2,1)}, u32[]{:S(2)}) copy-start(bf16[32,4,8,512]{3,2,1,0:T(8,128)(2,1)} %copy-done.4) | copy-start | bytes 3145732
  150.3 4.6 %copy-start.15 = (bf16[1,1024,256]{2,1,0:T(8,128)(2,1)S(1)}, bf16[1,1024,256]{2,1,0:T(8,128)(2,1)}, u32[]{:S(2)}) copy-start(bf16[1,1024,256]{2,1,0:T(8,128)(2,1)} %param.10) | copy-start | bytes 1572868
  151.6 4.5 %copy-start.18 = (f32[1,1,64,256]{3,2,1,0:T(8,128)S(1)}, f32[1,1,64,256]{3,2,1,0:T(8,128)}, u32[]{:S(2)}) copy-start(f32[1,1,64,256]{3,2,1,0:T(8,128)} %convert_add_fusion.15) | copy-start | bytes 196612
  151.8 9.5 %collective-permute-start.5 = (bf16[512,256]{1,0:T(8,128)(2,1)S(1)}, bf16[512,256]{1,0:T(8,128)(2,1)S(1)}, u32[]{:S(2)}, u32[]{:S(2)}) collective-permute-start(bf16[512,256]{1,0:T(8,128)(2,1)S(1)} %pad_maximum_fusion.1), channel_id=1, source_target_pairs={{0,128},{32,160},{64,192},{96,224},{128,0},{160,32},{192,64},{224,... | collective-permute-start | bytes 786440 | tf_op jit(solution)/shard_map/ppermute | solution.py:53
  176.6 10.4 %collective-permute-start.10 = (bf16[256,256]{1,0:T(8,128)(2,1)S(1)}, bf16[256,256]{1,0:T(8,128)(2,1)S(1)}, u32[]{:S(2)}, u32[]{:S(2)}) collective-permute-start(bf16[256,256]{1,0:T(8,128)(2,1)S(1)} %pad_maximum_fusion.2), channel_id=1, source_target_pairs={{0,256},{32,288},{64,320},{96,352},{128,384},{160,416},{192,448},{... | collective-permute-start | bytes 393224 | tf_op jit(solution)/shard_map/ppermute | solution.py:53
  183.0 8.9 %collective-permute-start.6 = (bf16[128,1024]{1,0:T(8,128)(2,1)S(1)}, bf16[128,1024]{1,0:T(8,128)(2,1)S(1)}, u32[]{:S(2)}, u32[]{:S(2)}) collective-permute-start(bf16[128,1024]{1,0:T(8,128)(2,1)S(1)} %bitcast.214), channel_id=1, source_target_pairs={{0,32},{32,0},{64,96},{96,64},{128,160},{160,128},{192,224},{224,1... | collective-permute-start | bytes 786440 | tf_op jit(solution)/shard_map/ppermute | solution.py:53
  187.1 9.4 %collective-permute-start.11 = (bf16[128,256]{1,0:T(8,128)(2,1)S(1)}, bf16[128,256]{1,0:T(8,128)(2,1)S(1)}, u32[]{:S(2)}, u32[]{:S(2)}) collective-permute-start(bf16[128,256]{1,0:T(8,128)(2,1)S(1)} %pad_maximum_fusion.3), channel_id=1, source_target_pairs={{0,64},{32,96},{64,0},{96,32},{128,192},{160,224},{192,128},{224,1... | collective-permute-start | bytes 196616 | tf_op jit(solution)/shard_map/ppermute | solution.py:53
  192.0 6.7 %collective-permute-start.7 = (bf16[64,1024]{1,0:T(8,128)(2,1)S(1)}, bf16[64,1024]{1,0:T(8,128)(2,1)S(1)}, u32[]{:S(2)}, u32[]{:S(2)}) collective-permute-start(bf16[64,1024]{1,0:T(8,128)(2,1)S(1)} %bitcast.220), channel_id=1, source_target_pairs={{0,128},{32,160},{64,192},{96,224},{128,0},{160,32},{192,64},{224,... | collective-permute-start | bytes 393224 | tf_op jit(solution)/shard_map/ppermute | solution.py:53
  198.7 6.5 %collective-permute-start.8 = (bf16[32,1024]{1,0:T(8,128)(2,1)S(1)}, bf16[32,1024]{1,0:T(8,128)(2,1)S(1)}, u32[]{:S(2)}, u32[]{:S(2)}) collective-permute-start(bf16[32,1024]{1,0:T(8,128)(2,1)S(1)} %bitcast.230), channel_id=1, source_target_pairs={{0,256},{32,288},{64,320},{96,352},{128,384},{160,416},{192,448},{... | collective-permute-start | bytes 196616 | tf_op jit(solution)/shard_map/ppermute | solution.py:53
  205.3 8.6 %collective-permute-start.9 = (bf16[16,1024]{1,0:T(8,128)(2,1)S(1)}, bf16[16,1024]{1,0:T(8,128)(2,1)S(1)}, u32[]{:S(2)}, u32[]{:S(2)}) collective-permute-start(bf16[16,1024]{1,0:T(8,128)(2,1)S(1)} %fusion.39), channel_id=1, source_target_pairs={{0,64},{32,96},{64,0},{96,32},{128,192},{160,224},{192,128},{224,1... | collective-permute-start | bytes 98312 | tf_op jit(solution)/shard_map/ppermute | solution.py:53

commit v10 on v8

--- a/solution.py
+++ b/solution.py
@@ -110,15 +110,14 @@
     hidden_sorted = chunk_order(hidden, 1, replicas)
     down_sorted = chunk_order(mixed_down, 1, replicas)
     g_left_one = jnp.einsum("jbt,jct->jbc", mixed_sorted, d_pre, preferred_element_type=fp)
-    g_right_two = jnp.einsum(
-        "jbt,kjgt->jbkg", hidden_sorted, d_down_inner, preferred_element_type=fp
-    ).reshape(hid_blocks, block_width, block_width)
+    d_down_rows = jnp.transpose(d_down_inner, (1, 0, 2, 3)).reshape(hid_blocks, all_in * sub_width, tok_rows)
+    g_right_two = jnp.einsum("jbt,jnt->jbn", hidden_sorted, d_down_rows, preferred_element_type=fp)
     g_left_two = jnp.einsum("kwt,tkc->kwc", down_sorted, cot_parts, preferred_element_type=fp)
 
     def view(g):
         return g.reshape(in_blocks if g.ndim == 2 else g.shape[0], replicas, -1, g.shape[-1])
 
-    early_stages = 2
+    early_stages = 3
     early = dp_reduce_scatter(
         [view(g_left_two), view(g_left_one), view(g_right_two)], replicas, 0, early_stages
     )

time: 208 us -> 201 us (0.966)
  the two profiles are of different devices: /device:TPU:76 before, /device:TPU:64 now
where the time goes in v10:
time: 201 us; the launch traced here: 200 us
  waiting for transfers between devices  103 us (51%)
  starting transfers between devices  59.6 us (30%)
  local copies, waits for them, and re-layouts  17.7 us (9%)
  matrix products  12.4 us (6%)
  other arithmetic  5.77 us (3%)
    ppermute x8, starting transfers between devices, dp_reduce_scatter(): got = lax.ppermute(packed, 'dp', perm)  30 us
    all_to_all x1, waiting for transfers between devices, layer(): lax.all_to_all(up_inner, 'tensor', split_axis=0, concat_axis=1, tiled=True)  26.5 us
    all_to_all x1, waiting for transfers between devices, layer(): lax.all_to_all(down_inner, 'tensor', split_axis=0, concat_axis=1, tiled=T...  21.9 us
    all_to_all x1, waiting for transfers between devices, layer(): lax.all_to_all(d_mixed_down, 'tensor', split_axis=1, concat_axis=0, tiled...  21.4 us
    ppermute x8, waiting for transfers between devices, dp_reduce_scatter(): got = lax.ppermute(packed, 'dp', perm)  19.9 us
    all_to_all x1, waiting for transfers between devices, layer(): lax.all_to_all(d_mixed_up, 'tensor', split_axis=1, concat_axis=0, tiled=T...  13.6 us
    all_to_all x1, starting transfers between devices, layer(): lax.all_to_all(up_inner, 'tensor', split_axis=0, concat_axis=1, tiled=True)  13.2 us
    unnamed x45, local copies, waits for them, and re-layouts  8.42 us
  transfers between devices with their start and end apart: 12, of which 11 were waited for; matrix products, arithmetic and copies ran while one was open for 10% of the time, Pallas kernels for 0%

profile of v10, /device:TPU:64, one launch (start us, length us, event | category | flops | bytes accessed | tf_op | source)
XLA Modules:
  0.0 200.1 jit_solution(17189166502094904778)
XLA Ops:
  0.6 1.3 copy.64
  2.0 1.4 fusion.10
  3.4 1.6 copy.66
  5.0 13.2 %all-to-all-start = ((bf16[128,1,8,512]{3,2,1,0:T(8,128)(2,1)}), bf16[128,1,8,512]{3,2,1,0:T(8,128)(2,1)S(1)}, u32[]{:S(2)}, u32[]{:S(2)}) async-start(bf16[128,1,8,512]{3,2,1,0:T(8,128)(2,1)} %copy.66), calls=%async_computation | async-start | bytes 2097152 | tf_op jit(solution)/shard_map/all_to_all | solution.py:85
  18.2 1.5 fusion.11
  19.6 26.5 %all-to-all-done = bf16[128,1,8,512]{3,2,1,0:T(8,128)(2,1)S(1)} async-done(((bf16[128,1,8,512]{3,2,1,0:T(8,128)(2,1)}), bf16[128,1,8,512]{3,2,1,0:T(8,128)(2,1)S(1)}, u32[]{:S(2)}, u32[]{:S(2)}) %all-to-all-start) | async-done | bytes 1048608 | tf_op jit(solution)/shard_map/all_to_all | solution.py:85
  46.1 5.4 %all-to-all-start.2 = ((bf16[1,128,8,512]{3,2,0,1:T(8,128)(2,1)}), bf16[1,128,8,512]{3,2,0,1:T(8,128)(2,1)S(1)}, u32[]{:S(2)}, u32[]{:S(2)}) async-start(bf16[1,128,8,512]{3,2,0,1:T(8,128)(2,1)} %fusion.11), calls=%async_computation.2 | async-start | bytes 2097152 | tf_op jit(solution)/shard_map/all_to_all | solution.py:103
  51.5 2.0 %copy.69 = bf16[4,256,256]{1,2,0:T(8,128)(2,1)} copy(bf16[4,256,256]{2,1,0:T(8,128)(2,1)} %param.9) | data formatting | bytes 1048576 | tf_op args[3]
  53.6 2.0 fusion.7
  55.5 0.4 fusion.12
  56.0 0.6 copy-done.1
  56.5 1.6 copy.71
  58.1 21.4 %all-to-all-done.2 = bf16[1,128,8,512]{3,2,0,1:T(8,128)(2,1)S(1)} async-done(((bf16[1,128,8,512]{3,2,0,1:T(8,128)(2,1)}), bf16[1,128,8,512]{3,2,0,1:T(8,128)(2,1)S(1)}, u32[]{:S(2)}, u32[]{:S(2)}) %all-to-all-start.2) | async-done | bytes 1048608 | tf_op jit(solution)/shard_map/all_to_all | solution.py:103
  79.5 5.6 %all-to-all-start.1 = ((bf16[32,4,8,512]{3,2,1,0:T(8,128)(2,1)}), bf16[32,4,8,512]{3,2,1,0:T(8,128)(2,1)}, u32[]{:S(2)}, u32[]{:S(2)}) async-start(bf16[32,4,8,512]{3,2,1,0:T(8,128)(2,1)} %copy.71), calls=%async_computation.1 | async-start | bytes 2097152 | tf_op jit(solution)/shard_map/all_to_all | solution.py:92
  85.1 0.1 copy.67
  85.2 0.1 copy.78
  85.3 1.0 copy-done.2
  86.3 0.1 copy.79
  86.4 0.6 copy-done.9
  87.1 1.2 fusion.5
  88.4 0.5 fusion.49
  88.9 0.5 fusion.19
  89.3 0.5 copy-done.5
  89.8 0.5 copy-done.3
  90.3 0.9 dynamic-slice_convert_fusion.1
  91.2 21.9 %all-to-all-done.1 = bf16[32,4,8,512]{3,2,1,0:T(8,128)(2,1)} async-done(((bf16[32,4,8,512]{3,2,1,0:T(8,128)(2,1)}), bf16[32,4,8,512]{3,2,1,0:T(8,128)(2,1)}, u32[]{:S(2)}, u32[]{:S(2)}) %all-to-all-start.1) | async-done | bytes 1048608 | tf_op jit(solution)/shard_map/all_to_all | solution.py:92
  113.1 1.4 copy.76
  114.5 0.4 fusion.29
  115.0 1.0 copy-done.7
  116.0 1.0 pad_maximum_fusion
  117.0 1.9 collective-permute-start
  118.9 2.6 %collective-permute-done = bf16[1536,256]{1,0:T(8,128)(2,1)} collective-permute-done((bf16[1536,256]{1,0:T(8,128)(2,1)}, bf16[1536,256]{1,0:T(8,128)(2,1)}, u32[]{:S(2)}, u32[]{:S(2)}) %collective-permute-start) | collective-permute-done | bytes 786464 | tf_op jit(solution)/shard_map/ppermute | solution.py:53
  121.5 1.2 fusion.45
  122.6 0.1 convert_add_fusion.2
  122.9 0.1 convert_add_fusion.1
  123.0 0.6 copy-done.12
  123.7 0.8 pad_maximum_fusion.1
  124.4 3.4 %collective-permute-start.1 = (bf16[768,256]{1,0:T(8,128)(2,1)}, bf16[768,256]{1,0:T(8,128)(2,1)}, u32[]{:S(2)}, u32[]{:S(2)}) collective-permute-start(bf16[768,256]{1,0:T(8,128)(2,1)} %pad_maximum_fusion.1), channel_id=1, source_target_pairs={{0,128},{32,160},{64,192},{96,224},{128,0},{160,32},{192,64},{224,... | collective-permute-start | bytes 1179656 | tf_op jit(solution)/shard_map/ppermute | solution.py:53
  127.9 0.1 copy.81
  128.0 0.4 fusion.13
  128.5 1.1 copy.75
  129.6 5.5 %all-to-all-start.3 = ((bf16[4,32,8,512]{3,2,0,1:T(8,128)(2,1)}), bf16[4,32,8,512]{3,2,0,1:T(8,128)(2,1)S(1)}, u32[]{:S(2)}, u32[]{:S(2)}) async-start(bf16[4,32,8,512]{3,2,0,1:T(8,128)(2,1)} %copy.75), calls=%async_computation.3 | async-start | bytes 2097152 | tf_op jit(solution)/shard_map/all_to_all | solution.py:108
  135.1 2.6 %collective-permute-done.1 = bf16[768,256]{1,0:T(8,128)(2,1)} collective-permute-done((bf16[768,256]{1,0:T(8,128)(2,1)}, bf16[768,256]{1,0:T(8,128)(2,1)}, u32[]{:S(2)}, u32[]{:S(2)}) %collective-permute-start.1) | collective-permute-done | bytes 393248 | tf_op jit(solution)/shard_map/ppermute | solution.py:53
  137.8 1.1 fusion.46
  138.8 1.0 convert_add_fusion.7
  140.0 4.9 %collective-permute-start.2 = (bf16[384,256]{1,0:T(8,128)(2,1)S(1)}, bf16[384,256]{1,0:T(8,128)(2,1)S(1)}, u32[]{:S(2)}, u32[]{:S(2)}) collective-permute-start(bf16[384,256]{1,0:T(8,128)(2,1)S(1)} %pad_maximum_fusion.2), channel_id=1, source_target_pairs={{0,256},{32,288},{64,320},{96,352},{128,384},{160,416},{192,448},{... | collective-permute-start | bytes 589832 | tf_op jit(solution)/shard_map/ppermute | solution.py:53
  145.0 2.4 %convolution_convert_fusion.4 = bf16[512,256]{1,0:T(8,128)(2,1)} fusion(bf16[1024,512]{1,0:T(8,128)(2,1)} %bitcast.11, bf16[1,1024,256]{2,1,0:T(8,128)(2,1)S(1)} %copy-done.18), kind=kOutput, calls=%fused_computation.23 | convolution fusion | flops 268566528 | bytes 1835008 | tf_op jit(solution)/shard_map/kwt,kwc->tkc/dot_general | solution.py:94
  147.4 2.1 %collective-permute-done.2 = bf16[384,256]{1,0:T(8,128)(2,1)S(1)} collective-permute-done((bf16[384,256]{1,0:T(8,128)(2,1)S(1)}, bf16[384,256]{1,0:T(8,128)(2,1)S(1)}, u32[]{:S(2)}, u32[]{:S(2)}) %collective-permute-start.2) | collective-permute-done | bytes 196640 | tf_op jit(solution)/shard_map/ppermute | solution.py:53
  149.6 13.6 %all-to-all-done.3 = bf16[4,32,8,512]{3,2,0,1:T(8,128)(2,1)S(1)} async-done(((bf16[4,32,8,512]{3,2,0,1:T(8,128)(2,1)}), bf16[4,32,8,512]{3,2,0,1:T(8,128)(2,1)S(1)}, u32[]{:S(2)}, u32[]{:S(2)}) %all-to-all-start.3) | async-done | bytes 1048608 | tf_op jit(solution)/shard_map/all_to_all | solution.py:108
  163.2 5.3 %collective-permute-start.7 = (bf16[192,256]{1,0:T(8,128)(2,1)S(1)}, bf16[192,256]{1,0:T(8,128)(2,1)S(1)}, u32[]{:S(2)}, u32[]{:S(2)}) collective-permute-start(bf16[192,256]{1,0:T(8,128)(2,1)S(1)} %pad_maximum_fusion.3), channel_id=1, source_target_pairs={{0,64},{32,96},{64,0},{96,32},{128,192},{160,224},{192,128},{224,1... | collective-permute-start | bytes 294920 | tf_op jit(solution)/shard_map/ppermute | solution.py:53
  168.6 0.5 fusion.16
  169.1 1.9 collective-permute-start.3
  171.0 1.2 fusion.14
  172.2 2.5 %collective-permute-done.7 = bf16[192,256]{1,0:T(8,128)(2,1)S(1)} collective-permute-done((bf16[192,256]{1,0:T(8,128)(2,1)S(1)}, bf16[192,256]{1,0:T(8,128)(2,1)S(1)}, u32[]{:S(2)}, u32[]{:S(2)}) %collective-permute-start.7) | collective-permute-done | bytes 98336 | tf_op jit(solution)/shard_map/ppermute | solution.py:53
  174.8 2.4 %collective-permute-start.4 = (bf16[64,1024]{1,0:T(8,128)(2,1)S(1)}, bf16[64,1024]{1,0:T(8,128)(2,1)S(1)}, u32[]{:S(2)}, u32[]{:S(2)}) collective-permute-start(bf16[64,1024]{1,0:T(8,128)(2,1)S(1)} %bitcast.234), channel_id=1, source_target_pairs={{0,128},{32,160},{64,192},{96,224},{128,0},{160,32},{192,64},{224,... | collective-permute-start | bytes 393224 | tf_op jit(solution)/shard_map/ppermute | solution.py:53
  177.3 0.6 fusion.36
  177.9 3.8 %collective-permute-done.4 = bf16[64,1024]{1,0:T(8,128)(2,1)S(1)} collective-permute-done((bf16[64,1024]{1,0:T(8,128)(2,1)S(1)}, bf16[64,1024]{1,0:T(8,128)(2,1)S(1)}, u32[]{:S(2)}, u32[]{:S(2)}) %collective-permute-start.4) | collective-permute-done | bytes 131104 | tf_op jit(solution)/shard_map/ppermute | solution.py:53
  181.7 4.6 %collective-permute-start.5 = (bf16[32,1024]{1,0:T(8,128)(2,1)S(1)}, bf16[32,1024]{1,0:T(8,128)(2,1)S(1)}, u32[]{:S(2)}, u32[]{:S(2)}) collective-permute-start(bf16[32,1024]{1,0:T(8,128)(2,1)S(1)} %bitcast.241), channel_id=1, source_target_pairs={{0,256},{32,288},{64,320},{96,352},{128,384},{160,416},{192,448},{... | collective-permute-start | bytes 196616 | tf_op jit(solution)/shard_map/ppermute | solution.py:53
  186.4 0.6 fusion.38
  187.0 2.4 %collective-permute-done.5 = bf16[32,1024]{1,0:T(8,128)(2,1)S(1)} collective-permute-done((bf16[32,1024]{1,0:T(8,128)(2,1)S(1)}, bf16[32,1024]{1,0:T(8,128)(2,1)S(1)}, u32[]{:S(2)}, u32[]{:S(2)}) %collective-permute-start.5) | collective-permute-done | bytes 65568 | tf_op jit(solution)/shard_map/ppermute | solution.py:53
  189.4 5.5 %collective-permute-start.6 = (bf16[16,1024]{1,0:T(8,128)(2,1)S(1)}, bf16[16,1024]{1,0:T(8,128)(2,1)S(1)}, u32[]{:S(2)}, u32[]{:S(2)}) collective-permute-start(bf16[16,1024]{1,0:T(8,128)(2,1)S(1)} %fusion.41), channel_id=1, source_target_pairs={{0,64},{32,96},{64,0},{96,32},{128,192},{160,224},{192,128},{224,1... | collective-permute-start | bytes 98312 | tf_op jit(solution)/shard_map/ppermute | solution.py:53
  194.9 0.6 fusion.34
  195.6 3.9 %collective-permute-done.6 = bf16[16,1024]{1,0:T(8,128)(2,1)S(1)} collective-permute-done((bf16[16,1024]{1,0:T(8,128)(2,1)S(1)}, bf16[16,1024]{1,0:T(8,128)(2,1)S(1)}, u32[]{:S(2)}, u32[]{:S(2)}) %collective-permute-start.6) | collective-permute-done | bytes 32800 | tf_op jit(solution)/shard_map/ppermute | solution.py:53
  199.5 0.6 fusion.40
  (64 shorter events, 0.8 us)
Async XLA Ops:
  0.6 52.9 %copy-start = (bf16[4,256,256]{2,1,0:T(8,128)(2,1)S(1)}, bf16[4,256,256]{2,1,0:T(8,128)(2,1)}, u32[]{:S(2)}) copy-start(bf16[4,256,256]{2,1,0:T(8,128)(2,1)} %param.8) | copy-start | bytes 1572868
  3.4 14.8 %copy-start.13 = (bf16[512,256]{1,0:T(8,128)(2,1)S(1)}, bf16[512,256]{1,0:T(8,128)(2,1)}, u32[]{:S(2)}) copy-start(bf16[512,256]{1,0:T(8,128)(2,1)} %param.11) | copy-start | bytes 786436
  3.4 14.8 %copy-start.17 = (bf16[1,1024,256]{2,1,0:T(8,128)(2,1)S(1)}, bf16[1,1024,256]{2,1,0:T(8,128)(2,1)}, u32[]{:S(2)}) copy-start(bf16[1,1024,256]{2,1,0:T(8,128)(2,1)} %param.10) | copy-start | bytes 1572868
  5.0 41.2 %all-to-all-start = ((bf16[128,1,8,512]{3,2,1,0:T(8,128)(2,1)}), bf16[128,1,8,512]{3,2,1,0:T(8,128)(2,1)S(1)}, u32[]{:S(2)}, u32[]{:S(2)}) async-start(bf16[128,1,8,512]{3,2,1,0:T(8,128)(2,1)} %copy.66), calls=%async_computation | async-start | bytes 2097152 | tf_op jit(solution)/shard_map/all_to_all | solution.py:85
  46.1 33.4 %all-to-all-start.2 = ((bf16[1,128,8,512]{3,2,0,1:T(8,128)(2,1)}), bf16[1,128,8,512]{3,2,0,1:T(8,128)(2,1)S(1)}, u32[]{:S(2)}, u32[]{:S(2)}) async-start(bf16[1,128,8,512]{3,2,0,1:T(8,128)(2,1)} %fusion.11), calls=%async_computation.2 | async-start | bytes 2097152 | tf_op jit(solution)/shard_map/all_to_all | solution.py:103
  53.6 2.0 copy-start.19
  55.5 1.0 copy-start.1
  79.5 33.6 %all-to-all-start.1 = ((bf16[32,4,8,512]{3,2,1,0:T(8,128)(2,1)}), bf16[32,4,8,512]{3,2,1,0:T(8,128)(2,1)}, u32[]{:S(2)}, u32[]{:S(2)}) async-start(bf16[32,4,8,512]{3,2,1,0:T(8,128)(2,1)} %copy.71), calls=%async_computation.1 | async-start | bytes 2097152 | tf_op jit(solution)/shard_map/all_to_all | solution.py:92
  85.1 1.2 copy-start.2
  85.2 1.8 copy-start.9
  85.2 1.9 copy-start.20
  88.8 1.0 copy-start.5
  89.3 1.0 copy-start.3
  113.1 2.9 %copy-start.15 = (bf16[4,8,16,256]{3,2,1,0:T(8,128)(2,1)S(1)}, bf16[4,8,16,256]{3,2,1,0:T(8,128)(2,1)}, u32[]{:S(2)}) copy-start(bf16[4,8,16,256]{3,2,1,0:T(8,128)(2,1)} %get-tuple-element.27) | copy-start | bytes 786436
  113.1 2.9 %copy-start.16 = (bf16[4,8,16,256]{3,2,1,0:T(8,128)(2,1)S(1)}, bf16[4,8,16,256]{3,2,1,0:T(8,128)(2,1)}, u32[]{:S(2)}) copy-start(bf16[4,8,16,256]{3,2,1,0:T(8,128)(2,1)} %get-tuple-element.28) | copy-start | bytes 786436
  114.9 1.0 copy-start.7
  115.9 6.7 %copy-start.6 = (f32[4,256,256]{2,1,0:T(8,128)S(1)}, f32[4,256,256]{2,1,0:T(8,128)}, u32[]{:S(2)}) copy-start(f32[4,256,256]{2,1,0:T(8,128)} %copy-done.5) | copy-start | bytes 3145732
  117.0 4.5 %collective-permute-start = (bf16[1536,256]{1,0:T(8,128)(2,1)}, bf16[1536,256]{1,0:T(8,128)(2,1)}, u32[]{:S(2)}, u32[]{:S(2)}) collective-permute-start(bf16[1536,256]{1,0:T(8,128)(2,1)} %pad_maximum_fusion), channel_id=1, source_target_pairs={{0,32},{32,0},{64,96},{96,64},{128,160},{160,128},{192,224},{224,1... | collective-permute-start | bytes 2359304 | tf_op jit(solution)/shard_map/ppermute | solution.py:53
  118.9 3.9 %copy-start.8 = (f32[16,64,256]{2,1,0:T(8,128)S(1)}, f32[16,64,256]{2,1,0:T(8,128)}, u32[]{:S(2)}) copy-start(f32[16,64,256]{2,1,0:T(8,128)} %copy-done.7) | copy-start | bytes 3145732
  118.9 4.0 %copy-start.4 = (f32[4,256,256]{2,1,0:T(8,128)S(1)}, f32[4,256,256]{2,1,0:T(8,128)}, u32[]{:S(2)}) copy-start(f32[4,256,256]{2,1,0:T(8,128)} %copy-done.3) | copy-start | bytes 3145732
  122.7 1.7 copy-start.10
  122.7 5.1 %copy-start.14 = (bf16[512,256]{1,0:T(8,128)(2,1)S(1)}, bf16[512,256]{1,0:T(8,128)(2,1)}, u32[]{:S(2)}) copy-start(bf16[512,256]{1,0:T(8,128)(2,1)} %param.6) | copy-start | bytes 786436
  122.8 0.8 copy-start.12
  124.4 13.4 %collective-permute-start.1 = (bf16[768,256]{1,0:T(8,128)(2,1)}, bf16[768,256]{1,0:T(8,128)(2,1)}, u32[]{:S(2)}, u32[]{:S(2)}) collective-permute-start(bf16[768,256]{1,0:T(8,128)(2,1)} %pad_maximum_fusion.1), channel_id=1, source_target_pairs={{0,128},{32,160},{64,192},{96,224},{128,0},{160,32},{192,64},{224,... | collective-permute-start | bytes 1179656 | tf_op jit(solution)/shard_map/ppermute | solution.py:53
  129.6 10.3 %copy-start.11 = (f32[4,8,16,256]{3,2,1,0:T(8,128)S(1)}, f32[4,8,16,256]{3,2,1,0:T(8,128)}, u32[]{:S(2)}) copy-start(f32[4,8,16,256]{3,2,1,0:T(8,128)} %copy-done.10) | copy-start | bytes 1572868
  129.6 33.6 %all-to-all-start.3 = ((bf16[4,32,8,512]{3,2,0,1:T(8,128)(2,1)}), bf16[4,32,8,512]{3,2,0,1:T(8,128)(2,1)S(1)}, u32[]{:S(2)}, u32[]{:S(2)}) async-start(bf16[4,32,8,512]{3,2,0,1:T(8,128)(2,1)} %copy.75), calls=%async_computation.3 | async-start | bytes 2097152 | tf_op jit(solution)/shard_map/all_to_all | solution.py:108
  135.1 9.8 %copy-start.18 = (bf16[1,1024,256]{2,1,0:T(8,128)(2,1)S(1)}, bf16[1,1024,256]{2,1,0:T(8,128)(2,1)}, u32[]{:S(2)}) copy-start(bf16[1,1024,256]{2,1,0:T(8,128)(2,1)} %param.10) | copy-start | bytes 1572868
  140.0 9.5 %collective-permute-start.2 = (bf16[384,256]{1,0:T(8,128)(2,1)S(1)}, bf16[384,256]{1,0:T(8,128)(2,1)S(1)}, u32[]{:S(2)}, u32[]{:S(2)}) collective-permute-start(bf16[384,256]{1,0:T(8,128)(2,1)S(1)} %pad_maximum_fusion.2), channel_id=1, source_target_pairs={{0,256},{32,288},{64,320},{96,352},{128,384},{160,416},{192,448},{... | collective-permute-start | bytes 589832 | tf_op jit(solution)/shard_map/ppermute | solution.py:53
  163.2 11.5 %collective-permute-start.7 = (bf16[192,256]{1,0:T(8,128)(2,1)S(1)}, bf16[192,256]{1,0:T(8,128)(2,1)S(1)}, u32[]{:S(2)}, u32[]{:S(2)}) collective-permute-start(bf16[192,256]{1,0:T(8,128)(2,1)S(1)} %pad_maximum_fusion.3), channel_id=1, source_target_pairs={{0,64},{32,96},{64,0},{96,32},{128,192},{160,224},{192,128},{224,1... | collective-permute-start | bytes 294920 | tf_op jit(solution)/shard_map/ppermute | solution.py:53
  169.1 5.6 %collective-permute-start.3 = (bf16[128,1024]{1,0:T(8,128)(2,1)S(1)}, bf16[128,1024]{1,0:T(8,128)(2,1)S(1)}, u32[]{:S(2)}, u32[]{:S(2)}) collective-permute-start(bf16[128,1024]{1,0:T(8,128)(2,1)S(1)} %bitcast.227), channel_id=1, source_target_pairs={{0,32},{32,0},{64,96},{96,64},{128,160},{160,128},{192,224},{224,1... | collective-permute-start | bytes 786440 | tf_op jit(solution)/shard_map/ppermute | solution.py:53
  174.8 6.9 %collective-permute-start.4 = (bf16[64,1024]{1,0:T(8,128)(2,1)S(1)}, bf16[64,1024]{1,0:T(8,128)(2,1)S(1)}, u32[]{:S(2)}, u32[]{:S(2)}) collective-permute-start(bf16[64,1024]{1,0:T(8,128)(2,1)S(1)} %bitcast.234), channel_id=1, source_target_pairs={{0,128},{32,160},{64,192},{96,224},{128,0},{160,32},{192,64},{224,... | collective-permute-start | bytes 393224 | tf_op jit(solution)/shard_map/ppermute | solution.py:53
  181.7 7.7 %collective-permute-start.5 = (bf16[32,1024]{1,0:T(8,128)(2,1)S(1)}, bf16[32,1024]{1,0:T(8,128)(2,1)S(1)}, u32[]{:S(2)}, u32[]{:S(2)}) collective-permute-start(bf16[32,1024]{1,0:T(8,128)(2,1)S(1)} %bitcast.241), channel_id=1, source_target_pairs={{0,256},{32,288},{64,320},{96,352},{128,384},{160,416},{192,448},{... | collective-permute-start | bytes 196616 | tf_op jit(solution)/shard_map/ppermute | solution.py:53
  189.4 10.0 %collective-permute-start.6 = (bf16[16,1024]{1,0:T(8,128)(2,1)S(1)}, bf16[16,1024]{1,0:T(8,128)(2,1)S(1)}, u32[]{:S(2)}, u32[]{:S(2)}) collective-permute-start(bf16[16,1024]{1,0:T(8,128)(2,1)S(1)} %fusion.41), channel_id=1, source_target_pairs={{0,64},{32,96},{64,0},{96,32},{128,192},{160,224},{192,128},{224,1... | collective-permute-start | bytes 98312 | tf_op jit(solution)/shard_map/ppermute | solution.py:53

commit v11 on v9

--- a/solution.py
+++ b/solution.py
@@ -107,9 +107,8 @@
 
     down_sorted = chunk_order(mixed_down, 1, replicas)
     g_left_two = jnp.einsum("kwt,tkc->kwc", down_sorted, cot_parts, preferred_element_type=fp)
-    (mid,) = dp_reduce_scatter([view(g_left_two)], replicas)
-    d_down_inner, mid = lax.optimization_barrier((d_down_inner, mid))
-    red_left_two = mid[:, 0]
+    mid = dp_reduce_scatter([view(g_left_two)], replicas, 0, 2)
+    d_down_inner, *mid = lax.optimization_barrier((d_down_inner, *mid))
     d_hidden = jnp.einsum("kjgt,jbkg->jbt", d_down_inner, right_two, preferred_element_type=fp)
     d_pre = (d_hidden * gelu_slope(pre_piece)).astype(bf)
     d_mixed_up = jnp.einsum("jct,jbc->jbt", d_pre, first_left, preferred_element_type=fp).astype(bf)
@@ -126,6 +125,7 @@
         [view(g_left_one), view(g_right_two)], replicas, 0, early_stages
     )
     d_up_inner, *early = lax.optimization_barrier((d_up_inner, *early))
+    early = early + mid
 
     grad_tokens = jnp.einsum(
         "jkgt,kbjg->tkb", d_up_inner, right_one, preferred_element_type=fp
@@ -141,7 +141,7 @@
         if early_stages + stage < stages:
             early = dp_reduce_scatter(early, replicas, early_stages + stage, early_stages + stage + 1)
     red_right_one = late[0][:, 0]
-    red_left_one, red_right_two = [e[:, 0] for e in early]
+    red_left_one, red_right_two, red_left_two = [e[:, 0] for e in early]
     reduced = (red_right_one, red_left_one, red_right_two, red_left_two)
     grad_right_one, grad_left_one, grad_right_two, grad_left_two = [r * grad_scale for r in reduced]
     return (layer_out, grad_tokens, grad_right_one, grad_left_one, grad_right_two, grad_left_two)

time: 217 us -> 207 us (0.954)
  the two profiles are of different devices: /device:TPU:1 before, /device:TPU:78 now
where the time goes in v11:
time: 207 us; the launch traced here: 206 us
  waiting for transfers between devices  104 us (50%)
  starting transfers between devices  59.5 us (29%)
  local copies, waits for them, and re-layouts  20.7 us (10%)
  matrix products  13.7 us (7%)
  other arithmetic  6.81 us (3%)
    ppermute x10, starting transfers between devices, dp_reduce_scatter(): got = lax.ppermute(packed, 'dp', perm)  30.3 us
    all_to_all x1, waiting for transfers between devices, layer(): lax.all_to_all(up_inner, 'tensor', split_axis=0, concat_axis=1, tiled=True)  27 us
    all_to_all x1, waiting for transfers between devices, layer(): lax.all_to_all(down_inner, 'tensor', split_axis=0, concat_axis=1, tiled=T...  25.5 us
    ppermute x10, waiting for transfers between devices, dp_reduce_scatter(): got = lax.ppermute(packed, 'dp', perm)  24.5 us
    all_to_all x1, waiting for transfers between devices, layer(): lax.all_to_all(d_mixed_up, 'tensor', split_axis=1, concat_axis=0, tiled=T...  16.2 us
    all_to_all x1, starting transfers between devices, layer(): lax.all_to_all(up_inner, 'tensor', split_axis=0, concat_axis=1, tiled=True)  13.1 us
    all_to_all x1, waiting for transfers between devices, layer(): lax.all_to_all(d_mixed_down, 'tensor', split_axis=1, concat_axis=0, tiled...  10.8 us
    unnamed x37, local copies, waits for them, and re-layouts  8.82 us
  transfers between devices with their start and end apart: 14, of which 11 were waited for; matrix products, arithmetic and copies ran while one was open for 10% of the time, Pallas kernels for 0%

profile of v11, /device:TPU:78, one launch (start us, length us, event | category | flops | bytes accessed | tf_op | source)
XLA Modules:
  0.0 206.0 jit_solution(8031194128623328513)
XLA Ops:
  0.6 1.3 copy.83
  2.0 1.4 fusion.10
  3.4 1.6 copy.85
  4.9 13.1 %all-to-all-start = ((bf16[128,1,8,512]{3,2,1,0:T(8,128)(2,1)}), bf16[128,1,8,512]{3,2,1,0:T(8,128)(2,1)S(1)}, u32[]{:S(2)}, u32[]{:S(2)}) async-start(bf16[128,1,8,512]{3,2,1,0:T(8,128)(2,1)} %copy.85), calls=%async_computation | async-start | bytes 2097152 | tf_op jit(solution)/shard_map/all_to_all | solution.py:85
  18.0 1.0 copy.88
  19.0 27.0 %all-to-all-done = bf16[128,1,8,512]{3,2,1,0:T(8,128)(2,1)S(1)} async-done(((bf16[128,1,8,512]{3,2,1,0:T(8,128)(2,1)}), bf16[128,1,8,512]{3,2,1,0:T(8,128)(2,1)S(1)}, u32[]{:S(2)}, u32[]{:S(2)}) %all-to-all-start) | async-done | bytes 1048608 | tf_op jit(solution)/shard_map/all_to_all | solution.py:85
  46.0 2.0 fusion.7
  48.0 1.0 copy-done.5
  49.0 0.4 fusion.12
  49.5 1.6 copy.90
  51.0 5.3 %all-to-all-start.1 = ((bf16[32,4,8,512]{3,2,1,0:T(8,128)(2,1)}), bf16[32,4,8,512]{3,2,1,0:T(8,128)(2,1)S(1)}, u32[]{:S(2)}, u32[]{:S(2)}) async-start(bf16[32,4,8,512]{3,2,1,0:T(8,128)(2,1)} %copy.90), calls=%async_computation.1 | async-start | bytes 2097152 | tf_op jit(solution)/shard_map/all_to_all | solution.py:92
  56.4 2.5 %fusion.11 = bf16[1,128,8,512]{3,2,0,1:T(8,128)(2,1)} fusion(bf16[512,256]{1,0:T(8,128)(2,1)S(1)} %copy-done.11, bf16[1,1024,256]{2,1,0:T(8,128)(2,1)} %param.10), kind=kOutput, calls=%fused_computation.18 | convolution fusion | flops 268959744 | bytes 1835008 | tf_op jit(solution)/shard_map/tkc,kwc->kwt/dot_general | solution.py:99
  58.9 25.5 %all-to-all-done.1 = bf16[32,4,8,512]{3,2,1,0:T(8,128)(2,1)S(1)} async-done(((bf16[32,4,8,512]{3,2,1,0:T(8,128)(2,1)}), bf16[32,4,8,512]{3,2,1,0:T(8,128)(2,1)S(1)}, u32[]{:S(2)}, u32[]{:S(2)}) %all-to-all-start.1) | async-done | bytes 1048608 | tf_op jit(solution)/shard_map/all_to_all | solution.py:92
  84.4 1.0 copy-done.3
  85.4 5.5 %all-to-all-start.2 = ((bf16[1,128,8,512]{3,2,0,1:T(8,128)(2,1)}), bf16[1,128,8,512]{3,2,0,1:T(8,128)(2,1)S(1)}, u32[]{:S(2)}, u32[]{:S(2)}) async-start(bf16[1,128,8,512]{3,2,0,1:T(8,128)(2,1)} %fusion.11), calls=%async_computation.2 | async-start | bytes 2097152 | tf_op jit(solution)/shard_map/all_to_all | solution.py:103
  90.9 1.3 copy.92
  92.2 0.4 fusion.30
  92.7 1.0 copy-done.8
  93.7 0.7 dynamic-slice_convert_fusion.3
  94.4 1.9 collective-permute-start
  96.3 1.7 collective-permute-done
  98.0 1.1 convert_add_fusion.3
  99.1 0.8 copy-done.9
  99.9 2.7 %collective-permute-start.1 = (bf16[256,256]{1,0:T(8,128)(2,1)S(1)}, bf16[256,256]{1,0:T(8,128)(2,1)S(1)}, u32[]{:S(2)}, u32[]{:S(2)}) collective-permute-start(bf16[256,256]{1,0:T(8,128)(2,1)S(1)} %bitcast.229), channel_id=1, source_target_pairs={{0,128},{32,160},{64,192},{96,224},{128,0},{160,32},{192,64},{224,... | collective-permute-start | bytes 393224 | tf_op jit(solution)/shard_map/ppermute | solution.py:53
  102.7 1.1 copy-done.6
  103.9 1.1 copy.98
  105.0 1.1 copy.97
  106.1 1.3 collective-permute-done.1
  107.4 0.7 fusion.29
  108.1 10.8 %all-to-all-done.2 = bf16[1,128,8,512]{3,2,0,1:T(8,128)(2,1)S(1)} async-done(((bf16[1,128,8,512]{3,2,0,1:T(8,128)(2,1)}), bf16[1,128,8,512]{3,2,0,1:T(8,128)(2,1)S(1)}, u32[]{:S(2)}, u32[]{:S(2)}) %all-to-all-start.2) | async-done | bytes 1048608 | tf_op jit(solution)/shard_map/all_to_all | solution.py:103
  118.9 2.7 %fusion.5 = bf16[4,256,512]{2,1,0:T(8,128)(2,1)S(1)} fusion(f32[4,512,256]{1,2,0:T(8,128)} %get-tuple-element.26, bf16[32,4,8,512]{3,2,1,0:T(8,128)(2,1)S(1)} %bitcast.191, bf16[4,256,256]{1,2,0:T(8,128)(2,1)} %copy.88), kind=kOutput, calls=%fused_computation.6 | convolution fusion | flops 273678336 | bytes 4718592 | tf_op jit(solution)/shard_map/kjgt,jbkg->jbt/dot_general | solution.py:112
  121.6 0.5 fusion.19
  122.1 0.7 copy-done.2
  122.8 0.5 fusion.49
  123.4 0.8 pad_maximum_fusion
  124.2 1.9 collective-permute-start.2
  126.1 0.8 copy.100
  127.0 1.0 copy.101
  128.0 0.4 fusion.13
  128.4 1.1 copy.95
  129.5 5.4 %all-to-all-start.3 = ((bf16[4,32,8,512]{3,2,0,1:T(8,128)(2,1)}), bf16[4,32,8,512]{3,2,0,1:T(8,128)(2,1)S(1)}, u32[]{:S(2)}, u32[]{:S(2)}) async-start(bf16[4,32,8,512]{3,2,0,1:T(8,128)(2,1)} %copy.95), calls=%async_computation.3 | async-start | bytes 2097152 | tf_op jit(solution)/shard_map/all_to_all | solution.py:116
  134.9 1.1 fusion.45
  136.0 1.2 convert_add_fusion.1
  137.4 2.7 %collective-permute-start.3 = (bf16[512,256]{1,0:T(8,128)(2,1)S(1)}, bf16[512,256]{1,0:T(8,128)(2,1)S(1)}, u32[]{:S(2)}, u32[]{:S(2)}) collective-permute-start(bf16[512,256]{1,0:T(8,128)(2,1)S(1)} %pad_maximum_fusion.1), channel_id=1, source_target_pairs={{0,128},{32,160},{64,192},{96,224},{128,0},{160,32},{192,64},{224,... | collective-permute-start | bytes 786440 | tf_op jit(solution)/shard_map/ppermute | solution.py:53
  140.2 1.2 convolution_convert_fusion.4
  141.3 0.9 dynamic-slice_convert_fusion.8
  142.3 5.2 %collective-permute-done.3 = bf16[512,256]{1,0:T(8,128)(2,1)S(1)} collective-permute-done((bf16[512,256]{1,0:T(8,128)(2,1)S(1)}, bf16[512,256]{1,0:T(8,128)(2,1)S(1)}, u32[]{:S(2)}, u32[]{:S(2)}) %collective-permute-start.3) | collective-permute-done | bytes 262176 | tf_op jit(solution)/shard_map/ppermute | solution.py:53
  147.5 16.2 %all-to-all-done.3 = bf16[4,32,8,512]{3,2,0,1:T(8,128)(2,1)S(1)} async-done(((bf16[4,32,8,512]{3,2,0,1:T(8,128)(2,1)}), bf16[4,32,8,512]{3,2,0,1:T(8,128)(2,1)S(1)}, u32[]{:S(2)}, u32[]{:S(2)}) %all-to-all-start.3) | async-done | bytes 1048608 | tf_op jit(solution)/shard_map/all_to_all | solution.py:116
  163.8 1.2 fusion.14
  165.1 3.4 %collective-permute-start.8 = (bf16[384,256]{1,0:T(8,128)(2,1)S(1)}, bf16[384,256]{1,0:T(8,128)(2,1)S(1)}, u32[]{:S(2)}, u32[]{:S(2)}) collective-permute-start(bf16[384,256]{1,0:T(8,128)(2,1)S(1)} %pad_maximum_fusion.2), channel_id=1, source_target_pairs={{0,256},{32,288},{64,320},{96,352},{128,384},{160,416},{192,448},{... | collective-permute-start | bytes 589832 | tf_op jit(solution)/shard_map/ppermute | solution.py:53
  168.5 0.5 fusion.16
  169.0 1.9 collective-permute-start.4
  170.9 3.3 %collective-permute-done.8 = bf16[384,256]{1,0:T(8,128)(2,1)S(1)} collective-permute-done((bf16[384,256]{1,0:T(8,128)(2,1)S(1)}, bf16[384,256]{1,0:T(8,128)(2,1)S(1)}, u32[]{:S(2)}, u32[]{:S(2)}) %collective-permute-start.8) | collective-permute-done | bytes 196640 | tf_op jit(solution)/shard_map/ppermute | solution.py:53
  174.5 4.9 %collective-permute-start.9 = (bf16[192,256]{1,0:T(8,128)(2,1)S(1)}, bf16[192,256]{1,0:T(8,128)(2,1)S(1)}, u32[]{:S(2)}, u32[]{:S(2)}) collective-permute-start(bf16[192,256]{1,0:T(8,128)(2,1)S(1)} %pad_maximum_fusion.3), channel_id=1, source_target_pairs={{0,64},{32,96},{64,0},{96,32},{128,192},{160,224},{192,128},{224,1... | collective-permute-start | bytes 294920 | tf_op jit(solution)/shard_map/ppermute | solution.py:53
  179.5 2.7 %collective-permute-start.5 = (bf16[64,1024]{1,0:T(8,128)(2,1)S(1)}, bf16[64,1024]{1,0:T(8,128)(2,1)S(1)}, u32[]{:S(2)}, u32[]{:S(2)}) collective-permute-start(bf16[64,1024]{1,0:T(8,128)(2,1)S(1)} %bitcast.230), channel_id=1, source_target_pairs={{0,128},{32,160},{64,192},{96,224},{128,0},{160,32},{192,64},{224,... | collective-permute-start | bytes 393224 | tf_op jit(solution)/shard_map/ppermute | solution.py:53
  182.2 4.6 %collective-permute-done.9 = bf16[192,256]{1,0:T(8,128)(2,1)S(1)} collective-permute-done((bf16[192,256]{1,0:T(8,128)(2,1)S(1)}, bf16[192,256]{1,0:T(8,128)(2,1)S(1)}, u32[]{:S(2)}, u32[]{:S(2)}) %collective-permute-start.9) | collective-permute-done | bytes 98336 | tf_op jit(solution)/shard_map/ppermute | solution.py:53
  186.9 0.6 fusion.38
  187.6 3.1 %collective-permute-start.6 = (bf16[32,1024]{1,0:T(8,128)(2,1)S(1)}, bf16[32,1024]{1,0:T(8,128)(2,1)S(1)}, u32[]{:S(2)}, u32[]{:S(2)}) collective-permute-start(bf16[32,1024]{1,0:T(8,128)(2,1)S(1)} %bitcast.238), channel_id=1, source_target_pairs={{0,256},{32,288},{64,320},{96,352},{128,384},{160,416},{192,448},{... | collective-permute-start | bytes 196616 | tf_op jit(solution)/shard_map/ppermute | solution.py:53
  190.7 0.6 fusion.36
  191.4 3.9 %collective-permute-done.6 = bf16[32,1024]{1,0:T(8,128)(2,1)S(1)} collective-permute-done((bf16[32,1024]{1,0:T(8,128)(2,1)S(1)}, bf16[32,1024]{1,0:T(8,128)(2,1)S(1)}, u32[]{:S(2)}, u32[]{:S(2)}) %collective-permute-start.6) | collective-permute-done | bytes 65568 | tf_op jit(solution)/shard_map/ppermute | solution.py:53
  195.3 4.9 %collective-permute-start.7 = (bf16[16,1024]{1,0:T(8,128)(2,1)S(1)}, bf16[16,1024]{1,0:T(8,128)(2,1)S(1)}, u32[]{:S(2)}, u32[]{:S(2)}) collective-permute-start(bf16[16,1024]{1,0:T(8,128)(2,1)S(1)} %fusion.41), channel_id=1, source_target_pairs={{0,64},{32,96},{64,0},{96,32},{128,192},{160,224},{192,128},{224,1... | collective-permute-start | bytes 98312 | tf_op jit(solution)/shard_map/ppermute | solution.py:53
  200.1 0.6 fusion.34
  200.8 4.5 %collective-permute-done.7 = bf16[16,1024]{1,0:T(8,128)(2,1)S(1)} collective-permute-done((bf16[16,1024]{1,0:T(8,128)(2,1)S(1)}, bf16[16,1024]{1,0:T(8,128)(2,1)S(1)}, u32[]{:S(2)}, u32[]{:S(2)}) %collective-permute-start.7) | collective-permute-done | bytes 32800 | tf_op jit(solution)/shard_map/ppermute | solution.py:53
  205.3 0.6 fusion.40
  (60 shorter events, 0.9 us)
Async XLA Ops:
  0.6 45.4 %copy-start = (bf16[4,256,256]{2,1,0:T(8,128)(2,1)S(1)}, bf16[4,256,256]{2,1,0:T(8,128)(2,1)}, u32[]{:S(2)}) copy-start(bf16[4,256,256]{2,1,0:T(8,128)(2,1)} %param.8) | copy-start | bytes 1572868
  3.4 14.6 %copy-start.15 = (bf16[4,256,256]{2,1,0:T(8,128)(2,1)S(1)}, bf16[4,256,256]{2,1,0:T(8,128)(2,1)}, u32[]{:S(2)}) copy-start(bf16[4,256,256]{2,1,0:T(8,128)(2,1)} %param.9) | copy-start | bytes 1572868
  4.9 41.1 %all-to-all-start = ((bf16[128,1,8,512]{3,2,1,0:T(8,128)(2,1)}), bf16[128,1,8,512]{3,2,1,0:T(8,128)(2,1)S(1)}, u32[]{:S(2)}, u32[]{:S(2)}) async-start(bf16[128,1,8,512]{3,2,1,0:T(8,128)(2,1)} %copy.85), calls=%async_computation | async-start | bytes 2097152 | tf_op jit(solution)/shard_map/all_to_all | solution.py:85
  46.0 3.0 %copy-start.16 = (bf16[4,256,256]{1,2,0:T(8,128)(2,1)S(1)}, bf16[4,256,256]{1,2,0:T(8,128)(2,1)}, u32[]{:S(2)}) copy-start(bf16[4,256,256]{1,2,0:T(8,128)(2,1)} %copy.88) | copy-start | bytes 1572868
  48.0 1.0 copy-start.5
  49.5 6.9 %copy-start.11 = (bf16[512,256]{1,0:T(8,128)(2,1)S(1)}, bf16[512,256]{1,0:T(8,128)(2,1)}, u32[]{:S(2)}) copy-start(bf16[512,256]{1,0:T(8,128)(2,1)} %param.11) | copy-start | bytes 786436
  51.0 33.4 %all-to-all-start.1 = ((bf16[32,4,8,512]{3,2,1,0:T(8,128)(2,1)}), bf16[32,4,8,512]{3,2,1,0:T(8,128)(2,1)S(1)}, u32[]{:S(2)}, u32[]{:S(2)}) async-start(bf16[32,4,8,512]{3,2,1,0:T(8,128)(2,1)} %copy.90), calls=%async_computation.1 | async-start | bytes 2097152 | tf_op jit(solution)/shard_map/all_to_all | solution.py:92
  84.4 1.0 copy-start.3
  85.4 33.5 %all-to-all-start.2 = ((bf16[1,128,8,512]{3,2,0,1:T(8,128)(2,1)}), bf16[1,128,8,512]{3,2,0,1:T(8,128)(2,1)S(1)}, u32[]{:S(2)}, u32[]{:S(2)}) async-start(bf16[1,128,8,512]{3,2,0,1:T(8,128)(2,1)} %fusion.11), calls=%async_computation.2 | async-start | bytes 2097152 | tf_op jit(solution)/shard_map/all_to_all | solution.py:103
  92.7 1.0 copy-start.8
  94.4 3.6 %collective-permute-start = (bf16[512,256]{1,0:T(8,128)(2,1)}, bf16[512,256]{1,0:T(8,128)(2,1)S(1)}, u32[]{:S(2)}, u32[]{:S(2)}) collective-permute-start(bf16[512,256]{1,0:T(8,128)(2,1)} %bitcast.20), channel_id=1, source_target_pairs={{0,32},{32,0},{64,96},{96,64},{128,160},{160,128},{192,224},{224,1... | collective-permute-start | bytes 786440 | tf_op jit(solution)/shard_map/ppermute | solution.py:53
  99.1 0.8 copy-start.9
  99.9 7.4 %collective-permute-start.1 = (bf16[256,256]{1,0:T(8,128)(2,1)S(1)}, bf16[256,256]{1,0:T(8,128)(2,1)S(1)}, u32[]{:S(2)}, u32[]{:S(2)}) collective-permute-start(bf16[256,256]{1,0:T(8,128)(2,1)S(1)} %bitcast.229), channel_id=1, source_target_pairs={{0,128},{32,160},{64,192},{96,224},{128,0},{160,32},{192,64},{224,... | collective-permute-start | bytes 393224 | tf_op jit(solution)/shard_map/ppermute | solution.py:53
  102.6 1.2 copy-start.6
  103.9 3.5 %copy-start.10 = (f32[8,64,256]{2,1,0:T(8,128)S(1)}, f32[8,64,256]{2,1,0:T(8,128)}, u32[]{:S(2)}) copy-start(f32[8,64,256]{2,1,0:T(8,128)} %copy-done.9) | copy-start | bytes 1572868
  118.9 2.7 %copy-start.1 = (bf16[4,2,2,2,2,16,512]{6,5,4,3,2,1,0:T(8,128)(2,1)S(1)}, bf16[4,2,2,2,2,16,512]{6,5,4,3,2,1,0:T(8,128)(2,1)}, u32[]{:S(2)}) copy-start(bf16[4,2,2,2,2,16,512]{6,5,4,3,2,1,0:T(8,128)(2,1)} %copy.98) | copy-start | bytes 3145732
  121.6 1.2 copy-start.2
  122.1 1.2 copy-start.7
  122.8 3.3 %copy-start.12 = (bf16[512,256]{1,0:T(8,128)(2,1)S(1)}, bf16[512,256]{1,0:T(8,128)(2,1)}, u32[]{:S(2)}) copy-start(bf16[512,256]{1,0:T(8,128)(2,1)} %param.6) | copy-start | bytes 786436
  124.2 10.7 %collective-permute-start.2 = (bf16[1024,256]{1,0:T(8,128)(2,1)}, bf16[1024,256]{1,0:T(8,128)(2,1)}, u32[]{:S(2)}, u32[]{:S(2)}) collective-permute-start(bf16[1024,256]{1,0:T(8,128)(2,1)} %pad_maximum_fusion), channel_id=1, source_target_pairs={{0,32},{32,0},{64,96},{96,64},{128,160},{160,128},{192,224},{224,1... | collective-permute-start | bytes 1572872 | tf_op jit(solution)/shard_map/ppermute | solution.py:53
  129.5 34.2 %all-to-all-start.3 = ((bf16[4,32,8,512]{3,2,0,1:T(8,128)(2,1)}), bf16[4,32,8,512]{3,2,0,1:T(8,128)(2,1)S(1)}, u32[]{:S(2)}, u32[]{:S(2)}) async-start(bf16[4,32,8,512]{3,2,0,1:T(8,128)(2,1)} %copy.95), calls=%async_computation.3 | async-start | bytes 2097152 | tf_op jit(solution)/shard_map/all_to_all | solution.py:116
  136.0 4.2 %copy-start.4 = (bf16[32,4,8,512]{3,2,1,0:T(8,128)(2,1)S(1)}, bf16[32,4,8,512]{3,2,1,0:T(8,128)(2,1)}, u32[]{:S(2)}) copy-start(bf16[32,4,8,512]{3,2,1,0:T(8,128)(2,1)} %copy-done.3) | copy-start | bytes 3145732
  136.0 4.2 %copy-start.14 = (bf16[1,1024,256]{2,1,0:T(8,128)(2,1)S(1)}, bf16[1,1024,256]{2,1,0:T(8,128)(2,1)}, u32[]{:S(2)}) copy-start(bf16[1,1024,256]{2,1,0:T(8,128)(2,1)} %param.10) | copy-start | bytes 1572868
  137.4 10.0 %collective-permute-start.3 = (bf16[512,256]{1,0:T(8,128)(2,1)S(1)}, bf16[512,256]{1,0:T(8,128)(2,1)S(1)}, u32[]{:S(2)}, u32[]{:S(2)}) collective-permute-start(bf16[512,256]{1,0:T(8,128)(2,1)S(1)} %pad_maximum_fusion.1), channel_id=1, source_target_pairs={{0,128},{32,160},{64,192},{96,224},{128,0},{160,32},{192,64},{224,... | collective-permute-start | bytes 786440 | tf_op jit(solution)/shard_map/ppermute | solution.py:53
  165.0 9.3 %copy-start.13 = (f32[1,4,64,256]{3,2,1,0:T(8,128)S(1)}, f32[1,4,64,256]{3,2,1,0:T(8,128)}, u32[]{:S(2)}) copy-start(f32[1,4,64,256]{3,2,1,0:T(8,128)} %fusion.29) | copy-start | bytes 786436
  165.1 9.2 %collective-permute-start.8 = (bf16[384,256]{1,0:T(8,128)(2,1)S(1)}, bf16[384,256]{1,0:T(8,128)(2,1)S(1)}, u32[]{:S(2)}, u32[]{:S(2)}) collective-permute-start(bf16[384,256]{1,0:T(8,128)(2,1)S(1)} %pad_maximum_fusion.2), channel_id=1, source_target_pairs={{0,256},{32,288},{64,320},{96,352},{128,384},{160,416},{192,448},{... | collective-permute-start | bytes 589832 | tf_op jit(solution)/shard_map/ppermute | solution.py:53
  169.0 10.4 %collective-permute-start.4 = (bf16[128,1024]{1,0:T(8,128)(2,1)S(1)}, bf16[128,1024]{1,0:T(8,128)(2,1)S(1)}, u32[]{:S(2)}, u32[]{:S(2)}) collective-permute-start(bf16[128,1024]{1,0:T(8,128)(2,1)S(1)} %bitcast.222), channel_id=1, source_target_pairs={{0,32},{32,0},{64,96},{96,64},{128,160},{160,128},{192,224},{224,1... | collective-permute-start | bytes 786440 | tf_op jit(solution)/shard_map/ppermute | solution.py:53
  174.5 12.4 %collective-permute-start.9 = (bf16[192,256]{1,0:T(8,128)(2,1)S(1)}, bf16[192,256]{1,0:T(8,128)(2,1)S(1)}, u32[]{:S(2)}, u32[]{:S(2)}) collective-permute-start(bf16[192,256]{1,0:T(8,128)(2,1)S(1)} %pad_maximum_fusion.3), channel_id=1, source_target_pairs={{0,64},{32,96},{64,0},{96,32},{128,192},{160,224},{192,128},{224,1... | collective-permute-start | bytes 294920 | tf_op jit(solution)/shard_map/ppermute | solution.py:53
  179.5 8.0 %collective-permute-start.5 = (bf16[64,1024]{1,0:T(8,128)(2,1)S(1)}, bf16[64,1024]{1,0:T(8,128)(2,1)S(1)}, u32[]{:S(2)}, u32[]{:S(2)}) collective-permute-start(bf16[64,1024]{1,0:T(8,128)(2,1)S(1)} %bitcast.230), channel_id=1, source_target_pairs={{0,128},{32,160},{64,192},{96,224},{128,0},{160,32},{192,64},{224,... | collective-permute-start | bytes 393224 | tf_op jit(solution)/shard_map/ppermute | solution.py:53
  187.6 7.7 %collective-permute-start.6 = (bf16[32,1024]{1,0:T(8,128)(2,1)S(1)}, bf16[32,1024]{1,0:T(8,128)(2,1)S(1)}, u32[]{:S(2)}, u32[]{:S(2)}) collective-permute-start(bf16[32,1024]{1,0:T(8,128)(2,1)S(1)} %bitcast.238), channel_id=1, source_target_pairs={{0,256},{32,288},{64,320},{96,352},{128,384},{160,416},{192,448},{... | collective-permute-start | bytes 196616 | tf_op jit(solution)/shard_map/ppermute | solution.py:53
  195.3 10.1 %collective-permute-start.7 = (bf16[16,1024]{1,0:T(8,128)(2,1)S(1)}, bf16[16,1024]{1,0:T(8,128)(2,1)S(1)}, u32[]{:S(2)}, u32[]{:S(2)}) collective-permute-start(bf16[16,1024]{1,0:T(8,128)(2,1)S(1)} %fusion.41), channel_id=1, source_target_pairs={{0,64},{32,96},{64,0},{96,32},{128,192},{160,224},{192,128},{224,1... | collective-permute-start | bytes 98312 | tf_op jit(solution)/shard_map/ppermute | solution.py:53
